TPU v7x, 128 devices: a whole 4x4x4 slice. The times are simulated.
128 devices in a mesh: pr: 8 (over z, core), pc: 16 (over y, x).
Axes of the slice: x: 4, y: 4, z: 4, core: 2. Of those that a mesh axis runs over, the one named last changes fastest.
Arguments:
- test_points: bfloat16 [131072, 512], P('pr'), may hold values from -15 to 15
- panel_points: bfloat16 [1024, 512], P('pc'), may hold values from -15 to 15
- factor_rows: float32 [1024, 32768], P('pc', 'pr'), may hold values from -0.03125 to 0.03125
- alpha_below: float32 [32768, 128], P(('pr', 'pc')), may hold values from -6 to 6
- targets: float32 [1024, 128], P('pc'), may hold values from -6 to 6
- inverse_block: float32 [1024, 1024], P('pc'), may hold values from -0.008 to 0.08, as said below
- predictions_in: float32 [131072, 128], P(('pr', 'pc')), may hold values from -6 to 6
Outputs:
- predictions: float32 [131072, 128], P(('pr', 'pc'))
Inputs may be any that keep to these rules, and one draw needn't show every extreme that they name: `inverse_block`: lower triangular with a positive diagonal.
All inputs are finite; a program needn't handle non-finite values.
Results may differ from a plain program's by a relative error of at most 0.0003.
Values may be sent and summed in bfloat16 or wider, within the bound.
No kernel may reach another device: no remote copies, remote signals or barrier semaphores. Data moves between devices by JAX's collectives and lax.ppermute only.
A program may use at most 128 MiB of HBM per device.

v0:
```python
import math

import jax
import jax.numpy as jnp
from jax import lax
from jax.sharding import PartitionSpec as P

LAYERS = 4


bias_var = 0.1
weight_var = 2.0


def arc_kernel(panel, test, test_norms):
    width = panel.shape[1]
    cross = jnp.dot(panel, test.T, preferred_element_type=jnp.float32) / width
    panel_var = jnp.einsum("pd,pd->p", panel, panel, preferred_element_type=jnp.float32) / width
    kern = bias_var + weight_var * cross
    panel_k = bias_var + weight_var * panel_var
    test_k = bias_var + weight_var * (test_norms / width)
    for level in range(LAYERS):
        spread = jnp.sqrt(panel_k[:, None] * test_k[None, :])
        cosine = kern / spread
        theta = jnp.arccos(cosine)
        kern = bias_var + weight_var / (2.0 * math.pi) * spread * (
            jnp.sqrt(1.0 - cosine * cosine) + (math.pi - theta) * cosine
        )
        panel_k = bias_var + 0.5 * weight_var * panel_k
        test_k = bias_var + 0.5 * weight_var * test_k
    return kern


def contract_rows(left, right):
    return lax.dot_general(
        left,
        right,
        (((0,), (0,)), ((), ())),
        precision=lax.Precision.HIGHEST,
        preferred_element_type=jnp.float32,
    )


def body(
    test_points, panel_points, factor_rows, alpha_below, targets, inverse_block, predictions_in
):
    partial_sum = jnp.dot(
        factor_rows,
        lax.all_gather(alpha_below, "pc", axis=0, tiled=True),
        precision=lax.Precision.HIGHEST,
        preferred_element_type=jnp.float32,
    )
    carried = lax.psum(partial_sum, "pr")
    residual = targets - carried
    alpha_panel = lax.psum_scatter(
        contract_rows(inverse_block, residual), "pc", scatter_dimension=0, tiled=True
    )
    test_norms = jnp.einsum(
        "nd,nd->n", test_points, test_points, preferred_element_type=jnp.float32
    )
    kern = arc_kernel(panel_points, test_points, test_norms)
    update = lax.psum_scatter(
        contract_rows(kern, alpha_panel), "pc", scatter_dimension=0, tiled=True
    )
    return predictions_in + update


def solution(mesh):
    placed = (
        P("pr", None),
        P("pc", None),
        P("pc", "pr"),
        P(("pr", "pc"), None),
        P("pc", None),
        P("pc", None),
        P(("pr", "pc"), None),
    )
    return jax.shard_map(
        body, mesh=mesh, in_specs=placed, out_specs=P(("pr", "pc"), None), check_vma=False
    )
```

profile of v0, /device:TPU:0, one launch (start us, length us, event | category | flops | bytes accessed | tf_op | source)
XLA Modules:
  0.0 328.8 jit_solution(5258146334610582226)
XLA Ops:
  6.5 0.0 copy-start
  6.5 0.0 all-gather.2.cloned.1.call-start
  6.5 0.7 all-gather.2.cloned.1.call-update
  7.3 0.0 reduce-scatter.7.cloned.1.call-start
  7.3 1.0 fusion.81
  8.3 0.0 copy-start.2
  8.3 0.0 copy-start.4
  8.3 7.2 %fusion = f32[16384]{0:T(1024)S(1)} fusion(bf16[16384,512]{1,0:T(8,128)(2,1)} %param.7), kind=kLoop, calls=%fused_computation.1 | loop fusion | flops 25149440 | bytes 16842752 | tf_op jit(solution)/shard_map/nd,nd->n/dot_general | solution.py:58
  15.5 0.0 copy-start.3
  15.6 41.2 %all-gather.2.cloned.1.call-done = f32[4096,128]{1,0:T(8,128)} async-done(((f32[256,128]{1,0:T(8,128)}), f32[4096,128]{1,0:T(8,128)}) %all-gather.2.cloned.1.call-update) | async-done | bytes 2097168 | tf_op jit(solution)/shard_map/all_gather | solution.py:49
  56.7 0.0 copy-done
  56.7 3.0 fusion.87
  59.7 24.3 %psum.7 = f32[64,128]{1,0:T(8,128)S(1)} all-reduce(f32[64,128]{1,0:T(8,128)S(1)} %fusion.87), channel_id=1, replica_groups=mesh['pr'=8,'pc'=16] {'pr'}, use_global_device_ids=true, to_apply=%region_0.0 | all-reduce | flops 8192 | bytes 65536 | tf_op jit(solution)/shard_map/psum | solution.py:53
  84.0 0.0 copy-done.2
  84.0 0.0 copy-done.4
  84.0 0.6 convolution_bitcast_fusion
  84.6 1.0 copy.16
  85.6 0.0 reduce-scatter.7.cloned.1.call-update
  85.7 0.0 reduce-scatter.5.cloned.1.call-start
  85.7 0.0 copy-done.3
  85.7 12.9 %fusion.2 = f32[64,16384]{1,0:T(8,128)} fusion(bf16[64,512]{1,0:T(8,128)(2,1)S(1)} %copy-done.3, bf16[16384,512]{1,0:T(8,128)(2,1)} %param.7, f32[16384]{0:T(1024)S(1)} %get-tuple-element.8, f32[64]{0:T(128)S(1)} %get-tuple-element.12), kind=kOutput, calls=%fused_computation.4 | convolution fusion | flops 1077936128 | bytes 21102848 | tf_op jit(solution)/shard_map/dot_general | solution.py:17
  98.6 57.3 %reduce-scatter.7.cloned.1.call-done = f32[64,128]{1,0:T(8,128)} async-done(((f32[1024,128]{1,0:T(8,128)}), f32[64,128]{1,0:T(8,128)}) %reduce-scatter.7.cloned.1.call-update) | async-done | bytes 32784
  156.0 78.8 %fusion.3 = f32[16384,128]{1,0:T(8,128)} fusion(f32[64,128]{1,0:T(8,128)} %reduce-scatter.7.cloned.1.call-done, f32[64,16384]{1,0:T(8,128)} %fusion.2, f32[16384]{0:T(1024)S(1)} %get-tuple-element.8, f32[64]{0:T(128)S(1)} %get-tuple-element.12, f32[16384]{0:T(1024)S(1)} %get-tuple-element.7, f32[64]{0:T(128)S(1)} %get-tuple-element.11, ...), kind=kOutput, calls=%fused_computation.5 | convolution fusion | flops 1664090112 | bytes 12878848 | tf_op jit(solution)/shard_map/dot_general | solution.py:35
  234.8 0.0 copy-start.1
  234.8 0.0 reduce-scatter.5.cloned.1.call-update
  234.8 85.3 %reduce-scatter.5.cloned.1.call-done = f32[1024,128]{1,0:T(8,128)} async-done(((f32[16384,128]{1,0:T(8,128)}), f32[1024,128]{1,0:T(8,128)}) %reduce-scatter.5.cloned.1.call-update) | async-done | bytes 524304 | tf_op jit(solution)/shard_map/reduce_scatter | solution.py:62
  320.0 0.0 copy-done.1
  320.0 1.9 add.111
  (2 shorter events, 0.0 us)
Async XLA Ops:
  6.5 50.2 %copy-start = (f32[64,4096]{1,0:T(8,128)S(1)}, f32[64,4096]{1,0:T(8,128)}, u32[]{:S(2)}) copy-start(f32[64,4096]{1,0:T(8,128)} %param.9) | copy-start | bytes 3145732
  6.5 50.2 %all-gather.2.cloned.1.call-start = ((), (), s32[]{:S(2)}) async-start(), calls=%async_computation.2 | async-start | bytes 2228224 | tf_op jit(solution)/shard_map/all_gather | solution.py:49
  7.3 148.7 %reduce-scatter.7.cloned.1.call-start = ((), (), s32[]{:S(2)}) async-start(), calls=%async_computation.4 | async-start | bytes 557056
  8.3 75.7 %copy-start.2 = (f32[64,1024]{1,0:T(8,128)S(1)}, f32[64,1024]{1,0:T(8,128)}, u32[]{:S(2)}) copy-start(f32[64,1024]{1,0:T(8,128)} %param.12) | copy-start | bytes 786436
  8.3 75.7 %copy-start.4 = (f32[64,128]{1,0:T(8,128)S(1)}, f32[64,128]{1,0:T(8,128)}, u32[]{:S(2)}) copy-start(f32[64,128]{1,0:T(8,128)} %param.11) | copy-start | bytes 98308
  15.5 70.2 %copy-start.3 = (bf16[64,512]{1,0:T(8,128)(2,1)S(1)}, bf16[64,512]{1,0:T(8,128)(2,1)}, u32[]{:S(2)}) copy-start(bf16[64,512]{1,0:T(8,128)(2,1)} %param.8) | copy-start | bytes 196612
  85.7 234.4 %reduce-scatter.5.cloned.1.call-start = ((), (), s32[]{:S(2)}) async-start(), calls=%async_computation.3 | async-start | bytes 8912896 | tf_op jit(solution)/shard_map/reduce_scatter | solution.py:62
  234.8 85.3 %copy-start.1 = (f32[1024,128]{1,0:T(8,128)S(1)}, f32[1024,128]{1,0:T(8,128)}, u32[]{:S(2)}) copy-start(f32[1024,128]{1,0:T(8,128)} %param.13) | copy-start | bytes 1572868
Sparse Core Ops, SparseCore 0:
  9.5 47.2 all-gather.1
  85.8 70.1 reduce-scatter.6
  234.9 85.0 reduce-scatter.4
where the time goes:
time: 334 us; the launch traced here: 329 us
  waiting for transfers between devices  184 us (55%)
  matrix products  95.3 us (29%)
  blocking collectives  24.3 us (7%)
  between operations  13.6 us (4%)
  other arithmetic  10.1 us (3%)
    reduce_scatter x1, waiting for transfers between devices, body(): lax.psum_scatter(contract_rows(kern, alpha_panel), 'pc', scatter_dimensio...  85.3 us
    dot_general x2, matrix products, contract_rows(): lax.dot_general(left, right, (((0,), (0,)), ((), ())), precision=lax.Prec...  79.4 us
    unnamed x4, waiting for transfers between devices  58.1 us
    all_gather x1, waiting for transfers between devices, body(): lax.all_gather(alpha_below, 'pc', axis=0, tiled=True)  41.2 us
    psum x1, blocking collectives, body(): carried = lax.psum(partial_sum, 'pr')  24.3 us
    dot_general x1, matrix products, arc_kernel(): cross = jnp.dot(panel, test.T, preferred_element_type=jnp.float32) / width  12.9 us
    dot_general x1, other arithmetic, body(): jnp.einsum('nd,nd->n', test_points, test_points, preferred_element_type=j...  7.24 us
  transfers between devices with their start and end apart: 3, of which 3 were waited for; matrix products, arithmetic and copies ran while one was open for 6% of the time, Pallas kernels for 0%

commit v1 on v0

--- a/solution.py
+++ b/solution.py
@@ -44,6 +44,8 @@
 def body(
     test_points, panel_points, factor_rows, alpha_below, targets, inverse_block, predictions_in
 ):
+    rows = predictions_in.shape[0]
+    own = lax.axis_index("pc")
     partial_sum = jnp.dot(
         factor_rows,
         lax.all_gather(alpha_below, "pc", axis=0, tiled=True),
@@ -52,16 +54,14 @@
     )
     carried = lax.psum(partial_sum, "pr")
     residual = targets - carried
-    alpha_panel = lax.psum_scatter(
-        contract_rows(inverse_block, residual), "pc", scatter_dimension=0, tiled=True
+    alpha_panel = lax.psum(contract_rows(inverse_block, residual), "pc")
+    panel_all = lax.all_gather(panel_points, "pc", axis=0, tiled=True)
+    test_own = lax.dynamic_slice_in_dim(test_points, own * rows, rows, 0)
+    test_norms = jnp.einsum(
+        "nd,nd->n", test_own, test_own, preferred_element_type=jnp.float32
     )
-    test_norms = jnp.einsum(
-        "nd,nd->n", test_points, test_points, preferred_element_type=jnp.float32
-    )
-    kern = arc_kernel(panel_points, test_points, test_norms)
-    update = lax.psum_scatter(
-        contract_rows(kern, alpha_panel), "pc", scatter_dimension=0, tiled=True
-    )
+    kern = lax.optimization_barrier(arc_kernel(panel_all, test_own, test_norms))
+    update = contract_rows(kern, alpha_panel)
     return predictions_in + update
 
 

time: 334 us -> 225 us (0.67); the launches traced: 329 us -> 225 us
  waiting for transfers between devices: 184 us -> 123 us
  matrix products: 95.3 us -> 60.9 us
  other arithmetic: 10.1 us -> 3.1 us
    reduce_scatter x1 -> x0, waiting for transfers between devices: 85.3 us -> none  [body(): lax.psum_scatter(contract_rows(kern, alpha_panel), 'pc', scatter_dimensio...]
    dot_general x2, matrix products: 79.4 us -> 7.94 us  [contract_rows(): lax.dot_general(left, right, (((0,), (0,)), ((), ())), precision=lax.Prec...]
    unnamed x4 -> x3, waiting for transfers between devices: 58.1 us -> 1.42 us
    all_gather x0 -> x1, waiting for transfers between devices: none -> 44.7 us  [body(): panel_all = lax.all_gather(panel_points, 'pc', axis=0, tiled=True)]
    dot_general x1, matrix products: 12.9 us -> 50 us  [arc_kernel(): cross = jnp.dot(panel, test.T, preferred_element_type=jnp.float32) / width]
    psum x0 -> x1, waiting for transfers between devices: none -> 32.4 us  [body(): alpha_panel = lax.psum(contract_rows(inverse_block, residual), 'pc')]
    dot_general x1, other arithmetic: 7.24 us -> 1.5 us  [body(): jnp.einsum('nd,nd->n', test_own, test_own, preferred_element_type=jnp.flo...]
    all_gather x1, waiting for transfers between devices: 41.2 us -> 44.7 us  [body(): lax.all_gather(alpha_below, 'pc', axis=0, tiled=True)]
  transfers between devices with their start and end apart: 3 -> 3, of which waited for: 3 -> 3; matrix products, arithmetic and copies ran while one was open for 6% -> 24% of each run, Pallas kernels for 0% -> 0%
where the time goes in v1:
time: 225 us
  waiting for transfers between devices  123 us (55%)
  matrix products  60.9 us (27%)
  blocking collectives  24.3 us (11%)
  between operations  13.2 us (6%)
  other arithmetic  3.1 us (1%)
    dot_general x1, matrix products, arc_kernel(): cross = jnp.dot(panel, test.T, preferred_element_type=jnp.float32) / width  50 us
    all_gather x1, waiting for transfers between devices, body(): panel_all = lax.all_gather(panel_points, 'pc', axis=0, tiled=True)  44.7 us
    all_gather x1, waiting for transfers between devices, body(): lax.all_gather(alpha_below, 'pc', axis=0, tiled=True)  44.7 us
    psum x1, waiting for transfers between devices, body(): alpha_panel = lax.psum(contract_rows(inverse_block, residual), 'pc')  32.4 us
    psum x1, blocking collectives, body(): carried = lax.psum(partial_sum, 'pr')  24.3 us
    dot_general x2, matrix products, contract_rows(): lax.dot_general(left, right, (((0,), (0,)), ((), ())), precision=lax.Prec...  7.94 us
  transfers between devices with their start and end apart: 3, of which 3 were waited for; matrix products, arithmetic and copies ran while one was open for 24% of the time, Pallas kernels for 0%

profile of v1, /device:TPU:0, one launch (start us, length us, event | category | flops | bytes accessed | tf_op | source)
XLA Modules:
  0.0 224.8 jit_solution(2418785735525503081)
XLA Ops:
  6.5 0.0 copy-start
  6.5 0.0 copy-start.3
  6.5 0.0 copy-start.4
  6.5 0.0 all-gather.3.cloned.1.call-start
  6.5 0.7 all-gather.3.cloned.1.call-update
  7.3 0.0 all-gather.5.cloned.1.call-start
  7.3 0.7 all-gather.5.cloned.1.call-update
  8.0 0.0 all-reduce.2.cloned.1.call-start
  8.1 1.5 fusion
  9.6 44.7 %all-gather.3.cloned.1.call-done = bf16[1024,512]{1,0:T(8,128)(2,1)} async-done(((bf16[64,512]{1,0:T(8,128)(2,1)}), bf16[1024,512]{1,0:T(8,128)(2,1)}) %all-gather.3.cloned.1.call-update) | async-done | bytes 1048592 | tf_op jit(solution)/shard_map/all_gather | solution.py:58
  54.3 0.0 copy-start.1
  54.3 1.6 fusion.1
  55.9 44.7 %all-gather.5.cloned.1.call-done = f32[4096,128]{1,0:T(8,128)} async-done(((f32[256,128]{1,0:T(8,128)}), f32[4096,128]{1,0:T(8,128)}) %all-gather.5.cloned.1.call-update) | async-done | bytes 2097168 | tf_op jit(solution)/shard_map/all_gather | solution.py:51
  100.6 0.0 copy-done
  100.6 3.0 %fusion.5 = f32[64,128]{1,0:T(8,128)S(1)} fusion(f32[64,4096]{1,0:T(8,128)S(1)} %copy-done, f32[4096,128]{1,0:T(8,128)} %all-gather.5.cloned.1.call-done), kind=kOutput, calls=%fused_computation.19 | convolution fusion | flops 402653184 | bytes 3178496 | tf_op jit(solution)/shard_map/dot_general | solution.py:49
  103.6 24.3 %psum.14 = f32[64,128]{1,0:T(8,128)S(1)} all-reduce(f32[64,128]{1,0:T(8,128)S(1)} %fusion.5), channel_id=1, replica_groups=mesh['pr'=8,'pc'=16] {'pr'}, use_global_device_ids=true, to_apply=%region_0.0 | all-reduce | flops 8192 | bytes 65536 | tf_op jit(solution)/shard_map/psum | solution.py:55
  127.9 0.0 copy-done.3
  127.9 0.0 copy-done.4
  127.9 1.4 convolution_bitcast_fusion
  129.3 0.0 all-reduce.2.cloned.1.call-update
  129.3 0.0 copy-done.1
  129.4 0.0 copy-start.2
  129.4 50.0 %multiply_add_fusion = f32[1024,1024]{0,1:T(8,128)} fusion(bf16[1024,512]{1,0:T(8,128)(2,1)S(1)} %copy-done.1, f32[1024]{0:T(1024)S(1)} %get-tuple-element.12, f32[1024]{0:T(1024)S(1)} %get-tuple-element.8, f32[1024]{0:T(1024)S(1)} %get-tuple-element.11, f32[1024]{0:T(1024)S(1)} %get-tuple-element.7, f32[1024]{0:T(1024)S(1)} %get-tuple-element.10, ...), kind=kOutput, calls=%fused_computation.1 | convolution fusion | flops 1130364928 | bytes 6324228 | tf_op jit(solution)/shard_map/dot_general | solution.py:17
  179.3 32.4 %all-reduce.2.cloned.1.call-done = f32[1024,128]{0,1:T(8,128)} async-done(((f32[1024,128]{0,1:T(8,128)}), f32[1024,128]{0,1:T(8,128)}) %all-reduce.2.cloned.1.call-update) | async-done | bytes 524304 | tf_op jit(solution)/shard_map/psum | solution.py:57
  211.7 0.0 copy-done.2
  211.7 6.5 %convolution_add_fusion = f32[1024,128]{1,0:T(8,128)} fusion(f32[1024,128]{1,0:T(8,128)S(1)} %copy-done.2, f32[1024,1024]{0,1:T(8,128)} %multiply_add_fusion, f32[1024,128]{0,1:T(8,128)} %all-reduce.2.cloned.1.call-done), kind=kOutput, calls=%fused_computation.6 | convolution fusion | flops 1610743808 | bytes 5767168 | tf_op jit(solution)/shard_map/dot_general | solution.py:35
  (2 shorter events, 0.0 us)
Async XLA Ops:
  6.5 94.1 %copy-start = (f32[64,4096]{1,0:T(8,128)S(1)}, f32[64,4096]{1,0:T(8,128)}, u32[]{:S(2)}) copy-start(f32[64,4096]{1,0:T(8,128)} %param.9) | copy-start | bytes 3145732
  6.5 121.4 %copy-start.3 = (f32[64,1024]{1,0:T(8,128)S(1)}, f32[64,1024]{1,0:T(8,128)}, u32[]{:S(2)}) copy-start(f32[64,1024]{1,0:T(8,128)} %param.12) | copy-start | bytes 786436
  6.5 121.4 %copy-start.4 = (f32[64,128]{1,0:T(8,128)S(1)}, f32[64,128]{1,0:T(8,128)}, u32[]{:S(2)}) copy-start(f32[64,128]{1,0:T(8,128)} %param.11) | copy-start | bytes 98308
  6.5 47.8 %all-gather.3.cloned.1.call-start = ((), (), s32[]{:S(2)}) async-start(), calls=%async_computation | async-start | bytes 1114112 | tf_op jit(solution)/shard_map/all_gather | solution.py:58
  7.3 93.4 %all-gather.5.cloned.1.call-start = ((), (), s32[]{:S(2)}) async-start(), calls=%async_computation.1 | async-start | bytes 2228224 | tf_op jit(solution)/shard_map/all_gather | solution.py:51
  8.0 203.7 %all-reduce.2.cloned.1.call-start = ((), (), s32[]{:S(2)}) async-start(), calls=%async_computation.2 | async-start | bytes 1048576 | tf_op jit(solution)/shard_map/psum | solution.py:57
  54.3 75.0 %copy-start.1 = (bf16[1024,512]{1,0:T(8,128)(2,1)S(1)}, bf16[1024,512]{1,0:T(8,128)(2,1)}, u32[]{:S(2)}) copy-start(bf16[1024,512]{1,0:T(8,128)(2,1)} %all-gather.3.cloned.1.call-done) | copy-start | bytes 3145732
  129.4 82.4 %copy-start.2 = (f32[1024,128]{1,0:T(8,128)S(1)}, f32[1024,128]{1,0:T(8,128)}, u32[]{:S(2)}) copy-start(f32[1024,128]{1,0:T(8,128)} %param.13) | copy-start | bytes 1572868
Sparse Core Ops, SparseCore 0:
  9.5 44.8 all-gather.2
  56.5 44.1 all-gather.4
  129.5 82.2 all-reduce.1

commit v2 on v1

--- a/solution.py
+++ b/solution.py
@@ -41,21 +41,41 @@
     )
 
 
+def gather_rows(x, axis, n):
+    copies = jnp.broadcast_to(x[None], (n,) + x.shape)
+    return lax.all_to_all(copies, axis, 0, 0, tiled=False).reshape((-1,) + x.shape[1:])
+
+
+def sum_rows(x, axis, n):
+    blocks = lax.all_to_all(x.reshape((n, -1) + x.shape[1:]), axis, 0, 0, tiled=False)
+    return gather_rows(blocks.sum(0), axis, n)
+
+
+def butterfly_sum(x, axis, n):
+    step = 1
+    while step < n:
+        x = x + lax.ppermute(x, axis, [(i, i ^ step) for i in range(n)])
+        step *= 2
+    return x
+
+
 def body(
     test_points, panel_points, factor_rows, alpha_below, targets, inverse_block, predictions_in
 ):
+    n_pr = lax.axis_size("pr")
+    n_pc = lax.axis_size("pc")
     rows = predictions_in.shape[0]
     own = lax.axis_index("pc")
+    panel_all = lax.all_gather(panel_points, "pc", axis=0, tiled=True)
     partial_sum = jnp.dot(
         factor_rows,
-        lax.all_gather(alpha_below, "pc", axis=0, tiled=True),
+        gather_rows(alpha_below, "pc", n_pc),
         precision=lax.Precision.HIGHEST,
         preferred_element_type=jnp.float32,
     )
-    carried = lax.psum(partial_sum, "pr")
+    carried = butterfly_sum(partial_sum, "pr", n_pr)
     residual = targets - carried
-    alpha_panel = lax.psum(contract_rows(inverse_block, residual), "pc")
-    panel_all = lax.all_gather(panel_points, "pc", axis=0, tiled=True)
+    alpha_panel = sum_rows(contract_rows(inverse_block, residual), "pc", n_pc)
     test_own = lax.dynamic_slice_in_dim(test_points, own * rows, rows, 0)
     test_norms = jnp.einsum(
         "nd,nd->n", test_own, test_own, preferred_element_type=jnp.float32

time: 225 us -> 148 us (0.66)
  waiting for transfers between devices: 123 us -> 45.7 us
  blocking collectives: 24.3 us -> 0 us
  starting transfers between devices: 0.08 us -> 22.1 us
  local copies, waits for them, and re-layouts: 0.02 us -> 4.39 us
    all_gather x1 -> x0, waiting for transfers between devices: 44.7 us -> none  [body(): lax.all_gather(alpha_below, 'pc', axis=0, tiled=True)]
    all_gather x1, waiting for transfers between devices: 44.7 us -> 9.62 us  [body(): panel_all = lax.all_gather(panel_points, 'pc', axis=0, tiled=True)]
    psum x1 -> x0, waiting for transfers between devices: 32.4 us -> none  [body(): alpha_panel = lax.psum(contract_rows(inverse_block, residual), 'pc')]
    all_to_all x0 -> x3, waiting for transfers between devices: none -> 31.8 us  [the longest x2 31.3 us: gather_rows(): lax.all_to_all(copies, axis, 0, 0, tiled=False).reshape((-1,) + x.shape[1:])]
    psum x1 -> x0, blocking collectives: 24.3 us -> none  [body(): carried = lax.psum(partial_sum, 'pr')]
    all_to_all x0 -> x3, starting transfers between devices: none -> 16 us  [the longest x2 12.5 us: gather_rows(): lax.all_to_all(copies, axis, 0, 0, tiled=False).reshape((-1,) + x.shape[1:])]
    ppermute x0 -> x3, starting transfers between devices: none -> 5.97 us  [butterfly_sum(): x = x + lax.ppermute(x, axis, [(i, i ^ step) for i in range(n)])]
    ppermute x0 -> x3, waiting for transfers between devices: none -> 3.58 us  [butterfly_sum(): x = x + lax.ppermute(x, axis, [(i, i ^ step) for i in range(n)])]
  transfers between devices with their start and end apart: 3 -> 7, of which waited for: 3 -> 6; matrix products, arithmetic and copies ran while one was open for 24% -> 38% of each run, Pallas kernels for 0% -> 0%
where the time goes in v2:
time: 148 us; the launch traced here: 147 us
  matrix products  58.8 us (40%)
  waiting for transfers between devices  45.7 us (31%)
  starting transfers between devices  22.1 us (15%)
  between operations  13.5 us (9%)
  local copies, waits for them, and re-layouts  4.39 us (3%)
  other arithmetic  3.05 us (2%)
    dot_general x1, matrix products, arc_kernel(): cross = jnp.dot(panel, test.T, preferred_element_type=jnp.float32) / width  50.3 us
    all_to_all x2, waiting for transfers between devices, gather_rows(): lax.all_to_all(copies, axis, 0, 0, tiled=False).reshape((-1,) + x.shape[1:])  31.3 us
    all_to_all x2, starting transfers between devices, gather_rows(): lax.all_to_all(copies, axis, 0, 0, tiled=False).reshape((-1,) + x.shape[1:])  12.5 us
    all_gather x1, waiting for transfers between devices, body(): panel_all = lax.all_gather(panel_points, 'pc', axis=0, tiled=True)  9.62 us
    dot_general x2, matrix products, contract_rows(): lax.dot_general(left, right, (((0,), (0,)), ((), ())), precision=lax.Prec...  7.03 us
    ppermute x3, starting transfers between devices, butterfly_sum(): x = x + lax.ppermute(x, axis, [(i, i ^ step) for i in range(n)])  5.97 us
    ppermute x3, waiting for transfers between devices, butterfly_sum(): x = x + lax.ppermute(x, axis, [(i, i ^ step) for i in range(n)])  3.58 us
    all_to_all x1, starting transfers between devices, sum_rows(): lax.all_to_all(x.reshape((n, -1) + x.shape[1:]), axis, 0, 0, tiled=False)  3.58 us
  transfers between devices with their start and end apart: 7, of which 6 were waited for; matrix products, arithmetic and copies ran while one was open for 38% of the time, Pallas kernels for 0%

profile of v2, /device:TPU:0, one launch (start us, length us, event | category | flops | bytes accessed | tf_op | source)
XLA Modules:
  0.0 147.5 jit_solution(9509684644393737140)
XLA Ops:
  6.5 0.0 copy-start
  6.5 2.5 %broadcast_in_dim.4 = f32[16,256,128]{2,1,0:T(8,128)} broadcast(f32[256,128]{1,0:T(8,128)} %param.10), dimensions={1,2} | broadcast | bytes 2228224 | tf_op jit(solution)/shard_map/broadcast_in_dim | solution.py:45
  9.1 0.0 copy-start.2
  9.1 0.0 copy-start.3
  9.1 7.3 %all-to-all-start = ((f32[16,256,128]{2,1,0:T(8,128)}), f32[16,256,128]{2,1,0:T(8,128)S(1)}, u32[]{:S(2)}, u32[]{:S(2)}) async-start(f32[16,256,128]{2,1,0:T(8,128)} %broadcast_in_dim.4), calls=%async_computation | async-start | bytes 4194304 | tf_op jit(solution)/shard_map/all_to_all | solution.py:46
  16.4 0.0 all-gather.2.cloned.1.call-start
  16.4 0.7 all-gather.2.cloned.1.call-update
  17.1 31.3 %all-to-all-done = f32[16,256,128]{2,1,0:T(8,128)S(1)} async-done(((f32[16,256,128]{2,1,0:T(8,128)}), f32[16,256,128]{2,1,0:T(8,128)S(1)}, u32[]{:S(2)}, u32[]{:S(2)}) %all-to-all-start) | async-done | bytes 2097184 | tf_op jit(solution)/shard_map/all_to_all | solution.py:46
  48.4 0.0 copy-done
  48.4 1.4 fusion.6
  49.8 0.1 collective-permute-start
  49.9 1.2 collective-permute-done
  51.1 1.9 %collective-permute-start.1 = (f32[64,128]{1,0:T(8,128)S(1)}, f32[64,128]{1,0:T(8,128)S(1)}, u32[]{:S(2)}, u32[]{:S(2)}) collective-permute-start(f32[64,128]{1,0:T(8,128)S(1)} %add.113), channel_id=1, source_target_pairs={{0,32},{16,48},{32,0},{48,16},{64,96},{80,112},{96,64},{112,80},{1... | collective-permute-start | bytes 98312 | tf_op jit(solution)/shard_map/ppermute | solution.py:57
  53.0 2.0 %collective-permute-done.1 = f32[64,128]{1,0:T(8,128)S(1)} collective-permute-done((f32[64,128]{1,0:T(8,128)S(1)}, f32[64,128]{1,0:T(8,128)S(1)}, u32[]{:S(2)}, u32[]{:S(2)}) %collective-permute-start.1) | collective-permute-done | bytes 32800 | tf_op jit(solution)/shard_map/ppermute | solution.py:57
  55.0 4.0 %collective-permute-start.2 = (f32[64,128]{1,0:T(8,128)S(1)}, f32[64,128]{1,0:T(8,128)S(1)}, u32[]{:S(2)}, u32[]{:S(2)}) collective-permute-start(f32[64,128]{1,0:T(8,128)S(1)} %add.114), channel_id=1, source_target_pairs={{0,64},{16,80},{32,96},{48,112},{64,0},{80,16},{96,32},{112,48},{1... | collective-permute-start | bytes 98312 | tf_op jit(solution)/shard_map/ppermute | solution.py:57
  59.0 1.5 %fusion = f32[1024]{0:T(1024)S(1)} fusion(bf16[16384,512]{1,0:T(8,128)(2,1)} %param.7, s32[]{:T(128)S(6)} %select_n.3), kind=kLoop, calls=%fused_computation.3 | loop fusion | flops 1571840 | bytes 1052676 | tf_op jit(solution)/shard_map/nd,nd->n/dot_general | solution.py:80
  60.5 0.4 collective-permute-done.2
  60.9 0.0 copy-done.2
  60.9 0.0 copy-done.3
  60.9 0.6 convolution_bitcast_fusion
  61.5 1.0 copy.10
  62.5 3.6 %all-to-all-start.1 = ((f32[16,64,128]{2,1,0:T(8,128)}), f32[16,64,128]{2,1,0:T(8,128)S(1)}, u32[]{:S(2)}, u32[]{:S(2)}) async-start(f32[16,64,128]{2,1,0:T(8,128)} %bitcast.3), calls=%async_computation.1 | async-start | bytes 1048576 | tf_op jit(solution)/shard_map/all_to_all | solution.py:50
  66.1 9.6 %all-gather.2.cloned.1.call-done = bf16[1024,512]{1,0:T(8,128)(2,1)} async-done(((bf16[64,512]{1,0:T(8,128)(2,1)}), bf16[1024,512]{1,0:T(8,128)(2,1)}) %all-gather.2.cloned.1.call-update) | async-done | bytes 1048592 | tf_op jit(solution)/shard_map/all_gather | solution.py:69
  75.7 1.5 %fusion.1 = f32[1024]{0:T(1024)S(1)} fusion(bf16[1024,512]{1,0:T(8,128)(2,1)} %all-gather.2.cloned.1.call-done), kind=kLoop, calls=%fused_computation.5 | loop fusion | flops 1571840 | bytes 1052672 | tf_op jit(solution)/shard_map/pd,pd->p/dot_general | solution.py:18
  77.3 0.5 all-to-all-done.1
  77.8 0.8 broadcast_in_dim.5
  78.7 5.2 %all-to-all-start.2 = ((f32[16,64,128]{2,1,0:T(8,128)}), f32[16,64,128]{2,1,0:T(8,128)S(1)}, u32[]{:S(2)}, u32[]{:S(2)}) async-start(f32[16,64,128]{2,1,0:T(8,128)} %broadcast_in_dim.5), calls=%async_computation.2 | async-start | bytes 1048576 | tf_op jit(solution)/shard_map/all_to_all | solution.py:46
  83.8 0.0 copy-start.1
  83.9 50.3 %multiply_add_fusion = f32[1024,1024]{0,1:T(8,128)} fusion(bf16[1024,512]{1,0:T(8,128)(2,1)} %all-gather.2.cloned.1.call-done, f32[1024]{0:T(1024)S(1)} %get-tuple-element.12, f32[1024]{0:T(1024)S(1)} %get-tuple-element.8, f32[1024]{0:T(1024)S(1)} %get-tuple-element.11, f32[1024]{0:T(1024)S(1)} %get-tuple-element.7, f32[1024]{0:T(1024)S(1)} %get-tuple-element.10, ...), kind=kOutput, calls=%fused_computation.1 | convolution fusion | flops 1130364928 | bytes 6324228 | tf_op jit(solution)/shard_map/dot_general | solution.py:17
  134.2 0.0 all-to-all-done.2
  134.2 0.0 copy-done.1
  134.2 6.4 %convolution_add_fusion = f32[1024,128]{1,0:T(8,128)} fusion(f32[1024,128]{1,0:T(8,128)S(1)} %copy-done.1, f32[1024,1024]{0,1:T(8,128)} %multiply_add_fusion, f32[1024,128]{1,0:T(8,128)S(1)} %bitcast.16), kind=kOutput, calls=%fused_computation.6 | convolution fusion | flops 1610743808 | bytes 5767168 | tf_op jit(solution)/shard_map/dot_general | solution.py:35
  (5 shorter events, 0.1 us)
Async XLA Ops:
  6.5 41.9 %copy-start = (f32[64,4096]{1,0:T(8,128)S(1)}, f32[64,4096]{1,0:T(8,128)}, u32[]{:S(2)}) copy-start(f32[64,4096]{1,0:T(8,128)} %param.9) | copy-start | bytes 3145732
  9.1 51.8 %copy-start.2 = (f32[64,1024]{1,0:T(8,128)S(1)}, f32[64,1024]{1,0:T(8,128)}, u32[]{:S(2)}) copy-start(f32[64,1024]{1,0:T(8,128)} %param.12) | copy-start | bytes 786436
  9.1 51.8 %copy-start.3 = (f32[64,128]{1,0:T(8,128)S(1)}, f32[64,128]{1,0:T(8,128)}, u32[]{:S(2)}) copy-start(f32[64,128]{1,0:T(8,128)} %param.11) | copy-start | bytes 98308
  9.1 39.3 %all-to-all-start = ((f32[16,256,128]{2,1,0:T(8,128)}), f32[16,256,128]{2,1,0:T(8,128)S(1)}, u32[]{:S(2)}, u32[]{:S(2)}) async-start(f32[16,256,128]{2,1,0:T(8,128)} %broadcast_in_dim.4), calls=%async_computation | async-start | bytes 4194304 | tf_op jit(solution)/shard_map/all_to_all | solution.py:46
  16.4 59.4 %all-gather.2.cloned.1.call-start = ((), (), s32[]{:S(2)}) async-start(), calls=%async_computation.3 | async-start | bytes 1114112 | tf_op jit(solution)/shard_map/all_gather | solution.py:69
  49.8 1.3 collective-permute-start
  51.1 3.9 %collective-permute-start.1 = (f32[64,128]{1,0:T(8,128)S(1)}, f32[64,128]{1,0:T(8,128)S(1)}, u32[]{:S(2)}, u32[]{:S(2)}) collective-permute-start(f32[64,128]{1,0:T(8,128)S(1)} %add.113), channel_id=1, source_target_pairs={{0,32},{16,48},{32,0},{48,16},{64,96},{80,112},{96,64},{112,80},{1... | collective-permute-start | bytes 98312 | tf_op jit(solution)/shard_map/ppermute | solution.py:57
  55.0 5.9 %collective-permute-start.2 = (f32[64,128]{1,0:T(8,128)S(1)}, f32[64,128]{1,0:T(8,128)S(1)}, u32[]{:S(2)}, u32[]{:S(2)}) collective-permute-start(f32[64,128]{1,0:T(8,128)S(1)} %add.114), channel_id=1, source_target_pairs={{0,64},{16,80},{32,96},{48,112},{64,0},{80,16},{96,32},{112,48},{1... | collective-permute-start | bytes 98312 | tf_op jit(solution)/shard_map/ppermute | solution.py:57
  62.5 15.3 %all-to-all-start.1 = ((f32[16,64,128]{2,1,0:T(8,128)}), f32[16,64,128]{2,1,0:T(8,128)S(1)}, u32[]{:S(2)}, u32[]{:S(2)}) async-start(f32[16,64,128]{2,1,0:T(8,128)} %bitcast.3), calls=%async_computation.1 | async-start | bytes 1048576 | tf_op jit(solution)/shard_map/all_to_all | solution.py:50
  78.7 55.6 %all-to-all-start.2 = ((f32[16,64,128]{2,1,0:T(8,128)}), f32[16,64,128]{2,1,0:T(8,128)S(1)}, u32[]{:S(2)}, u32[]{:S(2)}) async-start(f32[16,64,128]{2,1,0:T(8,128)} %broadcast_in_dim.5), calls=%async_computation.2 | async-start | bytes 1048576 | tf_op jit(solution)/shard_map/all_to_all | solution.py:46
  83.8 50.4 %copy-start.1 = (f32[1024,128]{1,0:T(8,128)S(1)}, f32[1024,128]{1,0:T(8,128)}, u32[]{:S(2)}) copy-start(f32[1024,128]{1,0:T(8,128)} %param.13) | copy-start | bytes 1572868
Sparse Core Ops, SparseCore 0:
  19.3 56.3 all-gather.1

commit v3 on v2

--- a/solution.py
+++ b/solution.py
@@ -12,6 +12,22 @@
 weight_var = 2.0
 
 
+ASIN_COEFFS = (4.2163199048e-2, 2.4181311049e-2, 4.5470025998e-2, 7.4953002686e-2, 1.6666752422e-1)
+
+
+def reflected_arccos(cosine):
+    size = jnp.abs(cosine)
+    big = size > 0.5
+    z = jnp.where(big, 0.5 - 0.5 * size, size * size)
+    x = jnp.where(big, jnp.sqrt(z), size)
+    poly = ASIN_COEFFS[0]
+    for coeff in ASIN_COEFFS[1:]:
+        poly = poly * z + coeff
+    arcsine = x + x * z * poly
+    arccos_size = jnp.where(big, 2.0 * arcsine, 0.5 * math.pi - arcsine)
+    return jnp.where(cosine >= 0.0, math.pi - arccos_size, arccos_size)
+
+
 def arc_kernel(panel, test, test_norms):
     width = panel.shape[1]
     cross = jnp.dot(panel, test.T, preferred_element_type=jnp.float32) / width
@@ -20,11 +36,13 @@
     panel_k = bias_var + weight_var * panel_var
     test_k = bias_var + weight_var * (test_norms / width)
     for level in range(LAYERS):
-        spread = jnp.sqrt(panel_k[:, None] * test_k[None, :])
-        cosine = kern / spread
-        theta = jnp.arccos(cosine)
-        kern = bias_var + weight_var / (2.0 * math.pi) * spread * (
-            jnp.sqrt(1.0 - cosine * cosine) + (math.pi - theta) * cosine
+        panel_root = jnp.sqrt(panel_k)
+        test_root = jnp.sqrt(test_k)
+        spread = panel_root[:, None] * test_root[None, :]
+        inverse = (1.0 / panel_root)[:, None] * (1.0 / test_root)[None, :]
+        cosine = jnp.clip(kern * inverse, -1.0, 1.0)
+        kern = bias_var + weight_var / (2.0 * math.pi) * (
+            spread * jnp.sqrt(1.0 - cosine * cosine) + reflected_arccos(cosine) * kern
         )
         panel_k = bias_var + 0.5 * weight_var * panel_k
         test_k = bias_var + 0.5 * weight_var * test_k

time: 148 us -> 128 us (0.86)
  matrix products: 58.8 us -> 38.7 us
    dot_general x1, matrix products: 50.3 us -> 30.3 us  [arc_kernel(): cross = jnp.dot(panel, test.T, preferred_element_type=jnp.float32) / width]
  transfers between devices with their start and end apart: 7 -> 7, of which waited for: 6 -> 6; matrix products, arithmetic and copies ran while one was open for 38% -> 29% of each run, Pallas kernels for 0% -> 0%
where the time goes in v3:
time: 128 us; the launch traced here: 127 us
  waiting for transfers between devices  45.7 us (36%)
  matrix products  38.7 us (30%)
  starting transfers between devices  22.1 us (17%)
  between operations  13.5 us (11%)
  local copies, waits for them, and re-layouts  4.39 us (3%)
  other arithmetic  3.07 us (2%)
    all_to_all x2, waiting for transfers between devices, gather_rows(): lax.all_to_all(copies, axis, 0, 0, tiled=False).reshape((-1,) + x.shape[1:])  31.3 us
    dot_general x1, matrix products, arc_kernel(): cross = jnp.dot(panel, test.T, preferred_element_type=jnp.float32) / width  30.3 us
    all_to_all x2, starting transfers between devices, gather_rows(): lax.all_to_all(copies, axis, 0, 0, tiled=False).reshape((-1,) + x.shape[1:])  12.5 us
    all_gather x1, waiting for transfers between devices, body(): panel_all = lax.all_gather(panel_points, 'pc', axis=0, tiled=True)  9.61 us
    dot_general x2, matrix products, contract_rows(): lax.dot_general(left, right, (((0,), (0,)), ((), ())), precision=lax.Prec...  7.03 us
    ppermute x3, starting transfers between devices, butterfly_sum(): x = x + lax.ppermute(x, axis, [(i, i ^ step) for i in range(n)])  5.97 us
    ppermute x3, waiting for transfers between devices, butterfly_sum(): x = x + lax.ppermute(x, axis, [(i, i ^ step) for i in range(n)])  3.58 us
    all_to_all x1, starting transfers between devices, sum_rows(): lax.all_to_all(x.reshape((n, -1) + x.shape[1:]), axis, 0, 0, tiled=False)  3.58 us
  transfers between devices with their start and end apart: 7, of which 6 were waited for; matrix products, arithmetic and copies ran while one was open for 29% of the time, Pallas kernels for 0%

profile of v3, /device:TPU:0, one launch (start us, length us, event | category | flops | bytes accessed | tf_op | source)
XLA Modules:
  0.0 127.4 jit_solution(16064448198404152644)
XLA Ops:
  6.5 0.0 copy-start
  6.5 2.5 %broadcast_in_dim.4 = f32[16,256,128]{2,1,0:T(8,128)} broadcast(f32[256,128]{1,0:T(8,128)} %param.10), dimensions={1,2} | broadcast | bytes 2228224 | tf_op jit(solution)/shard_map/broadcast_in_dim | solution.py:63
  9.1 0.0 copy-start.2
  9.1 0.0 copy-start.3
  9.1 7.3 %all-to-all-start = ((f32[16,256,128]{2,1,0:T(8,128)}), f32[16,256,128]{2,1,0:T(8,128)S(1)}, u32[]{:S(2)}, u32[]{:S(2)}) async-start(f32[16,256,128]{2,1,0:T(8,128)} %broadcast_in_dim.4), calls=%async_computation | async-start | bytes 4194304 | tf_op jit(solution)/shard_map/all_to_all | solution.py:64
  16.4 0.0 all-gather.2.cloned.1.call-start
  16.4 0.7 all-gather.2.cloned.1.call-update
  17.1 31.3 %all-to-all-done = f32[16,256,128]{2,1,0:T(8,128)S(1)} async-done(((f32[16,256,128]{2,1,0:T(8,128)}), f32[16,256,128]{2,1,0:T(8,128)S(1)}, u32[]{:S(2)}, u32[]{:S(2)}) %all-to-all-start) | async-done | bytes 2097184 | tf_op jit(solution)/shard_map/all_to_all | solution.py:64
  48.4 0.0 copy-done
  48.4 1.4 %fusion.27 = f32[64,128]{1,0:T(8,128)S(1)} fusion(f32[64,4096]{1,0:T(8,128)S(1)} %copy-done, f32[4096,128]{1,0:T(8,128)S(1)} %bitcast.24), kind=kOutput, calls=%fused_computation.59 | convolution fusion | flops 402653184 | bytes 3178496 | tf_op jit(solution)/shard_map/dot_general | solution.py:88
  49.8 0.1 collective-permute-start
  49.9 1.2 collective-permute-done
  51.1 1.9 %collective-permute-start.1 = (f32[64,128]{1,0:T(8,128)S(1)}, f32[64,128]{1,0:T(8,128)S(1)}, u32[]{:S(2)}, u32[]{:S(2)}) collective-permute-start(f32[64,128]{1,0:T(8,128)S(1)} %add.193), channel_id=1, source_target_pairs={{0,32},{16,48},{32,0},{48,16},{64,96},{80,112},{96,64},{112,80},{1... | collective-permute-start | bytes 98312 | tf_op jit(solution)/shard_map/ppermute | solution.py:75
  53.0 2.0 %collective-permute-done.1 = f32[64,128]{1,0:T(8,128)S(1)} collective-permute-done((f32[64,128]{1,0:T(8,128)S(1)}, f32[64,128]{1,0:T(8,128)S(1)}, u32[]{:S(2)}, u32[]{:S(2)}) %collective-permute-start.1) | collective-permute-done | bytes 32800 | tf_op jit(solution)/shard_map/ppermute | solution.py:75
  55.0 4.0 %collective-permute-start.2 = (f32[64,128]{1,0:T(8,128)S(1)}, f32[64,128]{1,0:T(8,128)S(1)}, u32[]{:S(2)}, u32[]{:S(2)}) collective-permute-start(f32[64,128]{1,0:T(8,128)S(1)} %add.194), channel_id=1, source_target_pairs={{0,64},{16,80},{32,96},{48,112},{64,0},{80,16},{96,32},{112,48},{1... | collective-permute-start | bytes 98312 | tf_op jit(solution)/shard_map/ppermute | solution.py:75
  59.0 1.5 %fusion.21 = f32[1024]{0:T(1024)S(1)} fusion(bf16[16384,512]{1,0:T(8,128)(2,1)} %param.7, s32[]{:T(128)S(6)} %select_n.52), kind=kLoop, calls=%fused_computation.34 | loop fusion | flops 1571840 | bytes 1052676 | tf_op jit(solution)/shard_map/nd,nd->n/dot_general | solution.py:98
  60.5 0.4 collective-permute-done.2
  60.9 0.0 copy-done.2
  60.9 0.0 copy-done.3
  60.9 0.6 convolution_bitcast_fusion
  61.5 1.0 copy.10
  62.5 3.6 %all-to-all-start.1 = ((f32[16,64,128]{2,1,0:T(8,128)}), f32[16,64,128]{2,1,0:T(8,128)S(1)}, u32[]{:S(2)}, u32[]{:S(2)}) async-start(f32[16,64,128]{2,1,0:T(8,128)} %bitcast.3), calls=%async_computation.1 | async-start | bytes 1048576 | tf_op jit(solution)/shard_map/all_to_all | solution.py:68
  66.1 9.6 %all-gather.2.cloned.1.call-done = bf16[1024,512]{1,0:T(8,128)(2,1)} async-done(((bf16[64,512]{1,0:T(8,128)(2,1)}), bf16[1024,512]{1,0:T(8,128)(2,1)}) %all-gather.2.cloned.1.call-update) | async-done | bytes 1048592 | tf_op jit(solution)/shard_map/all_gather | solution.py:87
  75.7 1.5 %fusion.22 = f32[1024]{0:T(1024)S(1)} fusion(bf16[1024,512]{1,0:T(8,128)(2,1)} %all-gather.2.cloned.1.call-done), kind=kLoop, calls=%fused_computation.36 | loop fusion | flops 1571840 | bytes 1052672 | tf_op jit(solution)/shard_map/pd,pd->p/dot_general | solution.py:34
  77.3 0.5 all-to-all-done.1
  77.8 0.8 broadcast_in_dim.5
  78.7 5.2 %all-to-all-start.2 = ((f32[16,64,128]{2,1,0:T(8,128)}), f32[16,64,128]{2,1,0:T(8,128)S(1)}, u32[]{:S(2)}, u32[]{:S(2)}) async-start(f32[16,64,128]{2,1,0:T(8,128)} %broadcast_in_dim.5), calls=%async_computation.2 | async-start | bytes 1048576 | tf_op jit(solution)/shard_map/all_to_all | solution.py:64
  83.9 0.0 copy-start.1
  83.9 30.3 %fusion.15 = f32[1024,1024]{0,1:T(8,128)} fusion(bf16[1024,512]{1,0:T(8,128)(2,1)} %all-gather.2.cloned.1.call-done, f32[1024]{0:T(1024)S(1)} %get-tuple-element.17, f32[1024]{0:T(1024)S(1)} %get-tuple-element.9, f32[1024]{0:T(1024)S(1)} %get-tuple-element.16, f32[1024]{0:T(1024)S(1)} %get-tuple-element.8, f32[1024]{0:T(1024)S(1)} %get-tuple-element.15, ...), kind=kOutput, calls=%fused_computation.19 | convolution fusion | flops 1218445312 | bytes 6356996 | tf_op jit(solution)/shard_map/dot_general | solution.py:33
  114.2 0.0 all-to-all-done.2
  114.2 0.0 copy-done.1
  114.2 6.4 %convolution_add_fusion = f32[1024,128]{1,0:T(8,128)} fusion(f32[1024,128]{1,0:T(8,128)S(1)} %copy-done.1, f32[1024,1024]{0,1:T(8,128)} %fusion.15, f32[1024,128]{1,0:T(8,128)S(1)} %bitcast.25), kind=kOutput, calls=%fused_computation.37 | convolution fusion | flops 1610743808 | bytes 5767168 | tf_op jit(solution)/shard_map/dot_general | solution.py:53
  (5 shorter events, 0.1 us)
Async XLA Ops:
  6.5 41.9 %copy-start = (f32[64,4096]{1,0:T(8,128)S(1)}, f32[64,4096]{1,0:T(8,128)}, u32[]{:S(2)}) copy-start(f32[64,4096]{1,0:T(8,128)} %param.9) | copy-start | bytes 3145732
  9.1 51.8 %copy-start.2 = (f32[64,1024]{1,0:T(8,128)S(1)}, f32[64,1024]{1,0:T(8,128)}, u32[]{:S(2)}) copy-start(f32[64,1024]{1,0:T(8,128)} %param.12) | copy-start | bytes 786436
  9.1 51.8 %copy-start.3 = (f32[64,128]{1,0:T(8,128)S(1)}, f32[64,128]{1,0:T(8,128)}, u32[]{:S(2)}) copy-start(f32[64,128]{1,0:T(8,128)} %param.11) | copy-start | bytes 98308
  9.1 39.3 %all-to-all-start = ((f32[16,256,128]{2,1,0:T(8,128)}), f32[16,256,128]{2,1,0:T(8,128)S(1)}, u32[]{:S(2)}, u32[]{:S(2)}) async-start(f32[16,256,128]{2,1,0:T(8,128)} %broadcast_in_dim.4), calls=%async_computation | async-start | bytes 4194304 | tf_op jit(solution)/shard_map/all_to_all | solution.py:64
  16.4 59.4 %all-gather.2.cloned.1.call-start = ((), (), s32[]{:S(2)}) async-start(), calls=%async_computation.3 | async-start | bytes 1114112 | tf_op jit(solution)/shard_map/all_gather | solution.py:87
  49.8 1.3 %collective-permute-start = (f32[64,128]{1,0:T(8,128)S(1)}, f32[64,128]{1,0:T(8,128)S(1)}, u32[]{:S(2)}, u32[]{:S(2)}) collective-permute-start(f32[64,128]{1,0:T(8,128)S(1)} %fusion.27), channel_id=1, source_target_pairs={{0,16},{16,0},{32,48},{48,32},{64,80},{80,64},{96,112},{112,96},{1... | collective-permute-start | bytes 98312 | tf_op jit(solution)/shard_map/ppermute | solution.py:75
  51.1 3.9 %collective-permute-start.1 = (f32[64,128]{1,0:T(8,128)S(1)}, f32[64,128]{1,0:T(8,128)S(1)}, u32[]{:S(2)}, u32[]{:S(2)}) collective-permute-start(f32[64,128]{1,0:T(8,128)S(1)} %add.193), channel_id=1, source_target_pairs={{0,32},{16,48},{32,0},{48,16},{64,96},{80,112},{96,64},{112,80},{1... | collective-permute-start | bytes 98312 | tf_op jit(solution)/shard_map/ppermute | solution.py:75
  55.0 5.9 %collective-permute-start.2 = (f32[64,128]{1,0:T(8,128)S(1)}, f32[64,128]{1,0:T(8,128)S(1)}, u32[]{:S(2)}, u32[]{:S(2)}) collective-permute-start(f32[64,128]{1,0:T(8,128)S(1)} %add.194), channel_id=1, source_target_pairs={{0,64},{16,80},{32,96},{48,112},{64,0},{80,16},{96,32},{112,48},{1... | collective-permute-start | bytes 98312 | tf_op jit(solution)/shard_map/ppermute | solution.py:75
  62.5 15.3 %all-to-all-start.1 = ((f32[16,64,128]{2,1,0:T(8,128)}), f32[16,64,128]{2,1,0:T(8,128)S(1)}, u32[]{:S(2)}, u32[]{:S(2)}) async-start(f32[16,64,128]{2,1,0:T(8,128)} %bitcast.3), calls=%async_computation.1 | async-start | bytes 1048576 | tf_op jit(solution)/shard_map/all_to_all | solution.py:68
  78.7 35.5 %all-to-all-start.2 = ((f32[16,64,128]{2,1,0:T(8,128)}), f32[16,64,128]{2,1,0:T(8,128)S(1)}, u32[]{:S(2)}, u32[]{:S(2)}) async-start(f32[16,64,128]{2,1,0:T(8,128)} %broadcast_in_dim.5), calls=%async_computation.2 | async-start | bytes 1048576 | tf_op jit(solution)/shard_map/all_to_all | solution.py:64
  83.9 30.3 %copy-start.1 = (f32[1024,128]{1,0:T(8,128)S(1)}, f32[1024,128]{1,0:T(8,128)}, u32[]{:S(2)}) copy-start(f32[1024,128]{1,0:T(8,128)} %param.13) | copy-start | bytes 1572868
Sparse Core Ops, SparseCore 0:
  19.3 56.3 all-gather.1

commit v4 on v3

--- a/solution.py
+++ b/solution.py
@@ -84,21 +84,23 @@
     n_pc = lax.axis_size("pc")
     rows = predictions_in.shape[0]
     own = lax.axis_index("pc")
-    panel_all = lax.all_gather(panel_points, "pc", axis=0, tiled=True)
+    panel_all = gather_rows(panel_points, "pc", n_pc)
+    test_own = lax.dynamic_slice_in_dim(test_points, own * rows, rows, 0)
+    test_norms = jnp.einsum(
+        "nd,nd->n", test_own, test_own, preferred_element_type=jnp.float32
+    )
+    kern = arc_kernel(panel_all, test_own, test_norms)
+    gathered = gather_rows(alpha_below, "pc", n_pc)
+    kern, gathered = lax.optimization_barrier((kern, gathered))
     partial_sum = jnp.dot(
         factor_rows,
-        gather_rows(alpha_below, "pc", n_pc),
+        gathered,
         precision=lax.Precision.HIGHEST,
         preferred_element_type=jnp.float32,
     )
     carried = butterfly_sum(partial_sum, "pr", n_pr)
     residual = targets - carried
     alpha_panel = sum_rows(contract_rows(inverse_block, residual), "pc", n_pc)
-    test_own = lax.dynamic_slice_in_dim(test_points, own * rows, rows, 0)
-    test_norms = jnp.einsum(
-        "nd,nd->n", test_own, test_own, preferred_element_type=jnp.float32
-    )
-    kern = lax.optimization_barrier(arc_kernel(panel_all, test_own, test_norms))
     update = contract_rows(kern, alpha_panel)
     return predictions_in + update
 

time: 128 us -> 115 us (0.90)
  blocking collectives: 0 us -> 30.2 us
  waiting for transfers between devices: 45.7 us -> 21.2 us
  between operations: 13.5 us -> 0.12 us
  starting transfers between devices: 22.1 us -> 16.7 us
    all_to_all x0 -> x2, blocking collectives: none -> 30.2 us  [the longest x1 17.1 us: sum_rows(): lax.all_to_all(x.reshape((n, -1) + x.shape[1:]), axis, 0, 0, tiled=False)]
    all_to_all x2, waiting for transfers between devices: 31.3 us -> 16.1 us  [gather_rows(): lax.all_to_all(copies, axis, 0, 0, tiled=False).reshape((-1,) + x.shape[1:])]
    all_gather x1 -> x0, waiting for transfers between devices: 9.61 us -> none  [body(): panel_all = lax.all_gather(panel_points, 'pc', axis=0, tiled=True)]
    all_to_all x1 -> x0, starting transfers between devices: 3.58 us -> none  [sum_rows(): lax.all_to_all(x.reshape((n, -1) + x.shape[1:]), axis, 0, 0, tiled=False)]
    all_to_all x2, starting transfers between devices: 12.5 us -> 10.9 us  [gather_rows(): lax.all_to_all(copies, axis, 0, 0, tiled=False).reshape((-1,) + x.shape[1:])]
    ppermute x3, waiting for transfers between devices: 3.58 us -> 5.09 us  [butterfly_sum(): x = x + lax.ppermute(x, axis, [(i, i ^ step) for i in range(n)])]
    broadcast_in_dim x2 -> x3, local copies, waits for them, and re-layouts: 3.38 us -> 3.69 us  [gather_rows(): copies = jnp.broadcast_to(x[None], (n,) + x.shape)]
  transfers between devices with their start and end apart: 7 -> 5, of which waited for: 6 -> 4; matrix products, arithmetic and copies ran while one was open for 29% -> 29% of each run, Pallas kernels for 0% -> 0%
where the time goes in v4:
time: 115 us; the launch traced here: 114 us
  matrix products  38.8 us (34%)
  blocking collectives  30.2 us (26%)
  waiting for transfers between devices  21.2 us (18%)
  starting transfers between devices  16.7 us (15%)
  local copies, waits for them, and re-layouts  3.91 us (3%)
  other arithmetic  3.08 us (3%)
    dot_general x1, matrix products, arc_kernel(): cross = jnp.dot(panel, test.T, preferred_element_type=jnp.float32) / width  30.3 us
    all_to_all x1, blocking collectives, sum_rows(): lax.all_to_all(x.reshape((n, -1) + x.shape[1:]), axis, 0, 0, tiled=False)  17.1 us
    all_to_all x2, waiting for transfers between devices, gather_rows(): lax.all_to_all(copies, axis, 0, 0, tiled=False).reshape((-1,) + x.shape[1:])  16.1 us
    all_to_all x1, blocking collectives, gather_rows(): lax.all_to_all(copies, axis, 0, 0, tiled=False).reshape((-1,) + x.shape[1:])  13.1 us
    all_to_all x2, starting transfers between devices, gather_rows(): lax.all_to_all(copies, axis, 0, 0, tiled=False).reshape((-1,) + x.shape[1:])  10.9 us
    dot_general x2, matrix products, contract_rows(): lax.dot_general(left, right, (((0,), (0,)), ((), ())), precision=lax.Prec...  7.03 us
    ppermute x3, starting transfers between devices, butterfly_sum(): x = x + lax.ppermute(x, axis, [(i, i ^ step) for i in range(n)])  5.87 us
    ppermute x3, waiting for transfers between devices, butterfly_sum(): x = x + lax.ppermute(x, axis, [(i, i ^ step) for i in range(n)])  5.09 us
  transfers between devices with their start and end apart: 5, of which 4 were waited for; matrix products, arithmetic and copies ran while one was open for 29% of the time, Pallas kernels for 0%

profile of v4, /device:TPU:0, one launch (start us, length us, event | category | flops | bytes accessed | tf_op | source)
XLA Modules:
  0.0 114.1 jit_solution(6549787338879516623)
XLA Ops:
  0.0 0.0 copy-start
  0.0 0.0 copy-start.4
  0.0 2.0 %broadcast_in_dim.6 = bf16[16,64,512]{2,1,0:T(8,128)(2,1)} broadcast(bf16[64,512]{1,0:T(8,128)(2,1)} %param.8), dimensions={1,2} | broadcast | bytes 1114112 | tf_op jit(solution)/shard_map/broadcast_in_dim | solution.py:63
  2.0 7.1 %all-to-all-start = ((bf16[16,64,512]{2,1,0:T(8,128)(2,1)}), bf16[16,64,512]{2,1,0:T(8,128)(2,1)S(1)}, u32[]{:S(2)}, u32[]{:S(2)}) async-start(bf16[16,64,512]{2,1,0:T(8,128)(2,1)} %broadcast_in_dim.6), calls=%async_computation | async-start | bytes 2097152 | tf_op jit(solution)/shard_map/all_to_all | solution.py:64
  9.2 1.5 %fusion.21 = f32[1024]{0:T(1024)S(1)} fusion(bf16[16384,512]{1,0:T(8,128)(2,1)} %param.7, s32[]{:T(128)S(6)} %select_n.52), kind=kLoop, calls=%fused_computation.34 | loop fusion | flops 1571840 | bytes 1052676 | tf_op jit(solution)/shard_map/nd,nd->n/dot_general | solution.py:89
  10.7 16.1 %all-to-all-done = bf16[16,64,512]{2,1,0:T(8,128)(2,1)S(1)} async-done(((bf16[16,64,512]{2,1,0:T(8,128)(2,1)}), bf16[16,64,512]{2,1,0:T(8,128)(2,1)S(1)}, u32[]{:S(2)}, u32[]{:S(2)}) %all-to-all-start) | async-done | bytes 1048608 | tf_op jit(solution)/shard_map/all_to_all | solution.py:64
  26.8 0.0 copy-done.4
  26.8 0.0 copy-start.1
  26.8 1.6 %broadcast_in_dim.7 = f32[16,256,128]{2,1,0:T(8,128)} broadcast(f32[256,128]{1,0:T(8,128)S(1)} %copy-done.4), dimensions={1,2} | broadcast | bytes 2228224 | tf_op jit(solution)/shard_map/broadcast_in_dim | solution.py:63
  28.5 0.0 copy-done.1
  28.5 3.7 %all-to-all-start.1 = ((f32[16,256,128]{2,1,0:T(8,128)}), f32[16,256,128]{2,1,0:T(8,128)S(1)}, u32[]{:S(2)}, u32[]{:S(2)}) async-start(f32[16,256,128]{2,1,0:T(8,128)} %broadcast_in_dim.7), calls=%async_computation.1 | async-start | bytes 4194304 | tf_op jit(solution)/shard_map/all_to_all | solution.py:64
  32.2 1.5 %fusion.22 = f32[1024]{0:T(1024)S(1)} fusion(bf16[16,64,512]{2,1,0:T(8,128)(2,1)} %copy-done.1), kind=kLoop, calls=%fused_computation.36 | loop fusion | flops 1571840 | bytes 1052672 | tf_op jit(solution)/shard_map/pd,pd->p/dot_general | solution.py:34
  33.7 0.0 copy-start.3
  33.8 0.0 copy-start.5
  33.8 30.3 %fusion.15 = f32[1024,1024]{0,1:T(8,128)} fusion(bf16[1024,512]{1,0:T(8,128)(2,1)} %bitcast.29, f32[1024]{0:T(1024)S(1)} %get-tuple-element.21, f32[1024]{0:T(1024)S(1)} %get-tuple-element.13, f32[1024]{0:T(1024)S(1)} %get-tuple-element.20, f32[1024]{0:T(1024)S(1)} %get-tuple-element.12, f32[1024]{0:T(1024)S(1)} %get-tuple-element.19, ...), kind=kOutput, calls=%fused_computation.19 | convolution fusion | flops 1218445312 | bytes 6356996 | tf_op jit(solution)/shard_map/dot_general | solution.py:33
  64.1 0.0 all-to-all-done.1
  64.1 0.0 copy-done
  64.1 1.5 %convolution_bitcast_fusion.1 = f32[64,128]{1,0:T(8,128)S(1)} fusion(f32[4096,128]{1,0:T(8,128)S(1)} %bitcast.28, f32[64,4096]{1,0:T(8,128)S(1)} %copy-done), kind=kOutput, calls=%fused_computation.39 | convolution fusion | flops 402653184 | bytes 3178496 | tf_op jit(solution)/shard_map/dot_general | solution.py:95
  65.5 0.0 copy-start.2
  65.6 0.1 collective-permute-start
  65.7 1.2 %collective-permute-done = f32[64,128]{1,0:T(8,128)S(1)} collective-permute-done((f32[64,128]{1,0:T(8,128)S(1)}, f32[64,128]{1,0:T(8,128)S(1)}, u32[]{:S(2)}, u32[]{:S(2)}) %collective-permute-start) | collective-permute-done | bytes 32800 | tf_op jit(solution)/shard_map/ppermute | solution.py:75
  66.9 1.9 %collective-permute-start.1 = (f32[64,128]{1,0:T(8,128)S(1)}, f32[64,128]{1,0:T(8,128)S(1)}, u32[]{:S(2)}, u32[]{:S(2)}) collective-permute-start(f32[64,128]{1,0:T(8,128)S(1)} %add.193), channel_id=1, source_target_pairs={{0,32},{16,48},{32,0},{48,16},{64,96},{80,112},{96,64},{112,80},{1... | collective-permute-start | bytes 98312 | tf_op jit(solution)/shard_map/ppermute | solution.py:75
  68.8 2.0 %collective-permute-done.1 = f32[64,128]{1,0:T(8,128)S(1)} collective-permute-done((f32[64,128]{1,0:T(8,128)S(1)}, f32[64,128]{1,0:T(8,128)S(1)}, u32[]{:S(2)}, u32[]{:S(2)}) %collective-permute-start.1) | collective-permute-done | bytes 32800 | tf_op jit(solution)/shard_map/ppermute | solution.py:75
  70.8 3.9 %collective-permute-start.2 = (f32[64,128]{1,0:T(8,128)S(1)}, f32[64,128]{1,0:T(8,128)S(1)}, u32[]{:S(2)}, u32[]{:S(2)}) collective-permute-start(f32[64,128]{1,0:T(8,128)S(1)} %add.194), channel_id=1, source_target_pairs={{0,64},{16,80},{32,96},{48,112},{64,0},{80,16},{96,32},{112,48},{1... | collective-permute-start | bytes 98312 | tf_op jit(solution)/shard_map/ppermute | solution.py:75
  74.6 1.9 %collective-permute-done.2 = f32[64,128]{1,0:T(8,128)S(1)} collective-permute-done((f32[64,128]{1,0:T(8,128)S(1)}, f32[64,128]{1,0:T(8,128)S(1)}, u32[]{:S(2)}, u32[]{:S(2)}) %collective-permute-start.2) | collective-permute-done | bytes 32800 | tf_op jit(solution)/shard_map/ppermute | solution.py:75
  76.5 0.0 copy-done.3
  76.5 0.0 copy-done.5
  76.5 0.6 convolution_bitcast_fusion
  77.2 0.2 copy.10
  77.4 17.1 %all_to_all.20 = f32[16,64,128]{2,1,0:T(8,128)S(1)} all-to-all(f32[16,64,128]{2,1,0:T(8,128)S(1)} %bitcast.30), channel_id=1, replica_groups=mesh['pr'=8,'pc'=16] {'pc'}, dimensions={0} | all-to-all | bytes 1048576 | tf_op jit(solution)/shard_map/all_to_all | solution.py:68
  94.5 13.1 %all_to_all.21 = f32[16,64,128]{2,1,0:T(8,128)S(1)} all-to-all(f32[16,64,128]{2,1,0:T(8,128)S(1)} %broadcast_in_dim.8), channel_id=1, replica_groups=mesh['pr'=8,'pc'=16] {'pc'}, dimensions={0} | all-to-all | bytes 1048576 | tf_op jit(solution)/shard_map/all_to_all | solution.py:64
  107.7 0.0 copy-done.2
  107.7 6.4 %convolution_add_fusion = f32[1024,128]{1,0:T(8,128)} fusion(f32[1024,128]{1,0:T(8,128)S(1)} %copy-done.2, f32[1024,1024]{0,1:T(8,128)} %fusion.15, f32[1024,128]{1,0:T(8,128)S(1)} %bitcast.31), kind=kOutput, calls=%fused_computation.37 | convolution fusion | flops 1610743808 | bytes 5767168 | tf_op jit(solution)/shard_map/dot_general | solution.py:53
  (6 shorter events, 0.1 us)
Async XLA Ops:
  0.0 64.1 %copy-start = (f32[64,4096]{1,0:T(8,128)S(1)}, f32[64,4096]{1,0:T(8,128)}, u32[]{:S(2)}) copy-start(f32[64,4096]{1,0:T(8,128)} %param.9) | copy-start | bytes 3145732
  0.0 26.8 %copy-start.4 = (f32[256,128]{1,0:T(8,128)S(1)}, f32[256,128]{1,0:T(8,128)}, u32[]{:S(2)}) copy-start(f32[256,128]{1,0:T(8,128)} %param.10) | copy-start | bytes 393220
  2.0 24.8 %all-to-all-start = ((bf16[16,64,512]{2,1,0:T(8,128)(2,1)}), bf16[16,64,512]{2,1,0:T(8,128)(2,1)S(1)}, u32[]{:S(2)}, u32[]{:S(2)}) async-start(bf16[16,64,512]{2,1,0:T(8,128)(2,1)} %broadcast_in_dim.6), calls=%async_computation | async-start | bytes 2097152 | tf_op jit(solution)/shard_map/all_to_all | solution.py:64
  26.8 1.6 %copy-start.1 = (bf16[16,64,512]{2,1,0:T(8,128)(2,1)}, bf16[16,64,512]{2,1,0:T(8,128)(2,1)S(1)}, u32[]{:S(2)}) copy-start(bf16[16,64,512]{2,1,0:T(8,128)(2,1)S(1)} %all-to-all-done) | copy-start | bytes 3145732
  28.5 35.6 %all-to-all-start.1 = ((f32[16,256,128]{2,1,0:T(8,128)}), f32[16,256,128]{2,1,0:T(8,128)S(1)}, u32[]{:S(2)}, u32[]{:S(2)}) async-start(f32[16,256,128]{2,1,0:T(8,128)} %broadcast_in_dim.7), calls=%async_computation.1 | async-start | bytes 4194304 | tf_op jit(solution)/shard_map/all_to_all | solution.py:64
  33.7 42.8 %copy-start.3 = (f32[64,1024]{1,0:T(8,128)S(1)}, f32[64,1024]{1,0:T(8,128)}, u32[]{:S(2)}) copy-start(f32[64,1024]{1,0:T(8,128)} %param.12) | copy-start | bytes 786436
  33.8 42.8 %copy-start.5 = (f32[64,128]{1,0:T(8,128)S(1)}, f32[64,128]{1,0:T(8,128)}, u32[]{:S(2)}) copy-start(f32[64,128]{1,0:T(8,128)} %param.11) | copy-start | bytes 98308
  65.5 42.1 %copy-start.2 = (f32[1024,128]{1,0:T(8,128)S(1)}, f32[1024,128]{1,0:T(8,128)}, u32[]{:S(2)}) copy-start(f32[1024,128]{1,0:T(8,128)} %param.13) | copy-start | bytes 1572868
  65.6 1.3 %collective-permute-start = (f32[64,128]{1,0:T(8,128)S(1)}, f32[64,128]{1,0:T(8,128)S(1)}, u32[]{:S(2)}, u32[]{:S(2)}) collective-permute-start(f32[64,128]{1,0:T(8,128)S(1)} %convolution_bitcast_fusion.1), channel_id=1, source_target_pairs={{0,16},{16,0},{32,48},{48,32},{64,80},{80,64},{96,112},{112,96},{1... | collective-permute-start | bytes 98312 | tf_op jit(solution)/shard_map/ppermute | solution.py:75
  66.9 3.9 %collective-permute-start.1 = (f32[64,128]{1,0:T(8,128)S(1)}, f32[64,128]{1,0:T(8,128)S(1)}, u32[]{:S(2)}, u32[]{:S(2)}) collective-permute-start(f32[64,128]{1,0:T(8,128)S(1)} %add.193), channel_id=1, source_target_pairs={{0,32},{16,48},{32,0},{48,16},{64,96},{80,112},{96,64},{112,80},{1... | collective-permute-start | bytes 98312 | tf_op jit(solution)/shard_map/ppermute | solution.py:75
  70.8 5.8 %collective-permute-start.2 = (f32[64,128]{1,0:T(8,128)S(1)}, f32[64,128]{1,0:T(8,128)S(1)}, u32[]{:S(2)}, u32[]{:S(2)}) collective-permute-start(f32[64,128]{1,0:T(8,128)S(1)} %add.194), channel_id=1, source_target_pairs={{0,64},{16,80},{32,96},{48,112},{64,0},{80,16},{96,32},{112,48},{1... | collective-permute-start | bytes 98312 | tf_op jit(solution)/shard_map/ppermute | solution.py:75

commit v5 on v4

--- a/solution.py
+++ b/solution.py
@@ -84,14 +84,12 @@
     n_pc = lax.axis_size("pc")
     rows = predictions_in.shape[0]
     own = lax.axis_index("pc")
-    panel_all = gather_rows(panel_points, "pc", n_pc)
+    gathered = gather_rows(alpha_below, "pc", n_pc)
+    panel_all = lax.all_gather(panel_points, "pc", axis=0, tiled=True)
     test_own = lax.dynamic_slice_in_dim(test_points, own * rows, rows, 0)
     test_norms = jnp.einsum(
         "nd,nd->n", test_own, test_own, preferred_element_type=jnp.float32
     )
-    kern = arc_kernel(panel_all, test_own, test_norms)
-    gathered = gather_rows(alpha_below, "pc", n_pc)
-    kern, gathered = lax.optimization_barrier((kern, gathered))
     partial_sum = jnp.dot(
         factor_rows,
         gathered,
@@ -100,8 +98,22 @@
     )
     carried = butterfly_sum(partial_sum, "pr", n_pr)
     residual = targets - carried
-    alpha_panel = sum_rows(contract_rows(inverse_block, residual), "pc", n_pc)
-    update = contract_rows(kern, alpha_panel)
+    spread_alpha = contract_rows(inverse_block, residual)
+    spread_alpha, panel_all = lax.optimization_barrier((spread_alpha, panel_all))
+    half = rows // 2
+    blocks = lax.all_to_all(
+        spread_alpha.reshape((n_pc, -1) + spread_alpha.shape[1:]), "pc", 0, 0, tiled=False
+    )
+    kern_a = arc_kernel(panel_all, test_own[:half], test_norms[:half])
+    kern_a, blocks = lax.optimization_barrier((kern_a, blocks))
+    own_block = blocks.sum(0)
+    own_block, panel_all = lax.optimization_barrier((own_block, panel_all))
+    alpha_panel = gather_rows(own_block, "pc", n_pc)
+    kern_b = arc_kernel(panel_all, test_own[half:], test_norms[half:])
+    kern_b, alpha_panel = lax.optimization_barrier((kern_b, alpha_panel))
+    update = jnp.concatenate(
+        [contract_rows(kern_a, alpha_panel), contract_rows(kern_b, alpha_panel)]
+    )
     return predictions_in + update
 
 

time: 115 us -> 138 us (1.20)
  blocking collectives: 30.2 us -> 0 us
  waiting for transfers between devices: 21.2 us -> 46.9 us
  between operations: 0.12 us -> 13.5 us
  starting transfers between devices: 16.7 us -> 25.3 us
  matrix products: 38.8 us -> 43.1 us
    all_to_all x2 -> x0, blocking collectives: 30.2 us -> none  [the longest x1 17.1 us: sum_rows(): lax.all_to_all(x.reshape((n, -1) + x.shape[1:]), axis, 0, 0, tiled=False)]
    all_to_all x2, waiting for transfers between devices: 16.1 us -> 31.3 us  [gather_rows(): lax.all_to_all(copies, axis, 0, 0, tiled=False).reshape((-1,) + x.shape[1:])]
    all_gather x0 -> x1, waiting for transfers between devices: none -> 11.4 us  [body(): panel_all = lax.all_gather(panel_points, 'pc', axis=0, tiled=True)]
    all_to_all x0 -> x1, starting transfers between devices: none -> 4.94 us  [body(): lax.all_to_all(spread_alpha.reshape((n_pc, -1) + spread_alpha.shape[1:]),...]
    all_to_all x2, starting transfers between devices: 10.9 us -> 14.4 us  [gather_rows(): lax.all_to_all(copies, axis, 0, 0, tiled=False).reshape((-1,) + x.shape[1:])]
    dot_general x1 -> x2, matrix products: 30.3 us -> 32.5 us  [arc_kernel(): cross = jnp.dot(panel, test.T, preferred_element_type=jnp.float32) / width]
    dot_general x2 -> x3, matrix products: 7.03 us -> 9.2 us  [contract_rows(): lax.dot_general(left, right, (((0,), (0,)), ((), ())), precision=lax.Prec...]
    ppermute x3, waiting for transfers between devices: 5.09 us -> 3.55 us  [butterfly_sum(): x = x + lax.ppermute(x, axis, [(i, i ^ step) for i in range(n)])]
  transfers between devices with their start and end apart: 5 -> 7, of which waited for: 4 -> 5; matrix products, arithmetic and copies ran while one was open for 29% -> 26% of each run, Pallas kernels for 0% -> 0%
where the time goes in v5:
time: 138 us
  waiting for transfers between devices  46.9 us (34%)
  matrix products  43.1 us (31%)
  starting transfers between devices  25.3 us (18%)
  between operations  13.5 us (10%)
  local copies, waits for them, and re-layouts  4.4 us (3%)
  other arithmetic  4.3 us (3%)
    dot_general x2, matrix products, arc_kernel(): cross = jnp.dot(panel, test.T, preferred_element_type=jnp.float32) / width  32.5 us
    all_to_all x2, waiting for transfers between devices, gather_rows(): lax.all_to_all(copies, axis, 0, 0, tiled=False).reshape((-1,) + x.shape[1:])  31.3 us
    all_to_all x2, starting transfers between devices, gather_rows(): lax.all_to_all(copies, axis, 0, 0, tiled=False).reshape((-1,) + x.shape[1:])  14.4 us
    all_gather x1, waiting for transfers between devices, body(): panel_all = lax.all_gather(panel_points, 'pc', axis=0, tiled=True)  11.4 us
    dot_general x3, matrix products, contract_rows(): lax.dot_general(left, right, (((0,), (0,)), ((), ())), precision=lax.Prec...  9.2 us
    ppermute x3, starting transfers between devices, butterfly_sum(): x = x + lax.ppermute(x, axis, [(i, i ^ step) for i in range(n)])  5.97 us
    all_to_all x1, starting transfers between devices, body(): lax.all_to_all(spread_alpha.reshape((n_pc, -1) + spread_alpha.shape[1:]),...  4.94 us
    ppermute x3, waiting for transfers between devices, butterfly_sum(): x = x + lax.ppermute(x, axis, [(i, i ^ step) for i in range(n)])  3.55 us
  transfers between devices with their start and end apart: 7, of which 5 were waited for; matrix products, arithmetic and copies ran while one was open for 26% of the time, Pallas kernels for 0%

profile of v5, /device:TPU:0, one launch (start us, length us, event | category | flops | bytes accessed | tf_op | source)
XLA Modules:
  0.0 137.6 jit_solution(13756742414199496830)
XLA Ops:
  6.5 0.0 copy-start
  6.5 2.5 %broadcast_in_dim.4 = f32[16,256,128]{2,1,0:T(8,128)} broadcast(f32[256,128]{1,0:T(8,128)} %param.10), dimensions={1,2} | broadcast | bytes 2228224 | tf_op jit(solution)/shard_map/broadcast_in_dim | solution.py:63
  9.1 7.1 %all-to-all-start = ((f32[16,256,128]{2,1,0:T(8,128)}), f32[16,256,128]{2,1,0:T(8,128)S(1)}, u32[]{:S(2)}, u32[]{:S(2)}) async-start(f32[16,256,128]{2,1,0:T(8,128)} %broadcast_in_dim.4), calls=%async_computation | async-start | bytes 4194304 | tf_op jit(solution)/shard_map/all_to_all | solution.py:64
  16.2 0.0 all-gather.2.cloned.1.call-start
  16.3 0.7 all-gather.2.cloned.1.call-update
  17.0 31.3 %all-to-all-done = f32[16,256,128]{2,1,0:T(8,128)S(1)} async-done(((f32[16,256,128]{2,1,0:T(8,128)}), f32[16,256,128]{2,1,0:T(8,128)S(1)}, u32[]{:S(2)}, u32[]{:S(2)}) %all-to-all-start) | async-done | bytes 2097184 | tf_op jit(solution)/shard_map/all_to_all | solution.py:64
  48.3 0.0 copy-done
  48.3 0.0 copy-start.4
  48.3 0.0 copy-start.5
  48.3 1.4 %fusion.49 = f32[64,128]{1,0:T(8,128)S(1)} fusion(f32[64,4096]{1,0:T(8,128)S(1)} %copy-done, f32[4096,128]{1,0:T(8,128)S(1)} %bitcast.14), kind=kOutput, calls=%fused_computation.112 | convolution fusion | flops 402653184 | bytes 3178496 | tf_op jit(solution)/shard_map/dot_general | solution.py:93
  49.7 0.1 collective-permute-start
  49.8 1.2 collective-permute-done
  51.0 1.9 %collective-permute-start.1 = (f32[64,128]{1,0:T(8,128)S(1)}, f32[64,128]{1,0:T(8,128)S(1)}, u32[]{:S(2)}, u32[]{:S(2)}) collective-permute-start(f32[64,128]{1,0:T(8,128)S(1)} %add.281), channel_id=1, source_target_pairs={{0,32},{16,48},{32,0},{48,16},{64,96},{80,112},{96,64},{112,80},{1... | collective-permute-start | bytes 98312 | tf_op jit(solution)/shard_map/ppermute | solution.py:75
  52.9 1.5 %fusion.33 = f32[1024]{0:T(1024)S(1)} fusion(bf16[16384,512]{1,0:T(8,128)(2,1)} %param.7, s32[]{:T(128)S(6)} %select_n.100), kind=kLoop, calls=%fused_computation.43 | loop fusion | flops 1571840 | bytes 1052676 | tf_op jit(solution)/shard_map/nd,nd->n/dot_general | solution.py:90
  54.4 0.5 collective-permute-done.1
  54.9 4.0 %collective-permute-start.2 = (f32[64,128]{1,0:T(8,128)S(1)}, f32[64,128]{1,0:T(8,128)S(1)}, u32[]{:S(2)}, u32[]{:S(2)}) collective-permute-start(f32[64,128]{1,0:T(8,128)S(1)} %add.282), channel_id=1, source_target_pairs={{0,64},{16,80},{32,96},{48,112},{64,0},{80,16},{96,32},{112,48},{1... | collective-permute-start | bytes 98312 | tf_op jit(solution)/shard_map/ppermute | solution.py:75
  58.9 1.9 %collective-permute-done.2 = f32[64,128]{1,0:T(8,128)S(1)} collective-permute-done((f32[64,128]{1,0:T(8,128)S(1)}, f32[64,128]{1,0:T(8,128)S(1)}, u32[]{:S(2)}, u32[]{:S(2)}) %collective-permute-start.2) | collective-permute-done | bytes 32800 | tf_op jit(solution)/shard_map/ppermute | solution.py:75
  60.8 0.0 copy-done.4
  60.8 0.0 copy-done.5
  60.8 0.6 convolution_bitcast_fusion
  61.4 11.4 %all-gather.2.cloned.1.call-done = bf16[1024,512]{1,0:T(8,128)(2,1)} async-done(((bf16[64,512]{1,0:T(8,128)(2,1)}), bf16[1024,512]{1,0:T(8,128)(2,1)}) %all-gather.2.cloned.1.call-update) | async-done | bytes 1048592 | tf_op jit(solution)/shard_map/all_gather | solution.py:88
  72.8 0.0 copy-start.1
  72.8 1.6 %fusion.34 = f32[1024]{0:T(1024)S(1)} fusion(bf16[1024,512]{1,0:T(8,128)(2,1)} %all-gather.2.cloned.1.call-done), kind=kLoop, calls=%fused_computation.45 | loop fusion | flops 1571840 | bytes 1052672 | tf_op jit(solution)/shard_map/pd,pd->p/dot_general | solution.py:34
  74.4 1.0 copy.8
  75.4 4.9 %all-to-all-start.1 = ((f32[16,64,128]{2,1,0:T(8,128)}), f32[16,64,128]{2,1,0:T(8,128)S(1)}, u32[]{:S(2)}, u32[]{:S(2)}) async-start(f32[16,64,128]{2,1,0:T(8,128)} %bitcast.2), calls=%async_computation.1 | async-start | bytes 1048576 | tf_op jit(solution)/shard_map/all_to_all | solution.py:104
  80.3 0.0 copy-done.1
  80.3 16.2 %fusion.15 = f32[1024,512]{1,0:T(8,128)} fusion(bf16[1024,512]{1,0:T(8,128)(2,1)S(1)} %copy-done.1, f32[512]{0:T(512)S(1)} %get-tuple-element.37, f32[1024]{0:T(1024)S(1)} %get-tuple-element.49, f32[512]{0:T(512)S(1)} %get-tuple-element.36, f32[1024]{0:T(1024)S(1)} %get-tuple-element.48, f32[512]{0:T(512)S(1)} %get-tuple-element.35, ...), kind=kOutput, calls=%fused_computation.23 | convolution fusion | flops 609222656 | bytes 3719172 | tf_op jit(solution)/shard_map/dot_general | solution.py:33
  96.6 0.0 all-to-all-done.1
  96.6 0.3 fusion.32
  96.9 0.8 broadcast_in_dim.5
  97.8 7.2 %all-to-all-start.2 = ((f32[16,64,128]{2,1,0:T(8,128)}), f32[16,64,128]{2,1,0:T(8,128)S(1)}, u32[]{:S(2)}, u32[]{:S(2)}) async-start(f32[16,64,128]{2,1,0:T(8,128)} %broadcast_in_dim.5), calls=%async_computation.2 | async-start | bytes 1048576 | tf_op jit(solution)/shard_map/all_to_all | solution.py:64
  105.0 16.3 %fusion.31 = f32[1024,512]{1,0:T(8,128)} fusion(bf16[1024,512]{1,0:T(8,128)(2,1)S(1)} %copy-done.1, f32[512]{0:T(512)S(1)} %get-tuple-element.33, f32[1024]{0:T(1024)S(1)} %get-tuple-element.25, f32[512]{0:T(512)S(1)} %get-tuple-element.32, f32[1024]{0:T(1024)S(1)} %get-tuple-element.24, f32[512]{0:T(512)S(1)} %get-tuple-element.31, ...), kind=kOutput, calls=%fused_computation.39 | convolution fusion | flops 609222656 | bytes 3719172 | tf_op jit(solution)/shard_map/dot_general | solution.py:33
  121.2 0.0 all-to-all-done.2
  121.2 0.0 copy-start.2
  121.2 5.2 %fusion.50 = f32[512,128]{1,0:T(8,128)S(1)} fusion(f32[1024,512]{1,0:T(8,128)} %fusion.15, f32[1024,128]{1,0:T(8,128)S(1)} %bitcast.15), kind=kOutput, calls=%fused_computation.113 | convolution fusion | flops 805306368 | bytes 2883584 | tf_op jit(solution)/shard_map/dot_general | solution.py:53
  126.4 0.0 copy-done.2
  126.4 0.0 copy-start.3
  126.4 3.4 %fusion.51 = f32[512,128]{1,0:T(8,128)S(1)} fusion(f32[1024,512]{1,0:T(8,128)S(1)} %copy-done.2, f32[1024,128]{1,0:T(8,128)S(1)} %bitcast.16), kind=kOutput, calls=%fused_computation.114 | convolution fusion | flops 805306368 | bytes 2883584 | tf_op jit(solution)/shard_map/dot_general | solution.py:53
  129.9 0.0 copy-done.3
  129.9 0.8 maximum_add_fusion
  (6 shorter events, 0.1 us)
Async XLA Ops:
  6.5 41.7 %copy-start = (f32[64,4096]{1,0:T(8,128)S(1)}, f32[64,4096]{1,0:T(8,128)}, u32[]{:S(2)}) copy-start(f32[64,4096]{1,0:T(8,128)} %param.9) | copy-start | bytes 3145732
  9.1 39.2 %all-to-all-start = ((f32[16,256,128]{2,1,0:T(8,128)}), f32[16,256,128]{2,1,0:T(8,128)S(1)}, u32[]{:S(2)}, u32[]{:S(2)}) async-start(f32[16,256,128]{2,1,0:T(8,128)} %broadcast_in_dim.4), calls=%async_computation | async-start | bytes 4194304 | tf_op jit(solution)/shard_map/all_to_all | solution.py:64
  16.2 56.5 %all-gather.2.cloned.1.call-start = ((), (), s32[]{:S(2)}) async-start(), calls=%async_computation.3 | async-start | bytes 1114112 | tf_op jit(solution)/shard_map/all_gather | solution.py:88
  48.3 12.5 %copy-start.4 = (f32[64,1024]{1,0:T(8,128)S(1)}, f32[64,1024]{1,0:T(8,128)}, u32[]{:S(2)}) copy-start(f32[64,1024]{1,0:T(8,128)} %param.12) | copy-start | bytes 786436
  48.3 12.5 %copy-start.5 = (f32[64,128]{1,0:T(8,128)S(1)}, f32[64,128]{1,0:T(8,128)}, u32[]{:S(2)}) copy-start(f32[64,128]{1,0:T(8,128)} %param.11) | copy-start | bytes 98308
  49.7 1.3 collective-permute-start
  51.0 3.9 %collective-permute-start.1 = (f32[64,128]{1,0:T(8,128)S(1)}, f32[64,128]{1,0:T(8,128)S(1)}, u32[]{:S(2)}, u32[]{:S(2)}) collective-permute-start(f32[64,128]{1,0:T(8,128)S(1)} %add.281), channel_id=1, source_target_pairs={{0,32},{16,48},{32,0},{48,16},{64,96},{80,112},{96,64},{112,80},{1... | collective-permute-start | bytes 98312 | tf_op jit(solution)/shard_map/ppermute | solution.py:75
  54.9 5.9 %collective-permute-start.2 = (f32[64,128]{1,0:T(8,128)S(1)}, f32[64,128]{1,0:T(8,128)S(1)}, u32[]{:S(2)}, u32[]{:S(2)}) collective-permute-start(f32[64,128]{1,0:T(8,128)S(1)} %add.282), channel_id=1, source_target_pairs={{0,64},{16,80},{32,96},{48,112},{64,0},{80,16},{96,32},{112,48},{1... | collective-permute-start | bytes 98312 | tf_op jit(solution)/shard_map/ppermute | solution.py:75
  72.8 7.6 %copy-start.1 = (bf16[1024,512]{1,0:T(8,128)(2,1)S(1)}, bf16[1024,512]{1,0:T(8,128)(2,1)}, u32[]{:S(2)}) copy-start(bf16[1024,512]{1,0:T(8,128)(2,1)} %all-gather.2.cloned.1.call-done) | copy-start | bytes 3145732
  75.4 21.2 %all-to-all-start.1 = ((f32[16,64,128]{2,1,0:T(8,128)}), f32[16,64,128]{2,1,0:T(8,128)S(1)}, u32[]{:S(2)}, u32[]{:S(2)}) async-start(f32[16,64,128]{2,1,0:T(8,128)} %bitcast.2), calls=%async_computation.1 | async-start | bytes 1048576 | tf_op jit(solution)/shard_map/all_to_all | solution.py:104
  97.8 23.5 %all-to-all-start.2 = ((f32[16,64,128]{2,1,0:T(8,128)}), f32[16,64,128]{2,1,0:T(8,128)S(1)}, u32[]{:S(2)}, u32[]{:S(2)}) async-start(f32[16,64,128]{2,1,0:T(8,128)} %broadcast_in_dim.5), calls=%async_computation.2 | async-start | bytes 1048576 | tf_op jit(solution)/shard_map/all_to_all | solution.py:64
  121.2 5.2 %copy-start.2 = (f32[1024,512]{1,0:T(8,128)S(1)}, f32[1024,512]{1,0:T(8,128)}, u32[]{:S(2)}) copy-start(f32[1024,512]{1,0:T(8,128)} %fusion.31) | copy-start | bytes 6291460
  126.4 3.4 %copy-start.3 = (f32[1024,128]{1,0:T(8,128)S(1)}, f32[1024,128]{1,0:T(8,128)}, u32[]{:S(2)}) copy-start(f32[1024,128]{1,0:T(8,128)} %param.13) | copy-start | bytes 1572868
Sparse Core Ops, SparseCore 0:
  19.2 53.5 all-gather.1

commit v6 on v4

--- a/solution.py
+++ b/solution.py
@@ -90,7 +90,7 @@
         "nd,nd->n", test_own, test_own, preferred_element_type=jnp.float32
     )
     kern = arc_kernel(panel_all, test_own, test_norms)
-    gathered = gather_rows(alpha_below, "pc", n_pc)
+    gathered = lax.all_gather(alpha_below, "pc", axis=0, tiled=True)
     kern, gathered = lax.optimization_barrier((kern, gathered))
     partial_sum = jnp.dot(
         factor_rows,

time: 115 us -> 122 us (1.061)
  between operations: 0.12 us -> 13.5 us
  starting transfers between devices: 16.7 us -> 11.9 us
  waiting for transfers between devices: 21.2 us -> 24.4 us
  blocking collectives: 30.2 us -> 28 us
  local copies, waits for them, and re-layouts: 3.91 us -> 2.26 us
  other arithmetic: 3.08 us -> 1.86 us
    all_to_all x2 -> x1, starting transfers between devices: 10.9 us -> 7.15 us  [gather_rows(): lax.all_to_all(copies, axis, 0, 0, tiled=False).reshape((-1,) + x.shape[1:])]
    all_gather x0 -> x1, waiting for transfers between devices: none -> 2.44 us  [body(): gathered = lax.all_gather(alpha_below, 'pc', axis=0, tiled=True)]
    all_to_all x1, blocking collectives: 17.1 us -> 14.8 us  [sum_rows(): lax.all_to_all(x.reshape((n, -1) + x.shape[1:]), axis, 0, 0, tiled=False)]
    broadcast_in_dim x3 -> x2, local copies, waits for them, and re-layouts: 3.69 us -> 2.05 us  [gather_rows(): copies = jnp.broadcast_to(x[None], (n,) + x.shape)]
    dot_general x1, matrix products: 1.47 us -> 3.05 us  [body(): jnp.dot(factor_rows, gathered, precision=lax.Precision.HIGHEST, preferred...]
    all_to_all x2 -> x1, waiting for transfers between devices: 16.1 us -> 15.4 us  [gather_rows(): lax.all_to_all(copies, axis, 0, 0, tiled=False).reshape((-1,) + x.shape[1:])]
  transfers between devices with their start and end apart: 5 -> 5, of which waited for: 4 -> 5; matrix products, arithmetic and copies ran while one was open for 29% -> 26% of each run, Pallas kernels for 0% -> 0%
where the time goes in v6:
time: 122 us
  matrix products  40 us (33%)
  blocking collectives  28 us (23%)
  waiting for transfers between devices  24.4 us (20%)
  between operations  13.5 us (11%)
  starting transfers between devices  11.9 us (10%)
  local copies, waits for them, and re-layouts  2.26 us (2%)
  other arithmetic  1.86 us (2%)
    dot_general x1, matrix products, arc_kernel(): cross = jnp.dot(panel, test.T, preferred_element_type=jnp.float32) / width  29.9 us
    all_to_all x1, waiting for transfers between devices, gather_rows(): lax.all_to_all(copies, axis, 0, 0, tiled=False).reshape((-1,) + x.shape[1:])  15.4 us
    all_to_all x1, blocking collectives, sum_rows(): lax.all_to_all(x.reshape((n, -1) + x.shape[1:]), axis, 0, 0, tiled=False)  14.8 us
    all_to_all x1, blocking collectives, gather_rows(): lax.all_to_all(copies, axis, 0, 0, tiled=False).reshape((-1,) + x.shape[1:])  13.1 us
    all_to_all x1, starting transfers between devices, gather_rows(): lax.all_to_all(copies, axis, 0, 0, tiled=False).reshape((-1,) + x.shape[1:])  7.15 us
    dot_general x2, matrix products, contract_rows(): lax.dot_general(left, right, (((0,), (0,)), ((), ())), precision=lax.Prec...  7.03 us
    ppermute x3, waiting for transfers between devices, butterfly_sum(): x = x + lax.ppermute(x, axis, [(i, i ^ step) for i in range(n)])  5.89 us
    ppermute x3, starting transfers between devices, butterfly_sum(): x = x + lax.ppermute(x, axis, [(i, i ^ step) for i in range(n)])  4.72 us
  transfers between devices with their start and end apart: 5, of which 5 were waited for; matrix products, arithmetic and copies ran while one was open for 26% of the time, Pallas kernels for 0%

profile of v6, /device:TPU:0, one launch (start us, length us, event | category | flops | bytes accessed | tf_op | source)
XLA Modules:
  0.0 121.9 jit_solution(10091205078545327270)
XLA Ops:
  6.5 0.0 copy-start
  6.5 2.0 %broadcast_in_dim.4 = bf16[16,64,512]{2,1,0:T(8,128)(2,1)} broadcast(bf16[64,512]{1,0:T(8,128)(2,1)} %param.8), dimensions={1,2} | broadcast | bytes 1114112 | tf_op jit(solution)/shard_map/broadcast_in_dim | solution.py:63
  8.5 7.1 %all-to-all-start = ((bf16[16,64,512]{2,1,0:T(8,128)(2,1)}), bf16[16,64,512]{2,1,0:T(8,128)(2,1)S(1)}, u32[]{:S(2)}, u32[]{:S(2)}) async-start(bf16[16,64,512]{2,1,0:T(8,128)(2,1)} %broadcast_in_dim.4), calls=%async_computation | async-start | bytes 2097152 | tf_op jit(solution)/shard_map/all_to_all | solution.py:64
  15.7 0.0 all-gather.2.cloned.1.call-start
  15.7 0.7 all-gather.2.cloned.1.call-update
  16.4 1.5 %fusion.21 = f32[1024]{0:T(1024)S(1)} fusion(bf16[16384,512]{1,0:T(8,128)(2,1)} %param.7, s32[]{:T(128)S(6)} %select_n.52), kind=kLoop, calls=%fused_computation.34 | loop fusion | flops 1571840 | bytes 1052676 | tf_op jit(solution)/shard_map/nd,nd->n/dot_general | solution.py:89
  18.0 15.4 %all-to-all-done = bf16[16,64,512]{2,1,0:T(8,128)(2,1)S(1)} async-done(((bf16[16,64,512]{2,1,0:T(8,128)(2,1)}), bf16[16,64,512]{2,1,0:T(8,128)(2,1)S(1)}, u32[]{:S(2)}, u32[]{:S(2)}) %all-to-all-start) | async-done | bytes 1048608 | tf_op jit(solution)/shard_map/all_to_all | solution.py:64
  33.4 0.3 fusion.22
  33.7 0.0 copy-start.2
  33.7 0.0 copy-start.3
  33.7 29.9 %fusion.15 = f32[1024,1024]{0,1:T(8,128)} fusion(bf16[1024,512]{1,0:T(8,128)(2,1)S(1)} %bitcast.27, f32[1024]{0:T(1024)S(1)} %get-tuple-element.21, f32[1024]{0:T(1024)S(1)} %get-tuple-element.13, f32[1024]{0:T(1024)S(1)} %get-tuple-element.20, f32[1024]{0:T(1024)S(1)} %get-tuple-element.12, f32[1024]{0:T(1024)S(1)} %get-tuple-element.19, ...), kind=kOutput, calls=%fused_computation.19 | convolution fusion | flops 1218445312 | bytes 6356996 | tf_op jit(solution)/shard_map/dot_general | solution.py:33
  63.6 0.0 copy-start.1
  63.6 2.4 %all-gather.2.cloned.1.call-done = f32[4096,128]{1,0:T(8,128)} async-done(((f32[256,128]{1,0:T(8,128)}), f32[4096,128]{1,0:T(8,128)}) %all-gather.2.cloned.1.call-update) | async-done | bytes 2097168 | tf_op jit(solution)/shard_map/all_gather | solution.py:93
  66.1 0.0 copy-done
  66.1 3.0 %convolution_bitcast_fusion.1 = f32[64,128]{1,0:T(8,128)S(1)} fusion(f32[4096,128]{1,0:T(8,128)} %all-gather.2.cloned.1.call-done, f32[64,4096]{1,0:T(8,128)S(1)} %copy-done), kind=kOutput, calls=%fused_computation.39 | convolution fusion | flops 402653184 | bytes 3178496 | tf_op jit(solution)/shard_map/dot_general | solution.py:95
  69.1 0.1 collective-permute-start
  69.2 1.2 collective-permute-done
  70.4 1.6 %collective-permute-start.1 = (f32[64,128]{1,0:T(8,128)S(1)}, f32[64,128]{1,0:T(8,128)S(1)}, u32[]{:S(2)}, u32[]{:S(2)}) collective-permute-start(f32[64,128]{1,0:T(8,128)S(1)} %add.193), channel_id=1, source_target_pairs={{0,32},{16,48},{32,0},{48,16},{64,96},{80,112},{96,64},{112,80},{1... | collective-permute-start | bytes 98312 | tf_op jit(solution)/shard_map/ppermute | solution.py:75
  72.0 2.4 %collective-permute-done.1 = f32[64,128]{1,0:T(8,128)S(1)} collective-permute-done((f32[64,128]{1,0:T(8,128)S(1)}, f32[64,128]{1,0:T(8,128)S(1)}, u32[]{:S(2)}, u32[]{:S(2)}) %collective-permute-start.1) | collective-permute-done | bytes 32800 | tf_op jit(solution)/shard_map/ppermute | solution.py:75
  74.3 3.1 %collective-permute-start.2 = (f32[64,128]{1,0:T(8,128)S(1)}, f32[64,128]{1,0:T(8,128)S(1)}, u32[]{:S(2)}, u32[]{:S(2)}) collective-permute-start(f32[64,128]{1,0:T(8,128)S(1)} %add.194), channel_id=1, source_target_pairs={{0,64},{16,80},{32,96},{48,112},{64,0},{80,16},{96,32},{112,48},{1... | collective-permute-start | bytes 98312 | tf_op jit(solution)/shard_map/ppermute | solution.py:75
  77.4 2.3 %collective-permute-done.2 = f32[64,128]{1,0:T(8,128)S(1)} collective-permute-done((f32[64,128]{1,0:T(8,128)S(1)}, f32[64,128]{1,0:T(8,128)S(1)}, u32[]{:S(2)}, u32[]{:S(2)}) %collective-permute-start.2) | collective-permute-done | bytes 32800 | tf_op jit(solution)/shard_map/ppermute | solution.py:75
  79.7 0.0 copy-done.2
  79.7 0.0 copy-done.3
  79.7 0.6 convolution_bitcast_fusion
  80.4 0.2 copy.10
  80.6 14.8 %all_to_all.15 = f32[16,64,128]{2,1,0:T(8,128)S(1)} all-to-all(f32[16,64,128]{2,1,0:T(8,128)S(1)} %bitcast.28), channel_id=1, replica_groups=mesh['pr'=8,'pc'=16] {'pc'}, dimensions={0} | all-to-all | bytes 1048576 | tf_op jit(solution)/shard_map/all_to_all | solution.py:68
  95.5 13.1 %all_to_all.16 = f32[16,64,128]{2,1,0:T(8,128)S(1)} all-to-all(f32[16,64,128]{2,1,0:T(8,128)S(1)} %broadcast_in_dim.5), channel_id=1, replica_groups=mesh['pr'=8,'pc'=16] {'pc'}, dimensions={0} | all-to-all | bytes 1048576 | tf_op jit(solution)/shard_map/all_to_all | solution.py:64
  108.6 0.0 copy-done.1
  108.6 6.4 %convolution_add_fusion = f32[1024,128]{1,0:T(8,128)} fusion(f32[1024,128]{1,0:T(8,128)S(1)} %copy-done.1, f32[1024,1024]{0,1:T(8,128)} %fusion.15, f32[1024,128]{1,0:T(8,128)S(1)} %bitcast.29), kind=kOutput, calls=%fused_computation.37 | convolution fusion | flops 1610743808 | bytes 5767168 | tf_op jit(solution)/shard_map/dot_general | solution.py:53
  (6 shorter events, 0.1 us)
Async XLA Ops:
  6.5 59.5 %copy-start = (f32[64,4096]{1,0:T(8,128)S(1)}, f32[64,4096]{1,0:T(8,128)}, u32[]{:S(2)}) copy-start(f32[64,4096]{1,0:T(8,128)} %param.9) | copy-start | bytes 3145732
  8.5 24.8 %all-to-all-start = ((bf16[16,64,512]{2,1,0:T(8,128)(2,1)}), bf16[16,64,512]{2,1,0:T(8,128)(2,1)S(1)}, u32[]{:S(2)}, u32[]{:S(2)}) async-start(bf16[16,64,512]{2,1,0:T(8,128)(2,1)} %broadcast_in_dim.4), calls=%async_computation | async-start | bytes 2097152 | tf_op jit(solution)/shard_map/all_to_all | solution.py:64
  15.7 50.4 %all-gather.2.cloned.1.call-start = ((), (), s32[]{:S(2)}) async-start(), calls=%async_computation.3 | async-start | bytes 2228224 | tf_op jit(solution)/shard_map/all_gather | solution.py:93
  33.7 46.1 %copy-start.2 = (f32[64,1024]{1,0:T(8,128)S(1)}, f32[64,1024]{1,0:T(8,128)}, u32[]{:S(2)}) copy-start(f32[64,1024]{1,0:T(8,128)} %param.12) | copy-start | bytes 786436
  33.7 46.1 %copy-start.3 = (f32[64,128]{1,0:T(8,128)S(1)}, f32[64,128]{1,0:T(8,128)}, u32[]{:S(2)}) copy-start(f32[64,128]{1,0:T(8,128)} %param.11) | copy-start | bytes 98308
  63.6 45.0 %copy-start.1 = (f32[1024,128]{1,0:T(8,128)S(1)}, f32[1024,128]{1,0:T(8,128)}, u32[]{:S(2)}) copy-start(f32[1024,128]{1,0:T(8,128)} %param.13) | copy-start | bytes 1572868
  69.1 1.3 %collective-permute-start = (f32[64,128]{1,0:T(8,128)S(1)}, f32[64,128]{1,0:T(8,128)S(1)}, u32[]{:S(2)}, u32[]{:S(2)}) collective-permute-start(f32[64,128]{1,0:T(8,128)S(1)} %convolution_bitcast_fusion.1), channel_id=1, source_target_pairs={{0,16},{16,0},{32,48},{48,32},{64,80},{80,64},{96,112},{112,96},{1... | collective-permute-start | bytes 98312 | tf_op jit(solution)/shard_map/ppermute | solution.py:75
  70.4 3.9 %collective-permute-start.1 = (f32[64,128]{1,0:T(8,128)S(1)}, f32[64,128]{1,0:T(8,128)S(1)}, u32[]{:S(2)}, u32[]{:S(2)}) collective-permute-start(f32[64,128]{1,0:T(8,128)S(1)} %add.193), channel_id=1, source_target_pairs={{0,32},{16,48},{32,0},{48,16},{64,96},{80,112},{96,64},{112,80},{1... | collective-permute-start | bytes 98312 | tf_op jit(solution)/shard_map/ppermute | solution.py:75
  74.3 5.4 %collective-permute-start.2 = (f32[64,128]{1,0:T(8,128)S(1)}, f32[64,128]{1,0:T(8,128)S(1)}, u32[]{:S(2)}, u32[]{:S(2)}) collective-permute-start(f32[64,128]{1,0:T(8,128)S(1)} %add.194), channel_id=1, source_target_pairs={{0,64},{16,80},{32,96},{48,112},{64,0},{80,16},{96,32},{112,48},{1... | collective-permute-start | bytes 98312 | tf_op jit(solution)/shard_map/ppermute | solution.py:75
Sparse Core Ops, SparseCore 0:
  18.6 47.3 all-gather.1

commit v7 on v4

--- a/solution.py
+++ b/solution.py
@@ -54,7 +54,7 @@
         left,
         right,
         (((0,), (0,)), ((), ())),
-        precision=lax.Precision.HIGHEST,
+        precision=lax.Precision.HIGH,
         preferred_element_type=jnp.float32,
     )
 
@@ -95,7 +95,7 @@
     partial_sum = jnp.dot(
         factor_rows,
         gathered,
-        precision=lax.Precision.HIGHEST,
+        precision=lax.Precision.HIGH,
         preferred_element_type=jnp.float32,
     )
     carried = butterfly_sum(partial_sum, "pr", n_pr)

time: 115 us -> 112 us (0.974)
  matrix products: 38.8 us -> 36.3 us
    dot_general x2, matrix products: 7.03 us -> 5.2 us  [contract_rows(): lax.dot_general(left, right, (((0,), (0,)), ((), ())), precision=lax.Prec...]
  transfers between devices with their start and end apart: 5 -> 5, of which waited for: 4 -> 4; matrix products, arithmetic and copies ran while one was open for 29% -> 30% of each run, Pallas kernels for 0% -> 0%
where the time goes in v7:
time: 112 us
  matrix products  36.3 us (32%)
  blocking collectives  30.2 us (27%)
  waiting for transfers between devices  21.2 us (19%)
  starting transfers between devices  16.8 us (15%)
  local copies, waits for them, and re-layouts  3.91 us (3%)
  other arithmetic  3.08 us (3%)
    dot_general x1, matrix products, arc_kernel(): cross = jnp.dot(panel, test.T, preferred_element_type=jnp.float32) / width  30.3 us
    all_to_all x1, blocking collectives, sum_rows(): lax.all_to_all(x.reshape((n, -1) + x.shape[1:]), axis, 0, 0, tiled=False)  17.1 us
    all_to_all x2, waiting for transfers between devices, gather_rows(): lax.all_to_all(copies, axis, 0, 0, tiled=False).reshape((-1,) + x.shape[1:])  16.1 us
    all_to_all x1, blocking collectives, gather_rows(): lax.all_to_all(copies, axis, 0, 0, tiled=False).reshape((-1,) + x.shape[1:])  13.1 us
    all_to_all x2, starting transfers between devices, gather_rows(): lax.all_to_all(copies, axis, 0, 0, tiled=False).reshape((-1,) + x.shape[1:])  10.9 us
    ppermute x3, starting transfers between devices, butterfly_sum(): x = x + lax.ppermute(x, axis, [(i, i ^ step) for i in range(n)])  5.89 us
    dot_general x2, matrix products, contract_rows(): lax.dot_general(left, right, (((0,), (0,)), ((), ())), precision=lax.Prec...  5.2 us
    ppermute x3, waiting for transfers between devices, butterfly_sum(): x = x + lax.ppermute(x, axis, [(i, i ^ step) for i in range(n)])  5.08 us
  transfers between devices with their start and end apart: 5, of which 4 were waited for; matrix products, arithmetic and copies ran while one was open for 30% of the time, Pallas kernels for 0%

profile of v7, /device:TPU:0, one launch (start us, length us, event | category | flops | bytes accessed | tf_op | source)
XLA Modules:
  0.0 111.5 jit_solution(15290844657415090948)
XLA Ops:
  0.0 0.0 copy-start
  0.0 0.0 copy-start.4
  0.0 2.0 %broadcast_in_dim.6 = bf16[16,64,512]{2,1,0:T(8,128)(2,1)} broadcast(bf16[64,512]{1,0:T(8,128)(2,1)} %param.8), dimensions={1,2} | broadcast | bytes 1114112 | tf_op jit(solution)/shard_map/broadcast_in_dim | solution.py:63
  2.0 7.1 %all-to-all-start = ((bf16[16,64,512]{2,1,0:T(8,128)(2,1)}), bf16[16,64,512]{2,1,0:T(8,128)(2,1)S(1)}, u32[]{:S(2)}, u32[]{:S(2)}) async-start(bf16[16,64,512]{2,1,0:T(8,128)(2,1)} %broadcast_in_dim.6), calls=%async_computation | async-start | bytes 2097152 | tf_op jit(solution)/shard_map/all_to_all | solution.py:64
  9.2 1.5 %fusion.21 = f32[1024]{0:T(1024)S(1)} fusion(bf16[16384,512]{1,0:T(8,128)(2,1)} %param.7, s32[]{:T(128)S(6)} %select_n.52), kind=kLoop, calls=%fused_computation.34 | loop fusion | flops 1571840 | bytes 1052676 | tf_op jit(solution)/shard_map/nd,nd->n/dot_general | solution.py:89
  10.7 16.1 %all-to-all-done = bf16[16,64,512]{2,1,0:T(8,128)(2,1)S(1)} async-done(((bf16[16,64,512]{2,1,0:T(8,128)(2,1)}), bf16[16,64,512]{2,1,0:T(8,128)(2,1)S(1)}, u32[]{:S(2)}, u32[]{:S(2)}) %all-to-all-start) | async-done | bytes 1048608 | tf_op jit(solution)/shard_map/all_to_all | solution.py:64
  26.8 0.0 copy-done.4
  26.8 0.0 copy-start.1
  26.8 1.6 %broadcast_in_dim.7 = f32[16,256,128]{2,1,0:T(8,128)} broadcast(f32[256,128]{1,0:T(8,128)S(1)} %copy-done.4), dimensions={1,2} | broadcast | bytes 2228224 | tf_op jit(solution)/shard_map/broadcast_in_dim | solution.py:63
  28.5 0.0 copy-done.1
  28.5 3.7 %all-to-all-start.1 = ((f32[16,256,128]{2,1,0:T(8,128)}), f32[16,256,128]{2,1,0:T(8,128)S(1)}, u32[]{:S(2)}, u32[]{:S(2)}) async-start(f32[16,256,128]{2,1,0:T(8,128)} %broadcast_in_dim.7), calls=%async_computation.1 | async-start | bytes 4194304 | tf_op jit(solution)/shard_map/all_to_all | solution.py:64
  32.2 1.5 %fusion.22 = f32[1024]{0:T(1024)S(1)} fusion(bf16[16,64,512]{2,1,0:T(8,128)(2,1)} %copy-done.1), kind=kLoop, calls=%fused_computation.36 | loop fusion | flops 1571840 | bytes 1052672 | tf_op jit(solution)/shard_map/pd,pd->p/dot_general | solution.py:34
  33.7 0.0 copy-start.3
  33.8 0.0 copy-start.5
  33.8 30.3 %fusion.15 = f32[1024,1024]{0,1:T(8,128)} fusion(bf16[1024,512]{1,0:T(8,128)(2,1)} %bitcast.29, f32[1024]{0:T(1024)S(1)} %get-tuple-element.21, f32[1024]{0:T(1024)S(1)} %get-tuple-element.13, f32[1024]{0:T(1024)S(1)} %get-tuple-element.20, f32[1024]{0:T(1024)S(1)} %get-tuple-element.12, f32[1024]{0:T(1024)S(1)} %get-tuple-element.19, ...), kind=kOutput, calls=%fused_computation.19 | convolution fusion | flops 1218445312 | bytes 6356996 | tf_op jit(solution)/shard_map/dot_general | solution.py:33
  64.1 0.0 all-to-all-done.1
  64.1 0.0 copy-done
  64.1 0.7 convolution_bitcast_fusion.1
  64.8 0.0 copy-start.2
  64.8 0.1 collective-permute-start
  64.9 1.2 %collective-permute-done = f32[64,128]{1,0:T(8,128)S(1)} collective-permute-done((f32[64,128]{1,0:T(8,128)S(1)}, f32[64,128]{1,0:T(8,128)S(1)}, u32[]{:S(2)}, u32[]{:S(2)}) %collective-permute-start) | collective-permute-done | bytes 32800 | tf_op jit(solution)/shard_map/ppermute | solution.py:75
  66.1 1.9 %collective-permute-start.1 = (f32[64,128]{1,0:T(8,128)S(1)}, f32[64,128]{1,0:T(8,128)S(1)}, u32[]{:S(2)}, u32[]{:S(2)}) collective-permute-start(f32[64,128]{1,0:T(8,128)S(1)} %add.193), channel_id=1, source_target_pairs={{0,32},{16,48},{32,0},{48,16},{64,96},{80,112},{96,64},{112,80},{1... | collective-permute-start | bytes 98312 | tf_op jit(solution)/shard_map/ppermute | solution.py:75
  68.1 2.0 %collective-permute-done.1 = f32[64,128]{1,0:T(8,128)S(1)} collective-permute-done((f32[64,128]{1,0:T(8,128)S(1)}, f32[64,128]{1,0:T(8,128)S(1)}, u32[]{:S(2)}, u32[]{:S(2)}) %collective-permute-start.1) | collective-permute-done | bytes 32800 | tf_op jit(solution)/shard_map/ppermute | solution.py:75
  70.0 3.9 %collective-permute-start.2 = (f32[64,128]{1,0:T(8,128)S(1)}, f32[64,128]{1,0:T(8,128)S(1)}, u32[]{:S(2)}, u32[]{:S(2)}) collective-permute-start(f32[64,128]{1,0:T(8,128)S(1)} %add.194), channel_id=1, source_target_pairs={{0,64},{16,80},{32,96},{48,112},{64,0},{80,16},{96,32},{112,48},{1... | collective-permute-start | bytes 98312 | tf_op jit(solution)/shard_map/ppermute | solution.py:75
  73.9 1.9 %collective-permute-done.2 = f32[64,128]{1,0:T(8,128)S(1)} collective-permute-done((f32[64,128]{1,0:T(8,128)S(1)}, f32[64,128]{1,0:T(8,128)S(1)}, u32[]{:S(2)}, u32[]{:S(2)}) %collective-permute-start.2) | collective-permute-done | bytes 32800 | tf_op jit(solution)/shard_map/ppermute | solution.py:75
  75.8 0.0 copy-done.3
  75.8 0.0 copy-done.5
  75.8 0.4 convolution_bitcast_fusion
  76.2 0.2 copy.10
  76.4 17.1 %all_to_all.20 = f32[16,64,128]{2,1,0:T(8,128)S(1)} all-to-all(f32[16,64,128]{2,1,0:T(8,128)S(1)} %bitcast.30), channel_id=1, replica_groups=mesh['pr'=8,'pc'=16] {'pc'}, dimensions={0} | all-to-all | bytes 1048576 | tf_op jit(solution)/shard_map/all_to_all | solution.py:68
  93.6 13.1 %all_to_all.21 = f32[16,64,128]{2,1,0:T(8,128)S(1)} all-to-all(f32[16,64,128]{2,1,0:T(8,128)S(1)} %broadcast_in_dim.8), channel_id=1, replica_groups=mesh['pr'=8,'pc'=16] {'pc'}, dimensions={0} | all-to-all | bytes 1048576 | tf_op jit(solution)/shard_map/all_to_all | solution.py:64
  106.7 0.0 copy-done.2
  106.7 4.8 %convolution_add_fusion = f32[1024,128]{1,0:T(8,128)} fusion(f32[1024,128]{1,0:T(8,128)S(1)} %copy-done.2, f32[1024,1024]{0,1:T(8,128)} %fusion.15, f32[1024,128]{1,0:T(8,128)S(1)} %bitcast.31), kind=kOutput, calls=%fused_computation.37 | convolution fusion | flops 805437440 | bytes 5767168 | tf_op jit(solution)/shard_map/dot_general | solution.py:53
  (6 shorter events, 0.1 us)
Async XLA Ops:
  0.0 64.1 %copy-start = (f32[64,4096]{1,0:T(8,128)S(1)}, f32[64,4096]{1,0:T(8,128)}, u32[]{:S(2)}) copy-start(f32[64,4096]{1,0:T(8,128)} %param.9) | copy-start | bytes 3145732
  0.0 26.8 %copy-start.4 = (f32[256,128]{1,0:T(8,128)S(1)}, f32[256,128]{1,0:T(8,128)}, u32[]{:S(2)}) copy-start(f32[256,128]{1,0:T(8,128)} %param.10) | copy-start | bytes 393220
  2.0 24.8 %all-to-all-start = ((bf16[16,64,512]{2,1,0:T(8,128)(2,1)}), bf16[16,64,512]{2,1,0:T(8,128)(2,1)S(1)}, u32[]{:S(2)}, u32[]{:S(2)}) async-start(bf16[16,64,512]{2,1,0:T(8,128)(2,1)} %broadcast_in_dim.6), calls=%async_computation | async-start | bytes 2097152 | tf_op jit(solution)/shard_map/all_to_all | solution.py:64
  26.8 1.6 %copy-start.1 = (bf16[16,64,512]{2,1,0:T(8,128)(2,1)}, bf16[16,64,512]{2,1,0:T(8,128)(2,1)S(1)}, u32[]{:S(2)}) copy-start(bf16[16,64,512]{2,1,0:T(8,128)(2,1)S(1)} %all-to-all-done) | copy-start | bytes 3145732
  28.5 35.6 %all-to-all-start.1 = ((f32[16,256,128]{2,1,0:T(8,128)}), f32[16,256,128]{2,1,0:T(8,128)S(1)}, u32[]{:S(2)}, u32[]{:S(2)}) async-start(f32[16,256,128]{2,1,0:T(8,128)} %broadcast_in_dim.7), calls=%async_computation.1 | async-start | bytes 4194304 | tf_op jit(solution)/shard_map/all_to_all | solution.py:64
  33.7 42.1 %copy-start.3 = (f32[64,1024]{1,0:T(8,128)S(1)}, f32[64,1024]{1,0:T(8,128)}, u32[]{:S(2)}) copy-start(f32[64,1024]{1,0:T(8,128)} %param.12) | copy-start | bytes 786436
  33.8 42.1 %copy-start.5 = (f32[64,128]{1,0:T(8,128)S(1)}, f32[64,128]{1,0:T(8,128)}, u32[]{:S(2)}) copy-start(f32[64,128]{1,0:T(8,128)} %param.11) | copy-start | bytes 98308
  64.8 41.9 %copy-start.2 = (f32[1024,128]{1,0:T(8,128)S(1)}, f32[1024,128]{1,0:T(8,128)}, u32[]{:S(2)}) copy-start(f32[1024,128]{1,0:T(8,128)} %param.13) | copy-start | bytes 1572868
  64.8 1.3 %collective-permute-start = (f32[64,128]{1,0:T(8,128)S(1)}, f32[64,128]{1,0:T(8,128)S(1)}, u32[]{:S(2)}, u32[]{:S(2)}) collective-permute-start(f32[64,128]{1,0:T(8,128)S(1)} %convolution_bitcast_fusion.1), channel_id=1, source_target_pairs={{0,16},{16,0},{32,48},{48,32},{64,80},{80,64},{96,112},{112,96},{1... | collective-permute-start | bytes 98312 | tf_op jit(solution)/shard_map/ppermute | solution.py:75
  66.1 3.9 %collective-permute-start.1 = (f32[64,128]{1,0:T(8,128)S(1)}, f32[64,128]{1,0:T(8,128)S(1)}, u32[]{:S(2)}, u32[]{:S(2)}) collective-permute-start(f32[64,128]{1,0:T(8,128)S(1)} %add.193), channel_id=1, source_target_pairs={{0,32},{16,48},{32,0},{48,16},{64,96},{80,112},{96,64},{112,80},{1... | collective-permute-start | bytes 98312 | tf_op jit(solution)/shard_map/ppermute | solution.py:75
  70.0 5.8 %collective-permute-start.2 = (f32[64,128]{1,0:T(8,128)S(1)}, f32[64,128]{1,0:T(8,128)S(1)}, u32[]{:S(2)}, u32[]{:S(2)}) collective-permute-start(f32[64,128]{1,0:T(8,128)S(1)} %add.194), channel_id=1, source_target_pairs={{0,64},{16,80},{32,96},{48,112},{64,0},{80,16},{96,32},{112,48},{1... | collective-permute-start | bytes 98312 | tf_op jit(solution)/shard_map/ppermute | solution.py:75

commit v8 on v7

--- a/solution.py
+++ b/solution.py
@@ -84,6 +84,7 @@
     n_pc = lax.axis_size("pc")
     rows = predictions_in.shape[0]
     own = lax.axis_index("pc")
+    inverse_full = lax.all_gather(inverse_block, "pc", axis=0, tiled=True)
     panel_all = gather_rows(panel_points, "pc", n_pc)
     test_own = lax.dynamic_slice_in_dim(test_points, own * rows, rows, 0)
     test_norms = jnp.einsum(
@@ -100,7 +101,7 @@
     )
     carried = butterfly_sum(partial_sum, "pr", n_pr)
     residual = targets - carried
-    alpha_panel = sum_rows(contract_rows(inverse_block, residual), "pc", n_pc)
+    alpha_panel = contract_rows(inverse_full, gather_rows(residual, "pc", n_pc))
     update = contract_rows(kern, alpha_panel)
     return predictions_in + update
 

time: 112 us -> 123 us (1.098)
  blocking collectives: 30.2 us -> 16.7 us
  between operations: 0.12 us -> 13.5 us
  waiting for transfers between devices: 21.2 us -> 31.1 us
    all_to_all x1 -> x0, blocking collectives: 17.1 us -> none  [sum_rows(): lax.all_to_all(x.reshape((n, -1) + x.shape[1:]), axis, 0, 0, tiled=False)]
    all_to_all x2, waiting for transfers between devices: 16.1 us -> 25.4 us  [gather_rows(): lax.all_to_all(copies, axis, 0, 0, tiled=False).reshape((-1,) + x.shape[1:])]
    all_to_all x1, blocking collectives: 13.1 us -> 16.7 us  [gather_rows(): lax.all_to_all(copies, axis, 0, 0, tiled=False).reshape((-1,) + x.shape[1:])]
  transfers between devices with their start and end apart: 5 -> 6, of which waited for: 4 -> 5; matrix products, arithmetic and copies ran while one was open for 30% -> 31% of each run, Pallas kernels for 0% -> 0%
where the time goes in v8:
time: 123 us
  matrix products  37.3 us (30%)
  waiting for transfers between devices  31.1 us (25%)
  starting transfers between devices  17.3 us (14%)
  blocking collectives  16.7 us (14%)
  between operations  13.5 us (11%)
  local copies, waits for them, and re-layouts  3.69 us (3%)
  other arithmetic  3.05 us (2%)
    dot_general x1, matrix products, arc_kernel(): cross = jnp.dot(panel, test.T, preferred_element_type=jnp.float32) / width  30.3 us
    all_to_all x2, waiting for transfers between devices, gather_rows(): lax.all_to_all(copies, axis, 0, 0, tiled=False).reshape((-1,) + x.shape[1:])  25.4 us
    all_to_all x1, blocking collectives, gather_rows(): lax.all_to_all(copies, axis, 0, 0, tiled=False).reshape((-1,) + x.shape[1:])  16.7 us
    all_to_all x2, starting transfers between devices, gather_rows(): lax.all_to_all(copies, axis, 0, 0, tiled=False).reshape((-1,) + x.shape[1:])  10.9 us
    ppermute x3, starting transfers between devices, butterfly_sum(): x = x + lax.ppermute(x, axis, [(i, i ^ step) for i in range(n)])  6.41 us
    dot_general x2, matrix products, contract_rows(): lax.dot_general(left, right, (((0,), (0,)), ((), ())), precision=lax.Prec...  6.23 us
    ppermute x3, waiting for transfers between devices, butterfly_sum(): x = x + lax.ppermute(x, axis, [(i, i ^ step) for i in range(n)])  4.98 us
    broadcast_in_dim x3, local copies, waits for them, and re-layouts, gather_rows(): copies = jnp.broadcast_to(x[None], (n,) + x.shape)  3.66 us
  transfers between devices with their start and end apart: 6, of which 5 were waited for; matrix products, arithmetic and copies ran while one was open for 31% of the time, Pallas kernels for 0%

profile of v8, /device:TPU:0, one launch (start us, length us, event | category | flops | bytes accessed | tf_op | source)
XLA Modules:
  0.0 122.7 jit_solution(7008076951389470779)
XLA Ops:
  6.5 0.0 copy-start
  6.5 0.0 copy-start.4
  6.5 0.0 all-gather.2.cloned.1.call-start
  6.5 0.7 all-gather.2.cloned.1.call-update
  7.3 1.9 %broadcast_in_dim.6 = bf16[16,64,512]{2,1,0:T(8,128)(2,1)} broadcast(bf16[64,512]{1,0:T(8,128)(2,1)} %param.8), dimensions={1,2} | broadcast | bytes 1114112 | tf_op jit(solution)/shard_map/broadcast_in_dim | solution.py:63
  9.2 7.1 %all-to-all-start = ((bf16[16,64,512]{2,1,0:T(8,128)(2,1)}), bf16[16,64,512]{2,1,0:T(8,128)(2,1)S(1)}, u32[]{:S(2)}, u32[]{:S(2)}) async-start(bf16[16,64,512]{2,1,0:T(8,128)(2,1)} %broadcast_in_dim.6), calls=%async_computation | async-start | bytes 2097152 | tf_op jit(solution)/shard_map/all_to_all | solution.py:64
  16.3 1.5 %fusion.21 = f32[1024]{0:T(1024)S(1)} fusion(bf16[16384,512]{1,0:T(8,128)(2,1)} %param.7, s32[]{:T(128)S(6)} %select_n.52), kind=kLoop, calls=%fused_computation.34 | loop fusion | flops 1571840 | bytes 1052676 | tf_op jit(solution)/shard_map/nd,nd->n/dot_general | solution.py:90
  17.9 17.9 %all-to-all-done = bf16[16,64,512]{2,1,0:T(8,128)(2,1)S(1)} async-done(((bf16[16,64,512]{2,1,0:T(8,128)(2,1)}), bf16[16,64,512]{2,1,0:T(8,128)(2,1)S(1)}, u32[]{:S(2)}, u32[]{:S(2)}) %all-to-all-start) | async-done | bytes 1048608 | tf_op jit(solution)/shard_map/all_to_all | solution.py:64
  35.8 0.0 copy-done.4
  35.8 0.0 copy-start.2
  35.8 1.7 %broadcast_in_dim.7 = f32[16,256,128]{2,1,0:T(8,128)} broadcast(f32[256,128]{1,0:T(8,128)S(1)} %copy-done.4), dimensions={1,2} | broadcast | bytes 2228224 | tf_op jit(solution)/shard_map/broadcast_in_dim | solution.py:63
  37.5 0.0 copy-done.2
  37.5 3.7 %all-to-all-start.1 = ((f32[16,256,128]{2,1,0:T(8,128)}), f32[16,256,128]{2,1,0:T(8,128)S(1)}, u32[]{:S(2)}, u32[]{:S(2)}) async-start(f32[16,256,128]{2,1,0:T(8,128)} %broadcast_in_dim.7), calls=%async_computation.1 | async-start | bytes 4194304 | tf_op jit(solution)/shard_map/all_to_all | solution.py:64
  41.2 1.5 %fusion.22 = f32[1024]{0:T(1024)S(1)} fusion(bf16[16,64,512]{2,1,0:T(8,128)(2,1)} %copy-done.2), kind=kLoop, calls=%fused_computation.36 | loop fusion | flops 1571840 | bytes 1052672 | tf_op jit(solution)/shard_map/pd,pd->p/dot_general | solution.py:34
  42.8 0.0 copy-start.5
  42.8 30.3 %fusion.15 = f32[1024,1024]{0,1:T(8,128)} fusion(bf16[1024,512]{1,0:T(8,128)(2,1)} %bitcast.27, f32[1024]{0:T(1024)S(1)} %get-tuple-element.21, f32[1024]{0:T(1024)S(1)} %get-tuple-element.13, f32[1024]{0:T(1024)S(1)} %get-tuple-element.20, f32[1024]{0:T(1024)S(1)} %get-tuple-element.12, f32[1024]{0:T(1024)S(1)} %get-tuple-element.19, ...), kind=kOutput, calls=%fused_computation.19 | convolution fusion | flops 1218445312 | bytes 6356996 | tf_op jit(solution)/shard_map/dot_general | solution.py:33
  73.1 7.5 %all-to-all-done.1 = f32[16,256,128]{2,1,0:T(8,128)S(1)} async-done(((f32[16,256,128]{2,1,0:T(8,128)}), f32[16,256,128]{2,1,0:T(8,128)S(1)}, u32[]{:S(2)}, u32[]{:S(2)}) %all-to-all-start.1) | async-done | bytes 2097184 | tf_op jit(solution)/shard_map/all_to_all | solution.py:64
  80.6 0.0 copy-done
  80.6 0.7 convolution_bitcast_fusion
  81.3 0.0 copy-start.3
  81.4 0.1 collective-permute-start
  81.5 1.2 collective-permute-done
  82.7 2.1 %collective-permute-start.1 = (f32[64,128]{1,0:T(8,128)S(1)}, f32[64,128]{1,0:T(8,128)S(1)}, u32[]{:S(2)}, u32[]{:S(2)}) collective-permute-start(f32[64,128]{1,0:T(8,128)S(1)} %add.193), channel_id=1, source_target_pairs={{0,32},{16,48},{32,0},{48,16},{64,96},{80,112},{96,64},{112,80},{1... | collective-permute-start | bytes 98312 | tf_op jit(solution)/shard_map/ppermute | solution.py:75
  84.8 1.9 %collective-permute-done.1 = f32[64,128]{1,0:T(8,128)S(1)} collective-permute-done((f32[64,128]{1,0:T(8,128)S(1)}, f32[64,128]{1,0:T(8,128)S(1)}, u32[]{:S(2)}, u32[]{:S(2)}) %collective-permute-start.1) | collective-permute-done | bytes 32800 | tf_op jit(solution)/shard_map/ppermute | solution.py:75
  86.7 4.2 %collective-permute-start.2 = (f32[64,128]{1,0:T(8,128)S(1)}, f32[64,128]{1,0:T(8,128)S(1)}, u32[]{:S(2)}, u32[]{:S(2)}) collective-permute-start(f32[64,128]{1,0:T(8,128)S(1)} %add.194), channel_id=1, source_target_pairs={{0,64},{16,80},{32,96},{48,112},{64,0},{80,16},{96,32},{112,48},{1... | collective-permute-start | bytes 98312 | tf_op jit(solution)/shard_map/ppermute | solution.py:75
  90.9 1.9 %collective-permute-done.2 = f32[64,128]{1,0:T(8,128)S(1)} collective-permute-done((f32[64,128]{1,0:T(8,128)S(1)}, f32[64,128]{1,0:T(8,128)S(1)}, u32[]{:S(2)}, u32[]{:S(2)}) %collective-permute-start.2) | collective-permute-done | bytes 32800 | tf_op jit(solution)/shard_map/ppermute | solution.py:75
  92.8 0.0 copy-done.5
  92.8 16.7 %all_to_all.15 = f32[16,64,128]{2,1,0:T(8,128)S(1)} all-to-all(f32[16,64,128]{2,1,0:T(8,128)S(1)} %broadcast_in_dim.8), channel_id=1, replica_groups=mesh['pr'=8,'pc'=16] {'pc'}, dimensions={0} | all-to-all | bytes 1048576 | tf_op jit(solution)/shard_map/all_to_all | solution.py:64
  109.5 0.0 all-gather.2.cloned.1.call-done
  109.5 0.0 copy-start.1
  109.5 3.6 %fusion.25 = f32[128,1024]{1,0:T(8,128)S(1)} fusion(f32[1024,128]{1,0:T(8,128)S(1)} %bitcast.28, f32[1024,1024]{1,0:T(8,128)} %all-gather.2.cloned.1.call-done), kind=kOutput, calls=%fused_computation.58 | convolution fusion | flops 805306368 | bytes 5242880 | tf_op jit(solution)/shard_map/dot_general | solution.py:53
  113.2 0.0 copy-done.3
  113.2 0.0 copy-done.1
  113.2 2.6 %convolution_add_fusion = f32[1024,128]{1,0:T(8,128)} fusion(f32[1024,128]{1,0:T(8,128)S(1)} %copy-done.3, f32[1024,1024]{0,1:T(8,128)S(1)} %copy-done.1, f32[128,1024]{1,0:T(8,128)S(1)} %fusion.25), kind=kOutput, calls=%fused_computation.37 | convolution fusion | flops 805437440 | bytes 5767168 | tf_op jit(solution)/shard_map/dot_general | solution.py:53
  (6 shorter events, 0.1 us)
Async XLA Ops:
  6.5 74.1 %copy-start = (f32[64,4096]{1,0:T(8,128)S(1)}, f32[64,4096]{1,0:T(8,128)}, u32[]{:S(2)}) copy-start(f32[64,4096]{1,0:T(8,128)} %param.9) | copy-start | bytes 3145732
  6.5 29.3 %copy-start.4 = (f32[256,128]{1,0:T(8,128)S(1)}, f32[256,128]{1,0:T(8,128)}, u32[]{:S(2)}) copy-start(f32[256,128]{1,0:T(8,128)} %param.10) | copy-start | bytes 393220
  6.5 103.0 %all-gather.2.cloned.1.call-start = ((), (), s32[]{:S(2)}) async-start(), calls=%async_computation.3 | async-start | bytes 4456448 | tf_op jit(solution)/shard_map/all_gather | solution.py:87
  9.2 26.6 %all-to-all-start = ((bf16[16,64,512]{2,1,0:T(8,128)(2,1)}), bf16[16,64,512]{2,1,0:T(8,128)(2,1)S(1)}, u32[]{:S(2)}, u32[]{:S(2)}) async-start(bf16[16,64,512]{2,1,0:T(8,128)(2,1)} %broadcast_in_dim.6), calls=%async_computation | async-start | bytes 2097152 | tf_op jit(solution)/shard_map/all_to_all | solution.py:64
  35.8 1.7 %copy-start.2 = (bf16[16,64,512]{2,1,0:T(8,128)(2,1)}, bf16[16,64,512]{2,1,0:T(8,128)(2,1)S(1)}, u32[]{:S(2)}) copy-start(bf16[16,64,512]{2,1,0:T(8,128)(2,1)S(1)} %all-to-all-done) | copy-start | bytes 3145732
  37.5 43.1 %all-to-all-start.1 = ((f32[16,256,128]{2,1,0:T(8,128)}), f32[16,256,128]{2,1,0:T(8,128)S(1)}, u32[]{:S(2)}, u32[]{:S(2)}) async-start(f32[16,256,128]{2,1,0:T(8,128)} %broadcast_in_dim.7), calls=%async_computation.1 | async-start | bytes 4194304 | tf_op jit(solution)/shard_map/all_to_all | solution.py:64
  42.8 50.0 %copy-start.5 = (f32[64,128]{1,0:T(8,128)S(1)}, f32[64,128]{1,0:T(8,128)}, u32[]{:S(2)}) copy-start(f32[64,128]{1,0:T(8,128)} %param.11) | copy-start | bytes 98308
  81.3 31.8 %copy-start.3 = (f32[1024,128]{1,0:T(8,128)S(1)}, f32[1024,128]{1,0:T(8,128)}, u32[]{:S(2)}) copy-start(f32[1024,128]{1,0:T(8,128)} %param.13) | copy-start | bytes 1572868
  81.4 1.3 %collective-permute-start = (f32[64,128]{1,0:T(8,128)S(1)}, f32[64,128]{1,0:T(8,128)S(1)}, u32[]{:S(2)}, u32[]{:S(2)}) collective-permute-start(f32[64,128]{1,0:T(8,128)S(1)} %convolution_bitcast_fusion), channel_id=1, source_target_pairs={{0,16},{16,0},{32,48},{48,32},{64,80},{80,64},{96,112},{112,96},{1... | collective-permute-start | bytes 98312 | tf_op jit(solution)/shard_map/ppermute | solution.py:75
  82.7 4.0 %collective-permute-start.1 = (f32[64,128]{1,0:T(8,128)S(1)}, f32[64,128]{1,0:T(8,128)S(1)}, u32[]{:S(2)}, u32[]{:S(2)}) collective-permute-start(f32[64,128]{1,0:T(8,128)S(1)} %add.193), channel_id=1, source_target_pairs={{0,32},{16,48},{32,0},{48,16},{64,96},{80,112},{96,64},{112,80},{1... | collective-permute-start | bytes 98312 | tf_op jit(solution)/shard_map/ppermute | solution.py:75
  86.7 6.1 %collective-permute-start.2 = (f32[64,128]{1,0:T(8,128)S(1)}, f32[64,128]{1,0:T(8,128)S(1)}, u32[]{:S(2)}, u32[]{:S(2)}) collective-permute-start(f32[64,128]{1,0:T(8,128)S(1)} %add.194), channel_id=1, source_target_pairs={{0,64},{16,80},{32,96},{48,112},{64,0},{80,16},{96,32},{112,48},{1... | collective-permute-start | bytes 98312 | tf_op jit(solution)/shard_map/ppermute | solution.py:75
  109.5 3.6 %copy-start.1 = (f32[1024,1024]{0,1:T(8,128)S(1)}, f32[1024,1024]{0,1:T(8,128)}, u32[]{:S(2)}) copy-start(f32[1024,1024]{0,1:T(8,128)} %fusion.15) | copy-start | bytes 12582916
Sparse Core Ops, SparseCore 0:
  9.5 73.9 all-gather.1

commit v9 on v7

--- a/solution.py
+++ b/solution.py
@@ -64,6 +64,17 @@
     return lax.all_to_all(copies, axis, 0, 0, tiled=False).reshape((-1,) + x.shape[1:])
 
 
+def doubling_gather(x, axis, n):
+    me = lax.axis_index(axis)
+    step = 1
+    while step < n:
+        upper = (me // step) % 2 == 1
+        other = lax.ppermute(x, axis, [(i, i ^ step) for i in range(n)])
+        x = jnp.where(upper, jnp.concatenate([other, x]), jnp.concatenate([x, other]))
+        step *= 2
+    return x
+
+
 def sum_rows(x, axis, n):
     blocks = lax.all_to_all(x.reshape((n, -1) + x.shape[1:]), axis, 0, 0, tiled=False)
     return gather_rows(blocks.sum(0), axis, n)
@@ -84,7 +95,7 @@
     n_pc = lax.axis_size("pc")
     rows = predictions_in.shape[0]
     own = lax.axis_index("pc")
-    panel_all = gather_rows(panel_points, "pc", n_pc)
+    panel_all = doubling_gather(panel_points, "pc", n_pc)
     test_own = lax.dynamic_slice_in_dim(test_points, own * rows, rows, 0)
     test_norms = jnp.einsum(
         "nd,nd->n", test_own, test_own, preferred_element_type=jnp.float32

time: 112 us -> 134 us (1.20)
  waiting for transfers between devices: 21.2 us -> 33.1 us
  starting transfers between devices: 16.8 us -> 21 us
  other arithmetic: 3.08 us -> 5.66 us
  blocking collectives: 30.2 us -> 32.4 us
  matrix products: 36.3 us -> 38.2 us
    ppermute x0 -> x4, waiting for transfers between devices: none -> 28 us  [doubling_gather(): other = lax.ppermute(x, axis, [(i, i ^ step) for i in range(n)])]
    all_to_all x2 -> x1, waiting for transfers between devices: 16.1 us -> 0.01 us  [gather_rows(): lax.all_to_all(copies, axis, 0, 0, tiled=False).reshape((-1,) + x.shape[1:])]
    ppermute x0 -> x4, starting transfers between devices: none -> 9.89 us  [doubling_gather(): other = lax.ppermute(x, axis, [(i, i ^ step) for i in range(n)])]
    all_to_all x2 -> x1, starting transfers between devices: 10.9 us -> 5.26 us  [gather_rows(): lax.all_to_all(copies, axis, 0, 0, tiled=False).reshape((-1,) + x.shape[1:])]
    all_to_all x1, blocking collectives: 17.1 us -> 19.3 us  [sum_rows(): lax.all_to_all(x.reshape((n, -1) + x.shape[1:]), axis, 0, 0, tiled=False)]
    select_n x0 -> x3, other arithmetic: none -> 2.01 us  [doubling_gather(): jnp.where(upper, jnp.concatenate([other, x]), jnp.concatenate([x, other]))]
    dot_general x2, matrix products: 5.2 us -> 6.84 us  [contract_rows(): lax.dot_general(left, right, (((0,), (0,)), ((), ())), precision=lax.Prec...]
    broadcast_in_dim x3 -> x2, local copies, waits for them, and re-layouts: 3.69 us -> 2.46 us  [gather_rows(): copies = jnp.broadcast_to(x[None], (n,) + x.shape)]
  transfers between devices with their start and end apart: 5 -> 8, of which waited for: 4 -> 7; matrix products, arithmetic and copies ran while one was open for 30% -> 28% of each run, Pallas kernels for 0% -> 0%
where the time goes in v9:
time: 134 us; the launch traced here: 133 us
  matrix products  38.2 us (29%)
  waiting for transfers between devices  33.1 us (25%)
  blocking collectives  32.4 us (24%)
  starting transfers between devices  21 us (16%)
  other arithmetic  5.66 us (4%)
  local copies, waits for them, and re-layouts  2.68 us (2%)
    dot_general x1, matrix products, arc_kernel(): cross = jnp.dot(panel, test.T, preferred_element_type=jnp.float32) / width  30.7 us
    ppermute x4, waiting for transfers between devices, doubling_gather(): other = lax.ppermute(x, axis, [(i, i ^ step) for i in range(n)])  28 us
    all_to_all x1, blocking collectives, sum_rows(): lax.all_to_all(x.reshape((n, -1) + x.shape[1:]), axis, 0, 0, tiled=False)  19.3 us
    all_to_all x1, blocking collectives, gather_rows(): lax.all_to_all(copies, axis, 0, 0, tiled=False).reshape((-1,) + x.shape[1:])  13.1 us
    ppermute x4, starting transfers between devices, doubling_gather(): other = lax.ppermute(x, axis, [(i, i ^ step) for i in range(n)])  9.89 us
    dot_general x2, matrix products, contract_rows(): lax.dot_general(left, right, (((0,), (0,)), ((), ())), precision=lax.Prec...  6.84 us
    ppermute x3, starting transfers between devices, butterfly_sum(): x = x + lax.ppermute(x, axis, [(i, i ^ step) for i in range(n)])  5.89 us
    all_to_all x1, starting transfers between devices, gather_rows(): lax.all_to_all(copies, axis, 0, 0, tiled=False).reshape((-1,) + x.shape[1:])  5.26 us
  transfers between devices with their start and end apart: 8, of which 7 were waited for; matrix products, arithmetic and copies ran while one was open for 28% of the time, Pallas kernels for 0%

profile of v9, /device:TPU:0, one launch (start us, length us, event | category | flops | bytes accessed | tf_op | source)
XLA Modules:
  0.0 133.3 jit_solution(1611489433298569725)
XLA Ops:
  0.0 0.0 copy-start
  0.0 1.6 %collective-permute-start = (bf16[64,512]{1,0:T(8,128)(2,1)}, bf16[64,512]{1,0:T(8,128)(2,1)S(1)}, u32[]{:S(2)}, u32[]{:S(2)}) collective-permute-start(bf16[64,512]{1,0:T(8,128)(2,1)} %param.8), channel_id=1, source_target_pairs={{0,1},{1,0},{2,3},{3,2},{4,5},{5,4},{6,7},{7,6},{8,9},{9,8},{10,11... | collective-permute-start | bytes 196616 | tf_op jit(solution)/shard_map/ppermute | solution.py:72
  1.6 2.9 %collective-permute-done = bf16[64,512]{1,0:T(8,128)(2,1)S(1)} collective-permute-done((bf16[64,512]{1,0:T(8,128)(2,1)}, bf16[64,512]{1,0:T(8,128)(2,1)S(1)}, u32[]{:S(2)}, u32[]{:S(2)}) %collective-permute-start) | collective-permute-done | bytes 65568 | tf_op jit(solution)/shard_map/ppermute | solution.py:72
  4.5 0.9 maximum_select_fusion.4
  5.4 3.2 %collective-permute-start.1 = (bf16[128,512]{1,0:T(8,128)(2,1)S(1)}, bf16[128,512]{1,0:T(8,128)(2,1)S(1)}, u32[]{:S(2)}, u32[]{:S(2)}) collective-permute-start(bf16[128,512]{1,0:T(8,128)(2,1)S(1)} %maximum_select_fusion.4), channel_id=1, source_target_pairs={{0,2},{1,3},{2,0},{3,1},{4,6},{5,7},{6,4},{7,5},{8,10},{9,11},{10,... | collective-permute-start | bytes 393224 | tf_op jit(solution)/shard_map/ppermute | solution.py:72
  8.6 3.3 %collective-permute-done.1 = bf16[128,512]{1,0:T(8,128)(2,1)S(1)} collective-permute-done((bf16[128,512]{1,0:T(8,128)(2,1)S(1)}, bf16[128,512]{1,0:T(8,128)(2,1)S(1)}, u32[]{:S(2)}, u32[]{:S(2)}) %collective-permute-start.1) | collective-permute-done | bytes 131104 | tf_op jit(solution)/shard_map/ppermute | solution.py:72
  12.0 0.1 maximum_select_fusion.2
  12.0 1.8 %collective-permute-start.2 = (bf16[256,512]{1,0:T(8,128)(2,1)S(1)}, bf16[256,512]{1,0:T(8,128)(2,1)S(1)}, u32[]{:S(2)}, u32[]{:S(2)}) collective-permute-start(bf16[256,512]{1,0:T(8,128)(2,1)S(1)} %maximum_select_fusion.2), channel_id=1, source_target_pairs={{0,4},{1,5},{2,6},{3,7},{4,0},{5,1},{6,2},{7,3},{8,12},{9,13},{10,... | collective-permute-start | bytes 786440 | tf_op jit(solution)/shard_map/ppermute | solution.py:72
  13.8 4.7 %collective-permute-done.2 = bf16[256,512]{1,0:T(8,128)(2,1)S(1)} collective-permute-done((bf16[256,512]{1,0:T(8,128)(2,1)S(1)}, bf16[256,512]{1,0:T(8,128)(2,1)S(1)}, u32[]{:S(2)}, u32[]{:S(2)}) %collective-permute-start.2) | collective-permute-done | bytes 262176 | tf_op jit(solution)/shard_map/ppermute | solution.py:72
  18.5 1.0 maximum_select_fusion.1
  19.5 3.3 %collective-permute-start.3 = (bf16[512,512]{1,0:T(8,128)(2,1)}, bf16[512,512]{1,0:T(8,128)(2,1)}, u32[]{:S(2)}, u32[]{:S(2)}) collective-permute-start(bf16[512,512]{1,0:T(8,128)(2,1)} %maximum_select_fusion.1), channel_id=1, source_target_pairs={{0,8},{1,9},{2,10},{3,11},{4,12},{5,13},{6,14},{7,15},{8,0},{9,1},... | collective-permute-start | bytes 1572872 | tf_op jit(solution)/shard_map/ppermute | solution.py:72
  22.8 2.4 %broadcast_in_dim.4 = f32[16,256,128]{2,1,0:T(8,128)} broadcast(f32[256,128]{1,0:T(8,128)} %param.10), dimensions={1,2} | broadcast | bytes 2228224 | tf_op jit(solution)/shard_map/broadcast_in_dim | solution.py:63
  25.2 5.3 %all-to-all-start = ((f32[16,256,128]{2,1,0:T(8,128)}), f32[16,256,128]{2,1,0:T(8,128)S(1)}, u32[]{:S(2)}, u32[]{:S(2)}) async-start(f32[16,256,128]{2,1,0:T(8,128)} %broadcast_in_dim.4), calls=%async_computation | async-start | bytes 4194304 | tf_op jit(solution)/shard_map/all_to_all | solution.py:64
  30.5 1.5 %fusion.20 = f32[1024]{0:T(1024)S(1)} fusion(bf16[16384,512]{1,0:T(8,128)(2,1)} %param.7, s32[]{:T(128)S(6)} %select_n.129), kind=kLoop, calls=%fused_computation.33 | loop fusion | flops 1571840 | bytes 1052676 | tf_op jit(solution)/shard_map/nd,nd->n/dot_general | solution.py:100
  32.1 17.1 %collective-permute-done.3 = bf16[512,512]{1,0:T(8,128)(2,1)} collective-permute-done((bf16[512,512]{1,0:T(8,128)(2,1)}, bf16[512,512]{1,0:T(8,128)(2,1)}, u32[]{:S(2)}, u32[]{:S(2)}) %collective-permute-start.3) | collective-permute-done | bytes 524320 | tf_op jit(solution)/shard_map/ppermute | solution.py:72
  49.2 2.1 %fusion.21 = f32[1024]{0:T(1024)S(1)} fusion(bf16[512,512]{1,0:T(8,128)(2,1)} %collective-permute-done.3, bf16[512,512]{1,0:T(8,128)(2,1)} %maximum_select_fusion.1, pred[]{:T(512)S(6)} %eq.17), kind=kLoop, calls=%fused_computation.35 | loop fusion | flops 6290432 | bytes 1052673 | tf_op jit(solution)/shard_map/pd,pd->p/dot_general | solution.py:34
  51.3 0.0 copy-start.2
  51.3 0.0 copy-start.3
  51.3 30.7 %fusion.15 = f32[1024,1024]{1,0:T(8,128)} fusion(f32[1024]{0:T(1024)S(1)} %get-tuple-element.21, f32[1024]{0:T(1024)S(1)} %get-tuple-element.13, f32[1024]{0:T(1024)S(1)} %get-tuple-element.20, f32[1024]{0:T(1024)S(1)} %get-tuple-element.12, f32[1024]{0:T(1024)S(1)} %get-tuple-element.19, f32[1024]{0:T(1024)S(1)} %get-tuple-element.11, ...), kind=kOutput, calls=%fused_computation.19 | convolution fusion | flops 1223163904 | bytes 6356997 | tf_op jit(solution)/shard_map/dot_general | solution.py:33
  81.9 0.0 all-to-all-done
  81.9 0.0 copy-done
  81.9 0.7 convolution_bitcast_fusion.1
  82.7 0.0 copy-start.1
  82.7 0.1 collective-permute-start.4
  82.8 1.2 collective-permute-done.4
  84.0 1.9 %collective-permute-start.5 = (f32[64,128]{1,0:T(8,128)S(1)}, f32[64,128]{1,0:T(8,128)S(1)}, u32[]{:S(2)}, u32[]{:S(2)}) collective-permute-start(f32[64,128]{1,0:T(8,128)S(1)} %add.210), channel_id=1, source_target_pairs={{0,32},{16,48},{32,0},{48,16},{64,96},{80,112},{96,64},{112,80},{1... | collective-permute-start | bytes 98312 | tf_op jit(solution)/shard_map/ppermute | solution.py:86
  85.9 2.0 %collective-permute-done.5 = f32[64,128]{1,0:T(8,128)S(1)} collective-permute-done((f32[64,128]{1,0:T(8,128)S(1)}, f32[64,128]{1,0:T(8,128)S(1)}, u32[]{:S(2)}, u32[]{:S(2)}) %collective-permute-start.5) | collective-permute-done | bytes 32800 | tf_op jit(solution)/shard_map/ppermute | solution.py:86
  87.9 3.9 %collective-permute-start.6 = (f32[64,128]{1,0:T(8,128)S(1)}, f32[64,128]{1,0:T(8,128)S(1)}, u32[]{:S(2)}, u32[]{:S(2)}) collective-permute-start(f32[64,128]{1,0:T(8,128)S(1)} %add.211), channel_id=1, source_target_pairs={{0,64},{16,80},{32,96},{48,112},{64,0},{80,16},{96,32},{112,48},{1... | collective-permute-start | bytes 98312 | tf_op jit(solution)/shard_map/ppermute | solution.py:86
  91.8 1.9 %collective-permute-done.6 = f32[64,128]{1,0:T(8,128)S(1)} collective-permute-done((f32[64,128]{1,0:T(8,128)S(1)}, f32[64,128]{1,0:T(8,128)S(1)}, u32[]{:S(2)}, u32[]{:S(2)}) %collective-permute-start.6) | collective-permute-done | bytes 32800 | tf_op jit(solution)/shard_map/ppermute | solution.py:86
  93.7 0.0 copy-done.2
  93.7 0.0 copy-done.3
  93.7 0.4 convolution_bitcast_fusion
  94.1 0.2 copy.8
  94.3 19.3 %all_to_all.15 = f32[16,64,128]{2,1,0:T(8,128)S(1)} all-to-all(f32[16,64,128]{2,1,0:T(8,128)S(1)} %bitcast.13), channel_id=1, replica_groups=mesh['pr'=8,'pc'=16] {'pc'}, dimensions={0} | all-to-all | bytes 1048576 | tf_op jit(solution)/shard_map/all_to_all | solution.py:79
  113.7 13.1 %all_to_all.16 = f32[16,64,128]{2,1,0:T(8,128)S(1)} all-to-all(f32[16,64,128]{2,1,0:T(8,128)S(1)} %broadcast_in_dim.5), channel_id=1, replica_groups=mesh['pr'=8,'pc'=16] {'pc'}, dimensions={0} | all-to-all | bytes 1048576 | tf_op jit(solution)/shard_map/all_to_all | solution.py:64
  126.8 0.0 copy-done.1
  126.8 6.4 %convolution_add_fusion = f32[1024,128]{1,0:T(8,128)} fusion(f32[1024,128]{1,0:T(8,128)S(1)} %copy-done.1, f32[1024,1024]{1,0:T(8,128)} %fusion.15, f32[1024,128]{1,0:T(8,128)S(1)} %bitcast.14), kind=kOutput, calls=%fused_computation.36 | convolution fusion | flops 805437440 | bytes 5767168 | tf_op jit(solution)/shard_map/dot_general | solution.py:53
  (6 shorter events, 0.1 us)
Async XLA Ops:
  0.0 81.9 %copy-start = (f32[64,4096]{1,0:T(8,128)S(1)}, f32[64,4096]{1,0:T(8,128)}, u32[]{:S(2)}) copy-start(f32[64,4096]{1,0:T(8,128)} %param.9) | copy-start | bytes 3145732
  0.0 4.5 %collective-permute-start = (bf16[64,512]{1,0:T(8,128)(2,1)}, bf16[64,512]{1,0:T(8,128)(2,1)S(1)}, u32[]{:S(2)}, u32[]{:S(2)}) collective-permute-start(bf16[64,512]{1,0:T(8,128)(2,1)} %param.8), channel_id=1, source_target_pairs={{0,1},{1,0},{2,3},{3,2},{4,5},{5,4},{6,7},{7,6},{8,9},{9,8},{10,11... | collective-permute-start | bytes 196616 | tf_op jit(solution)/shard_map/ppermute | solution.py:72
  5.4 6.6 %collective-permute-start.1 = (bf16[128,512]{1,0:T(8,128)(2,1)S(1)}, bf16[128,512]{1,0:T(8,128)(2,1)S(1)}, u32[]{:S(2)}, u32[]{:S(2)}) collective-permute-start(bf16[128,512]{1,0:T(8,128)(2,1)S(1)} %maximum_select_fusion.4), channel_id=1, source_target_pairs={{0,2},{1,3},{2,0},{3,1},{4,6},{5,7},{6,4},{7,5},{8,10},{9,11},{10,... | collective-permute-start | bytes 393224 | tf_op jit(solution)/shard_map/ppermute | solution.py:72
  12.0 6.5 %collective-permute-start.2 = (bf16[256,512]{1,0:T(8,128)(2,1)S(1)}, bf16[256,512]{1,0:T(8,128)(2,1)S(1)}, u32[]{:S(2)}, u32[]{:S(2)}) collective-permute-start(bf16[256,512]{1,0:T(8,128)(2,1)S(1)} %maximum_select_fusion.2), channel_id=1, source_target_pairs={{0,4},{1,5},{2,6},{3,7},{4,0},{5,1},{6,2},{7,3},{8,12},{9,13},{10,... | collective-permute-start | bytes 786440 | tf_op jit(solution)/shard_map/ppermute | solution.py:72
  19.5 29.7 %collective-permute-start.3 = (bf16[512,512]{1,0:T(8,128)(2,1)}, bf16[512,512]{1,0:T(8,128)(2,1)}, u32[]{:S(2)}, u32[]{:S(2)}) collective-permute-start(bf16[512,512]{1,0:T(8,128)(2,1)} %maximum_select_fusion.1), channel_id=1, source_target_pairs={{0,8},{1,9},{2,10},{3,11},{4,12},{5,13},{6,14},{7,15},{8,0},{9,1},... | collective-permute-start | bytes 1572872 | tf_op jit(solution)/shard_map/ppermute | solution.py:72
  25.2 56.7 %all-to-all-start = ((f32[16,256,128]{2,1,0:T(8,128)}), f32[16,256,128]{2,1,0:T(8,128)S(1)}, u32[]{:S(2)}, u32[]{:S(2)}) async-start(f32[16,256,128]{2,1,0:T(8,128)} %broadcast_in_dim.4), calls=%async_computation | async-start | bytes 4194304 | tf_op jit(solution)/shard_map/all_to_all | solution.py:64
  51.3 42.4 %copy-start.2 = (f32[64,1024]{1,0:T(8,128)S(1)}, f32[64,1024]{1,0:T(8,128)}, u32[]{:S(2)}) copy-start(f32[64,1024]{1,0:T(8,128)} %param.12) | copy-start | bytes 786436
  51.3 42.4 %copy-start.3 = (f32[64,128]{1,0:T(8,128)S(1)}, f32[64,128]{1,0:T(8,128)}, u32[]{:S(2)}) copy-start(f32[64,128]{1,0:T(8,128)} %param.11) | copy-start | bytes 98308
  82.7 44.2 %copy-start.1 = (f32[1024,128]{1,0:T(8,128)S(1)}, f32[1024,128]{1,0:T(8,128)}, u32[]{:S(2)}) copy-start(f32[1024,128]{1,0:T(8,128)} %param.13) | copy-start | bytes 1572868
  82.7 1.3 collective-permute-start.4
  84.0 3.9 %collective-permute-start.5 = (f32[64,128]{1,0:T(8,128)S(1)}, f32[64,128]{1,0:T(8,128)S(1)}, u32[]{:S(2)}, u32[]{:S(2)}) collective-permute-start(f32[64,128]{1,0:T(8,128)S(1)} %add.210), channel_id=1, source_target_pairs={{0,32},{16,48},{32,0},{48,16},{64,96},{80,112},{96,64},{112,80},{1... | collective-permute-start | bytes 98312 | tf_op jit(solution)/shard_map/ppermute | solution.py:86
  87.9 5.8 %collective-permute-start.6 = (f32[64,128]{1,0:T(8,128)S(1)}, f32[64,128]{1,0:T(8,128)S(1)}, u32[]{:S(2)}, u32[]{:S(2)}) collective-permute-start(f32[64,128]{1,0:T(8,128)S(1)} %add.211), channel_id=1, source_target_pairs={{0,64},{16,80},{32,96},{48,112},{64,0},{80,16},{96,32},{112,48},{1... | collective-permute-start | bytes 98312 | tf_op jit(solution)/shard_map/ppermute | solution.py:86

commit v10 on v7

--- a/solution.py
+++ b/solution.py
@@ -98,9 +98,9 @@
         precision=lax.Precision.HIGH,
         preferred_element_type=jnp.float32,
     )
-    carried = butterfly_sum(partial_sum, "pr", n_pr)
-    residual = targets - carried
-    alpha_panel = sum_rows(contract_rows(inverse_block, residual), "pc", n_pc)
+    first_row = lax.axis_index("pr") == 0
+    share = jnp.where(first_row, targets, jnp.zeros_like(targets)) - partial_sum
+    alpha_panel = sum_rows(contract_rows(inverse_block, share), ("pr", "pc"), n_pr * n_pc)
     update = contract_rows(kern, alpha_panel)
     return predictions_in + update
 

time: 112 us -> 114 us (1.018)
  blocking collectives: 30.2 us -> 42.4 us
  starting transfers between devices: 16.8 us -> 10.9 us
  waiting for transfers between devices: 21.2 us -> 16.1 us
    all_to_all x1, blocking collectives: 17.1 us -> 24.6 us  [sum_rows(): lax.all_to_all(x.reshape((n, -1) + x.shape[1:]), axis, 0, 0, tiled=False)]
    ppermute x3 -> x0, starting transfers between devices: 5.89 us -> none  [butterfly_sum(): x = x + lax.ppermute(x, axis, [(i, i ^ step) for i in range(n)])]
    ppermute x3 -> x0, waiting for transfers between devices: 5.08 us -> none  [butterfly_sum(): x = x + lax.ppermute(x, axis, [(i, i ^ step) for i in range(n)])]
    all_to_all x1, blocking collectives: 13.1 us -> 17.9 us  [gather_rows(): lax.all_to_all(copies, axis, 0, 0, tiled=False).reshape((-1,) + x.shape[1:])]
  transfers between devices with their start and end apart: 5 -> 2, of which waited for: 4 -> 1; matrix products, arithmetic and copies ran while one was open for 30% -> 30% of each run, Pallas kernels for 0% -> 0%
where the time goes in v10:
time: 114 us; the launch traced here: 113 us
  blocking collectives  42.4 us (37%)
  matrix products  36.3 us (32%)
  waiting for transfers between devices  16.1 us (14%)
  starting transfers between devices  10.9 us (10%)
  local copies, waits for them, and re-layouts  3.88 us (3%)
  other arithmetic  3.17 us (3%)
    dot_general x1, matrix products, arc_kernel(): cross = jnp.dot(panel, test.T, preferred_element_type=jnp.float32) / width  30.3 us
    all_to_all x1, blocking collectives, sum_rows(): lax.all_to_all(x.reshape((n, -1) + x.shape[1:]), axis, 0, 0, tiled=False)  24.6 us
    all_to_all x1, blocking collectives, gather_rows(): lax.all_to_all(copies, axis, 0, 0, tiled=False).reshape((-1,) + x.shape[1:])  17.9 us
    all_to_all x2, waiting for transfers between devices, gather_rows(): lax.all_to_all(copies, axis, 0, 0, tiled=False).reshape((-1,) + x.shape[1:])  16.1 us
    all_to_all x2, starting transfers between devices, gather_rows(): lax.all_to_all(copies, axis, 0, 0, tiled=False).reshape((-1,) + x.shape[1:])  10.9 us
    dot_general x2, matrix products, contract_rows(): lax.dot_general(left, right, (((0,), (0,)), ((), ())), precision=lax.Prec...  5.21 us
    broadcast_in_dim x3, local copies, waits for them, and re-layouts, gather_rows(): copies = jnp.broadcast_to(x[None], (n,) + x.shape)  3.66 us
  transfers between devices with their start and end apart: 2, of which 1 were waited for; matrix products, arithmetic and copies ran while one was open for 30% of the time, Pallas kernels for 0%

profile of v10, /device:TPU:0, one launch (start us, length us, event | category | flops | bytes accessed | tf_op | source)
XLA Modules:
  0.0 112.9 jit_solution(14981011024677649975)
XLA Ops:
  0.0 0.0 copy-start
  0.0 0.0 copy-start.4
  0.0 2.0 %broadcast_in_dim.8 = bf16[16,64,512]{2,1,0:T(8,128)(2,1)} broadcast(bf16[64,512]{1,0:T(8,128)(2,1)} %param.8), dimensions={1,2} | broadcast | bytes 1114112 | tf_op jit(solution)/shard_map/broadcast_in_dim | solution.py:63
  2.0 7.1 %all-to-all-start = ((bf16[16,64,512]{2,1,0:T(8,128)(2,1)}), bf16[16,64,512]{2,1,0:T(8,128)(2,1)S(1)}, u32[]{:S(2)}, u32[]{:S(2)}) async-start(bf16[16,64,512]{2,1,0:T(8,128)(2,1)} %broadcast_in_dim.8), calls=%async_computation | async-start | bytes 2097152 | tf_op jit(solution)/shard_map/all_to_all | solution.py:64
  9.2 1.5 %fusion.21 = f32[1024]{0:T(1024)S(1)} fusion(bf16[16384,512]{1,0:T(8,128)(2,1)} %param.7, s32[]{:T(128)S(6)} %select_n.60), kind=kLoop, calls=%fused_computation.34 | loop fusion | flops 1571840 | bytes 1052676 | tf_op jit(solution)/shard_map/nd,nd->n/dot_general | solution.py:89
  10.7 16.1 %all-to-all-done = bf16[16,64,512]{2,1,0:T(8,128)(2,1)S(1)} async-done(((bf16[16,64,512]{2,1,0:T(8,128)(2,1)}), bf16[16,64,512]{2,1,0:T(8,128)(2,1)S(1)}, u32[]{:S(2)}, u32[]{:S(2)}) %all-to-all-start) | async-done | bytes 1048608 | tf_op jit(solution)/shard_map/all_to_all | solution.py:64
  26.8 0.0 copy-done.4
  26.8 0.0 copy-start.1
  26.8 1.6 %broadcast_in_dim.9 = f32[16,256,128]{2,1,0:T(8,128)} broadcast(f32[256,128]{1,0:T(8,128)S(1)} %copy-done.4), dimensions={1,2} | broadcast | bytes 2228224 | tf_op jit(solution)/shard_map/broadcast_in_dim | solution.py:63
  28.5 0.0 copy-done.1
  28.5 3.7 %all-to-all-start.1 = ((f32[16,256,128]{2,1,0:T(8,128)}), f32[16,256,128]{2,1,0:T(8,128)S(1)}, u32[]{:S(2)}, u32[]{:S(2)}) async-start(f32[16,256,128]{2,1,0:T(8,128)} %broadcast_in_dim.9), calls=%async_computation.1 | async-start | bytes 4194304 | tf_op jit(solution)/shard_map/all_to_all | solution.py:64
  32.2 1.5 %fusion.22 = f32[1024]{0:T(1024)S(1)} fusion(bf16[16,64,512]{2,1,0:T(8,128)(2,1)} %copy-done.1), kind=kLoop, calls=%fused_computation.36 | loop fusion | flops 1571840 | bytes 1052672 | tf_op jit(solution)/shard_map/pd,pd->p/dot_general | solution.py:34
  33.7 0.0 copy-start.5
  33.7 0.0 copy-start.3
  33.7 30.3 %fusion.15 = f32[1024,1024]{0,1:T(8,128)} fusion(bf16[1024,512]{1,0:T(8,128)(2,1)} %bitcast.33, f32[1024]{0:T(1024)S(1)} %get-tuple-element.21, f32[1024]{0:T(1024)S(1)} %get-tuple-element.13, f32[1024]{0:T(1024)S(1)} %get-tuple-element.20, f32[1024]{0:T(1024)S(1)} %get-tuple-element.12, f32[1024]{0:T(1024)S(1)} %get-tuple-element.19, ...), kind=kOutput, calls=%fused_computation.19 | convolution fusion | flops 1218445312 | bytes 6356996 | tf_op jit(solution)/shard_map/dot_general | solution.py:33
  64.0 0.0 all-to-all-done.1
  64.0 0.0 copy-done
  64.0 0.0 copy-done.5
  64.1 0.8 fusion.23
  64.8 0.0 copy-done.3
  64.8 0.0 copy-start.2
  64.8 0.4 convolution_bitcast_fusion
  65.3 0.2 copy.10
  65.5 24.6 %all_to_all.20 = f32[128,8,128]{2,1,0:T(8,128)S(1)} all-to-all(f32[128,8,128]{2,1,0:T(8,128)S(1)} %bitcast.34), channel_id=1, replica_groups=mesh['pr'=8,'pc'=16] {'pr','pc'}, dimensions={0} | all-to-all | bytes 1048576 | tf_op jit(solution)/shard_map/all_to_all | solution.py:68
  90.0 0.1 reduce_sum.9
  90.2 17.9 %all_to_all.21 = f32[128,8,128]{2,1,0:T(8,128)S(1)} all-to-all(f32[128,8,128]{2,1,0:T(8,128)S(1)} %broadcast_in_dim.11), channel_id=1, replica_groups=mesh['pr'=8,'pc'=16] {'pr','pc'}, dimensions={0} | all-to-all | bytes 1048576 | tf_op jit(solution)/shard_map/all_to_all | solution.py:64
  108.1 0.0 copy-done.2
  108.1 4.8 %convolution_add_fusion = f32[1024,128]{1,0:T(8,128)} fusion(f32[1024,128]{1,0:T(8,128)S(1)} %copy-done.2, f32[1024,1024]{0,1:T(8,128)} %fusion.15, f32[128,8,128]{2,1,0:T(8,128)S(1)} %all_to_all.21), kind=kOutput, calls=%fused_computation.37 | convolution fusion | flops 805437440 | bytes 5767168 | tf_op jit(solution)/shard_map/dot_general | solution.py:53
  (3 shorter events, 0.1 us)
Async XLA Ops:
  0.0 64.0 %copy-start = (f32[64,4096]{1,0:T(8,128)S(1)}, f32[64,4096]{1,0:T(8,128)}, u32[]{:S(2)}) copy-start(f32[64,4096]{1,0:T(8,128)} %param.9) | copy-start | bytes 3145732
  0.0 26.8 %copy-start.4 = (f32[256,128]{1,0:T(8,128)S(1)}, f32[256,128]{1,0:T(8,128)}, u32[]{:S(2)}) copy-start(f32[256,128]{1,0:T(8,128)} %param.10) | copy-start | bytes 393220
  2.0 24.8 %all-to-all-start = ((bf16[16,64,512]{2,1,0:T(8,128)(2,1)}), bf16[16,64,512]{2,1,0:T(8,128)(2,1)S(1)}, u32[]{:S(2)}, u32[]{:S(2)}) async-start(bf16[16,64,512]{2,1,0:T(8,128)(2,1)} %broadcast_in_dim.8), calls=%async_computation | async-start | bytes 2097152 | tf_op jit(solution)/shard_map/all_to_all | solution.py:64
  26.8 1.6 %copy-start.1 = (bf16[16,64,512]{2,1,0:T(8,128)(2,1)}, bf16[16,64,512]{2,1,0:T(8,128)(2,1)S(1)}, u32[]{:S(2)}) copy-start(bf16[16,64,512]{2,1,0:T(8,128)(2,1)S(1)} %all-to-all-done) | copy-start | bytes 3145732
  28.5 35.6 %all-to-all-start.1 = ((f32[16,256,128]{2,1,0:T(8,128)}), f32[16,256,128]{2,1,0:T(8,128)S(1)}, u32[]{:S(2)}, u32[]{:S(2)}) async-start(f32[16,256,128]{2,1,0:T(8,128)} %broadcast_in_dim.9), calls=%async_computation.1 | async-start | bytes 4194304 | tf_op jit(solution)/shard_map/all_to_all | solution.py:64
  33.7 30.3 %copy-start.5 = (f32[64,128]{1,0:T(8,128)S(1)}, f32[64,128]{1,0:T(8,128)}, u32[]{:S(2)}) copy-start(f32[64,128]{1,0:T(8,128)} %param.11) | copy-start | bytes 98308
  33.7 31.1 %copy-start.3 = (f32[64,1024]{1,0:T(8,128)S(1)}, f32[64,1024]{1,0:T(8,128)}, u32[]{:S(2)}) copy-start(f32[64,1024]{1,0:T(8,128)} %param.12) | copy-start | bytes 786436
  64.8 43.3 %copy-start.2 = (f32[1024,128]{1,0:T(8,128)S(1)}, f32[1024,128]{1,0:T(8,128)}, u32[]{:S(2)}) copy-start(f32[1024,128]{1,0:T(8,128)} %param.13) | copy-start | bytes 1572868

commit v11 on v7

--- a/solution.py
+++ b/solution.py
@@ -89,9 +89,10 @@
     test_norms = jnp.einsum(
         "nd,nd->n", test_own, test_own, preferred_element_type=jnp.float32
     )
-    kern = arc_kernel(panel_all, test_own, test_norms)
+    split = rows - rows // 8
+    kern_a = arc_kernel(panel_all, test_own[:split], test_norms[:split])
     gathered = gather_rows(alpha_below, "pc", n_pc)
-    kern, gathered = lax.optimization_barrier((kern, gathered))
+    kern_a, gathered = lax.optimization_barrier((kern_a, gathered))
     partial_sum = jnp.dot(
         factor_rows,
         gathered,
@@ -100,8 +101,15 @@
     )
     carried = butterfly_sum(partial_sum, "pr", n_pr)
     residual = targets - carried
-    alpha_panel = sum_rows(contract_rows(inverse_block, residual), "pc", n_pc)
-    update = contract_rows(kern, alpha_panel)
+    spread_alpha = contract_rows(inverse_block, residual)
+    spread_alpha, panel_late = lax.optimization_barrier((spread_alpha, panel_all))
+    blocks = lax.all_to_all(
+        spread_alpha.reshape((n_pc, -1) + spread_alpha.shape[1:]), "pc", 0, 0, tiled=False
+    )
+    kern_b = arc_kernel(panel_late, test_own[split:], test_norms[split:])
+    kern_b, blocks = lax.optimization_barrier((kern_b, blocks))
+    alpha_panel = gather_rows(blocks.sum(0), "pc", n_pc)
+    update = contract_rows(jnp.concatenate([kern_a, kern_b], axis=1), alpha_panel)
     return predictions_in + update
 
 

time: 112 us -> 111 us (level)
  blocking collectives: 30.2 us -> 13.1 us
  waiting for transfers between devices: 21.2 us -> 27.7 us
  starting transfers between devices: 16.8 us -> 22.8 us
  matrix products: 36.3 us -> 39.6 us
    all_to_all x1 -> x0, blocking collectives: 17.1 us -> none  [sum_rows(): lax.all_to_all(x.reshape((n, -1) + x.shape[1:]), axis, 0, 0, tiled=False)]
    all_to_all x0 -> x1, starting transfers between devices: none -> 5.3 us  [body(): lax.all_to_all(spread_alpha.reshape((n_pc, -1) + spread_alpha.shape[1:]),...]
    all_to_all x0 -> x1, waiting for transfers between devices: none -> 4.63 us  [body(): lax.all_to_all(spread_alpha.reshape((n_pc, -1) + spread_alpha.shape[1:]),...]
    all_to_all x2, waiting for transfers between devices: 16.1 us -> 18 us  [gather_rows(): lax.all_to_all(copies, axis, 0, 0, tiled=False).reshape((-1,) + x.shape[1:])]
    dot_general x1 -> x2, matrix products: 30.3 us -> 32 us  [arc_kernel(): cross = jnp.dot(panel, test.T, preferred_element_type=jnp.float32) / width]
    dot_general x1, matrix products: 0.75 us -> 2.34 us  [body(): jnp.dot(factor_rows, gathered, precision=lax.Precision.HIGH, preferred_el...]
  transfers between devices with their start and end apart: 5 -> 6, of which waited for: 4 -> 6; matrix products, arithmetic and copies ran while one was open for 30% -> 31% of each run, Pallas kernels for 0% -> 0%
where the time goes in v11:
time: 111 us; the launch traced here: 110 us
  matrix products  39.6 us (36%)
  waiting for transfers between devices  27.7 us (25%)
  starting transfers between devices  22.8 us (21%)
  blocking collectives  13.1 us (12%)
  local copies, waits for them, and re-layouts  4.59 us (4%)
  other arithmetic  2.16 us (2%)
    dot_general x2, matrix products, arc_kernel(): cross = jnp.dot(panel, test.T, preferred_element_type=jnp.float32) / width  32 us
    all_to_all x2, waiting for transfers between devices, gather_rows(): lax.all_to_all(copies, axis, 0, 0, tiled=False).reshape((-1,) + x.shape[1:])  18 us
    all_to_all x1, blocking collectives, gather_rows(): lax.all_to_all(copies, axis, 0, 0, tiled=False).reshape((-1,) + x.shape[1:])  13.1 us
    all_to_all x2, starting transfers between devices, gather_rows(): lax.all_to_all(copies, axis, 0, 0, tiled=False).reshape((-1,) + x.shape[1:])  11.6 us
    ppermute x3, starting transfers between devices, butterfly_sum(): x = x + lax.ppermute(x, axis, [(i, i ^ step) for i in range(n)])  5.88 us
    all_to_all x1, starting transfers between devices, body(): lax.all_to_all(spread_alpha.reshape((n_pc, -1) + spread_alpha.shape[1:]),...  5.3 us
    dot_general x2, matrix products, contract_rows(): lax.dot_general(left, right, (((0,), (0,)), ((), ())), precision=lax.Prec...  5.23 us
    ppermute x3, waiting for transfers between devices, butterfly_sum(): x = x + lax.ppermute(x, axis, [(i, i ^ step) for i in range(n)])  5.06 us
  transfers between devices with their start and end apart: 6, of which 6 were waited for; matrix products, arithmetic and copies ran while one was open for 31% of the time, Pallas kernels for 0%

profile of v11, /device:TPU:0, one launch (start us, length us, event | category | flops | bytes accessed | tf_op | source)
XLA Modules:
  0.0 110.0 jit_solution(11134789214720708057)
XLA Ops:
  0.0 0.0 copy-start
  0.0 0.0 copy-start.3
  0.0 2.0 %broadcast_in_dim.6 = bf16[16,64,512]{2,1,0:T(8,128)(2,1)} broadcast(bf16[64,512]{1,0:T(8,128)(2,1)} %param.8), dimensions={1,2} | broadcast | bytes 1114112 | tf_op jit(solution)/shard_map/broadcast_in_dim | solution.py:63
  2.0 7.1 %all-to-all-start = ((bf16[16,64,512]{2,1,0:T(8,128)(2,1)}), bf16[16,64,512]{2,1,0:T(8,128)(2,1)S(1)}, u32[]{:S(2)}, u32[]{:S(2)}) async-start(bf16[16,64,512]{2,1,0:T(8,128)(2,1)} %broadcast_in_dim.6), calls=%async_computation | async-start | bytes 2097152 | tf_op jit(solution)/shard_map/all_to_all | solution.py:64
  9.2 1.5 %fusion.26 = f32[1024]{0:T(1024)S(1)} fusion(bf16[16384,512]{1,0:T(8,128)(2,1)} %param.7, s32[]{:T(128)S(6)} %select_n.101), kind=kLoop, calls=%fused_computation.40 | loop fusion | flops 1571840 | bytes 1052676 | tf_op jit(solution)/shard_map/nd,nd->n/dot_general | solution.py:89
  10.7 16.1 %all-to-all-done = bf16[16,64,512]{2,1,0:T(8,128)(2,1)S(1)} async-done(((bf16[16,64,512]{2,1,0:T(8,128)(2,1)}), bf16[16,64,512]{2,1,0:T(8,128)(2,1)S(1)}, u32[]{:S(2)}, u32[]{:S(2)}) %all-to-all-start) | async-done | bytes 1048608 | tf_op jit(solution)/shard_map/all_to_all | solution.py:64
  26.8 0.0 copy-done.3
  26.8 1.5 %broadcast_in_dim.7 = f32[16,256,128]{2,1,0:T(8,128)} broadcast(f32[256,128]{1,0:T(8,128)S(1)} %copy-done.3), dimensions={1,2} | broadcast | bytes 2228224 | tf_op jit(solution)/shard_map/broadcast_in_dim | solution.py:63
  28.4 4.4 %all-to-all-start.1 = ((f32[16,256,128]{2,1,0:T(8,128)}), f32[16,256,128]{2,1,0:T(8,128)}, u32[]{:S(2)}, u32[]{:S(2)}) async-start(f32[16,256,128]{2,1,0:T(8,128)} %broadcast_in_dim.7), calls=%async_computation.1 | async-start | bytes 4194304 | tf_op jit(solution)/shard_map/all_to_all | solution.py:64
  32.8 0.3 fusion.27
  33.1 0.0 copy-start.2
  33.1 0.0 copy-start.4
  33.1 26.6 %fusion.19 = f32[1024,896]{0,1:T(8,128)} fusion(bf16[1024,512]{1,0:T(8,128)(2,1)S(1)} %bitcast.28, f32[896]{0:T(1024)S(1)} %get-tuple-element.45, f32[1024]{0:T(1024)S(1)} %get-tuple-element.37, f32[896]{0:T(1024)S(1)} %get-tuple-element.44, f32[1024]{0:T(1024)S(1)} %get-tuple-element.36, f32[896]{0:T(1024)S(1)} %get-tuple-element.43, ...), kind=kOutput, calls=%fused_computation.23 | convolution fusion | flops 1066139648 | bytes 5697540 | tf_op jit(solution)/shard_map/dot_general | solution.py:33
  59.7 1.8 %all-to-all-done.1 = f32[16,256,128]{2,1,0:T(8,128)} async-done(((f32[16,256,128]{2,1,0:T(8,128)}), f32[16,256,128]{2,1,0:T(8,128)}, u32[]{:S(2)}, u32[]{:S(2)}) %all-to-all-start.1) | async-done | bytes 2097184 | tf_op jit(solution)/shard_map/all_to_all | solution.py:64
  61.6 0.0 copy-done
  61.6 2.3 %convolution_bitcast_fusion.1 = f32[64,128]{1,0:T(8,128)S(1)} fusion(f32[4096,128]{1,0:T(8,128)} %bitcast.2, f32[64,4096]{1,0:T(8,128)S(1)} %copy-done), kind=kOutput, calls=%fused_computation.47 | convolution fusion | flops 201326592 | bytes 3178496 | tf_op jit(solution)/shard_map/dot_general | solution.py:96
  63.9 0.1 collective-permute-start
  64.0 1.2 %collective-permute-done = f32[64,128]{1,0:T(8,128)S(1)} collective-permute-done((f32[64,128]{1,0:T(8,128)S(1)}, f32[64,128]{1,0:T(8,128)S(1)}, u32[]{:S(2)}, u32[]{:S(2)}) %collective-permute-start) | collective-permute-done | bytes 32800 | tf_op jit(solution)/shard_map/ppermute | solution.py:75
  65.2 1.9 %collective-permute-start.1 = (f32[64,128]{1,0:T(8,128)S(1)}, f32[64,128]{1,0:T(8,128)S(1)}, u32[]{:S(2)}, u32[]{:S(2)}) collective-permute-start(f32[64,128]{1,0:T(8,128)S(1)} %add.335), channel_id=1, source_target_pairs={{0,32},{16,48},{32,0},{48,16},{64,96},{80,112},{96,64},{112,80},{1... | collective-permute-start | bytes 98312 | tf_op jit(solution)/shard_map/ppermute | solution.py:75
  67.1 2.0 %collective-permute-done.1 = f32[64,128]{1,0:T(8,128)S(1)} collective-permute-done((f32[64,128]{1,0:T(8,128)S(1)}, f32[64,128]{1,0:T(8,128)S(1)}, u32[]{:S(2)}, u32[]{:S(2)}) %collective-permute-start.1) | collective-permute-done | bytes 32800 | tf_op jit(solution)/shard_map/ppermute | solution.py:75
  69.1 3.9 %collective-permute-start.2 = (f32[64,128]{1,0:T(8,128)S(1)}, f32[64,128]{1,0:T(8,128)S(1)}, u32[]{:S(2)}, u32[]{:S(2)}) collective-permute-start(f32[64,128]{1,0:T(8,128)S(1)} %add.336), channel_id=1, source_target_pairs={{0,64},{16,80},{32,96},{48,112},{64,0},{80,16},{96,32},{112,48},{1... | collective-permute-start | bytes 98312 | tf_op jit(solution)/shard_map/ppermute | solution.py:75
  73.0 1.9 %collective-permute-done.2 = f32[64,128]{1,0:T(8,128)S(1)} collective-permute-done((f32[64,128]{1,0:T(8,128)S(1)}, f32[64,128]{1,0:T(8,128)S(1)}, u32[]{:S(2)}, u32[]{:S(2)}) %collective-permute-start.2) | collective-permute-done | bytes 32800 | tf_op jit(solution)/shard_map/ppermute | solution.py:75
  74.9 0.0 copy-done.2
  74.9 0.0 copy-done.4
  74.9 0.4 convolution_bitcast_fusion
  75.3 1.0 copy.10
  76.3 0.3 fusion.25
  76.6 5.3 %all-to-all-start.2 = ((f32[16,64,128]{2,1,0:T(8,128)}), f32[16,64,128]{2,1,0:T(8,128)S(1)}, u32[]{:S(2)}, u32[]{:S(2)}) async-start(f32[16,64,128]{2,1,0:T(8,128)} %bitcast.5), calls=%async_computation.2 | async-start | bytes 1048576 | tf_op jit(solution)/shard_map/all_to_all | solution.py:106
  81.9 0.0 copy-start.1
  81.9 5.4 %fusion.48 = f32[1024,128]{0,1:T(8,128)} fusion(bf16[1024,512]{1,0:T(8,128)(2,1)S(1)} %bitcast.30, f32[128]{0:T(128)S(1)} %get-tuple-element.29, f32[1024]{0:T(1024)S(1)} %get-tuple-element.21, f32[128]{0:T(128)S(1)} %get-tuple-element.30, f32[1024]{0:T(1024)S(1)} %get-tuple-element.20, f32[128]{0:T(128)S(1)} %get-tuple-element.31, ...), kind=kOutput, calls=%fused_computation.68 | convolution fusion | flops 152305664 | bytes 1740804 | tf_op jit(solution)/shard_map/dot_general | solution.py:33
  87.3 4.6 %all-to-all-done.2 = f32[16,64,128]{2,1,0:T(8,128)S(1)} async-done(((f32[16,64,128]{2,1,0:T(8,128)}), f32[16,64,128]{2,1,0:T(8,128)S(1)}, u32[]{:S(2)}, u32[]{:S(2)}) %all-to-all-start.2) | async-done | bytes 524320 | tf_op jit(solution)/shard_map/all_to_all | solution.py:106
  92.1 13.1 %all_to_all.20 = f32[16,64,128]{2,1,0:T(8,128)S(1)} all-to-all(f32[16,64,128]{2,1,0:T(8,128)S(1)} %broadcast_in_dim.8), channel_id=1, replica_groups=mesh['pr'=8,'pc'=16] {'pc'}, dimensions={0} | all-to-all | bytes 1048576 | tf_op jit(solution)/shard_map/all_to_all | solution.py:64
  105.2 0.0 copy-done.1
  105.2 4.8 %fusion.29 = f32[1024,128]{1,0:T(8,128)} fusion(f32[1024,128]{1,0:T(8,128)S(1)} %copy-done.1, f32[1024,128]{1,0:T(8,128)S(1)} %bitcast.31, f32[1024,128]{0,1:T(8,128)} %fusion.48, f32[1024,896]{0,1:T(8,128)} %fusion.19), kind=kOutput, calls=%fused_computation.46 | convolution fusion | flops 806486016 | bytes 5767168 | tf_op jit(solution)/shard_map/dot_general | solution.py:53
  (8 shorter events, 0.2 us)
Async XLA Ops:
  0.0 61.6 %copy-start = (f32[64,4096]{1,0:T(8,128)S(1)}, f32[64,4096]{1,0:T(8,128)}, u32[]{:S(2)}) copy-start(f32[64,4096]{1,0:T(8,128)} %param.9) | copy-start | bytes 3145732
  0.0 26.8 %copy-start.3 = (f32[256,128]{1,0:T(8,128)S(1)}, f32[256,128]{1,0:T(8,128)}, u32[]{:S(2)}) copy-start(f32[256,128]{1,0:T(8,128)} %param.10) | copy-start | bytes 393220
  2.0 24.8 %all-to-all-start = ((bf16[16,64,512]{2,1,0:T(8,128)(2,1)}), bf16[16,64,512]{2,1,0:T(8,128)(2,1)S(1)}, u32[]{:S(2)}, u32[]{:S(2)}) async-start(bf16[16,64,512]{2,1,0:T(8,128)(2,1)} %broadcast_in_dim.6), calls=%async_computation | async-start | bytes 2097152 | tf_op jit(solution)/shard_map/all_to_all | solution.py:64
  28.4 33.2 %all-to-all-start.1 = ((f32[16,256,128]{2,1,0:T(8,128)}), f32[16,256,128]{2,1,0:T(8,128)}, u32[]{:S(2)}, u32[]{:S(2)}) async-start(f32[16,256,128]{2,1,0:T(8,128)} %broadcast_in_dim.7), calls=%async_computation.1 | async-start | bytes 4194304 | tf_op jit(solution)/shard_map/all_to_all | solution.py:64
  33.1 41.8 %copy-start.2 = (f32[64,1024]{1,0:T(8,128)S(1)}, f32[64,1024]{1,0:T(8,128)}, u32[]{:S(2)}) copy-start(f32[64,1024]{1,0:T(8,128)} %param.12) | copy-start | bytes 786436
  33.1 41.8 %copy-start.4 = (f32[64,128]{1,0:T(8,128)S(1)}, f32[64,128]{1,0:T(8,128)}, u32[]{:S(2)}) copy-start(f32[64,128]{1,0:T(8,128)} %param.11) | copy-start | bytes 98308
  63.9 1.3 %collective-permute-start = (f32[64,128]{1,0:T(8,128)S(1)}, f32[64,128]{1,0:T(8,128)S(1)}, u32[]{:S(2)}, u32[]{:S(2)}) collective-permute-start(f32[64,128]{1,0:T(8,128)S(1)} %convolution_bitcast_fusion.1), channel_id=1, source_target_pairs={{0,16},{16,0},{32,48},{48,32},{64,80},{80,64},{96,112},{112,96},{1... | collective-permute-start | bytes 98312 | tf_op jit(solution)/shard_map/ppermute | solution.py:75
  65.2 3.9 %collective-permute-start.1 = (f32[64,128]{1,0:T(8,128)S(1)}, f32[64,128]{1,0:T(8,128)S(1)}, u32[]{:S(2)}, u32[]{:S(2)}) collective-permute-start(f32[64,128]{1,0:T(8,128)S(1)} %add.335), channel_id=1, source_target_pairs={{0,32},{16,48},{32,0},{48,16},{64,96},{80,112},{96,64},{112,80},{1... | collective-permute-start | bytes 98312 | tf_op jit(solution)/shard_map/ppermute | solution.py:75
  69.1 5.8 %collective-permute-start.2 = (f32[64,128]{1,0:T(8,128)S(1)}, f32[64,128]{1,0:T(8,128)S(1)}, u32[]{:S(2)}, u32[]{:S(2)}) collective-permute-start(f32[64,128]{1,0:T(8,128)S(1)} %add.336), channel_id=1, source_target_pairs={{0,64},{16,80},{32,96},{48,112},{64,0},{80,16},{96,32},{112,48},{1... | collective-permute-start | bytes 98312 | tf_op jit(solution)/shard_map/ppermute | solution.py:75
  76.6 15.4 %all-to-all-start.2 = ((f32[16,64,128]{2,1,0:T(8,128)}), f32[16,64,128]{2,1,0:T(8,128)S(1)}, u32[]{:S(2)}, u32[]{:S(2)}) async-start(f32[16,64,128]{2,1,0:T(8,128)} %bitcast.5), calls=%async_computation.2 | async-start | bytes 1048576 | tf_op jit(solution)/shard_map/all_to_all | solution.py:106
  81.9 23.3 %copy-start.1 = (f32[1024,128]{1,0:T(8,128)S(1)}, f32[1024,128]{1,0:T(8,128)}, u32[]{:S(2)}) copy-start(f32[1024,128]{1,0:T(8,128)} %param.13) | copy-start | bytes 1572868

commit v12 on v11

--- a/solution.py
+++ b/solution.py
@@ -89,6 +89,8 @@
     test_norms = jnp.einsum(
         "nd,nd->n", test_own, test_own, preferred_element_type=jnp.float32
     )
+    inverse_t = jnp.transpose(inverse_block)
+    inverse_t, alpha_below = lax.optimization_barrier((inverse_t, alpha_below))
     split = rows - rows // 8
     kern_a = arc_kernel(panel_all, test_own[:split], test_norms[:split])
     gathered = gather_rows(alpha_below, "pc", n_pc)
@@ -101,7 +103,9 @@
     )
     carried = butterfly_sum(partial_sum, "pr", n_pr)
     residual = targets - carried
-    spread_alpha = contract_rows(inverse_block, residual)
+    spread_alpha = jnp.dot(
+        inverse_t, residual, precision=lax.Precision.HIGH, preferred_element_type=jnp.float32
+    )
     spread_alpha, panel_late = lax.optimization_barrier((spread_alpha, panel_all))
     blocks = lax.all_to_all(
         spread_alpha.reshape((n_pc, -1) + spread_alpha.shape[1:]), "pc", 0, 0, tiled=False

time: 111 us -> 111 us (level)
    dot_general x0 -> x1, matrix products: none -> 1.39 us  [body(): jnp.dot(inverse_t, residual, precision=lax.Precision.HIGH, preferred_elem...]
    dot_general x2 -> x1, matrix products: 5.23 us -> 4.81 us  [contract_rows(): lax.dot_general(left, right, (((0,), (0,)), ((), ())), precision=lax.Prec...]
where the time goes in v12:
time: 111 us; the launch traced here: 110 us
  matrix products  40.6 us (37%)
  waiting for transfers between devices  27.7 us (25%)
  starting transfers between devices  22.8 us (21%)
  blocking collectives  13.1 us (12%)
  local copies, waits for them, and re-layouts  3.6 us (3%)
  other arithmetic  2.16 us (2%)
    dot_general x2, matrix products, arc_kernel(): cross = jnp.dot(panel, test.T, preferred_element_type=jnp.float32) / width  32 us
    all_to_all x2, waiting for transfers between devices, gather_rows(): lax.all_to_all(copies, axis, 0, 0, tiled=False).reshape((-1,) + x.shape[1:])  18 us
    all_to_all x1, blocking collectives, gather_rows(): lax.all_to_all(copies, axis, 0, 0, tiled=False).reshape((-1,) + x.shape[1:])  13.1 us
    all_to_all x2, starting transfers between devices, gather_rows(): lax.all_to_all(copies, axis, 0, 0, tiled=False).reshape((-1,) + x.shape[1:])  11.6 us
    ppermute x3, starting transfers between devices, butterfly_sum(): x = x + lax.ppermute(x, axis, [(i, i ^ step) for i in range(n)])  5.88 us
    all_to_all x1, starting transfers between devices, body(): lax.all_to_all(spread_alpha.reshape((n_pc, -1) + spread_alpha.shape[1:]),...  5.3 us
    ppermute x3, waiting for transfers between devices, butterfly_sum(): x = x + lax.ppermute(x, axis, [(i, i ^ step) for i in range(n)])  5.06 us
    dot_general x1, matrix products, contract_rows(): lax.dot_general(left, right, (((0,), (0,)), ((), ())), precision=lax.Prec...  4.81 us
  transfers between devices with their start and end apart: 6, of which 6 were waited for; matrix products, arithmetic and copies ran while one was open for 31% of the time, Pallas kernels for 0%

profile of v12, /device:TPU:0, one launch (start us, length us, event | category | flops | bytes accessed | tf_op | source)
XLA Modules:
  0.0 110.0 jit_solution(16362464588068967999)
XLA Ops:
  0.0 0.0 copy-start
  0.0 0.0 copy-start.3
  0.0 2.0 %broadcast_in_dim.6 = bf16[16,64,512]{2,1,0:T(8,128)(2,1)} broadcast(bf16[64,512]{1,0:T(8,128)(2,1)} %param.8), dimensions={1,2} | broadcast | bytes 1114112 | tf_op jit(solution)/shard_map/broadcast_in_dim | solution.py:63
  2.0 7.1 %all-to-all-start = ((bf16[16,64,512]{2,1,0:T(8,128)(2,1)}), bf16[16,64,512]{2,1,0:T(8,128)(2,1)S(1)}, u32[]{:S(2)}, u32[]{:S(2)}) async-start(bf16[16,64,512]{2,1,0:T(8,128)(2,1)} %broadcast_in_dim.6), calls=%async_computation | async-start | bytes 2097152 | tf_op jit(solution)/shard_map/all_to_all | solution.py:64
  9.2 1.5 %fusion.26 = f32[1024]{0:T(1024)S(1)} fusion(bf16[16384,512]{1,0:T(8,128)(2,1)} %param.7, s32[]{:T(128)S(6)} %select_n.101), kind=kLoop, calls=%fused_computation.40 | loop fusion | flops 1571840 | bytes 1052676 | tf_op jit(solution)/shard_map/nd,nd->n/dot_general | solution.py:89
  10.7 16.1 %all-to-all-done = bf16[16,64,512]{2,1,0:T(8,128)(2,1)S(1)} async-done(((bf16[16,64,512]{2,1,0:T(8,128)(2,1)}), bf16[16,64,512]{2,1,0:T(8,128)(2,1)S(1)}, u32[]{:S(2)}, u32[]{:S(2)}) %all-to-all-start) | async-done | bytes 1048608 | tf_op jit(solution)/shard_map/all_to_all | solution.py:64
  26.8 0.0 copy-done.3
  26.8 1.5 %broadcast_in_dim.7 = f32[16,256,128]{2,1,0:T(8,128)} broadcast(f32[256,128]{1,0:T(8,128)S(1)} %copy-done.3), dimensions={1,2} | broadcast | bytes 2228224 | tf_op jit(solution)/shard_map/broadcast_in_dim | solution.py:63
  28.4 4.4 %all-to-all-start.1 = ((f32[16,256,128]{2,1,0:T(8,128)}), f32[16,256,128]{2,1,0:T(8,128)}, u32[]{:S(2)}, u32[]{:S(2)}) async-start(f32[16,256,128]{2,1,0:T(8,128)} %broadcast_in_dim.7), calls=%async_computation.1 | async-start | bytes 4194304 | tf_op jit(solution)/shard_map/all_to_all | solution.py:64
  32.8 0.3 fusion.27
  33.1 0.0 copy-start.2
  33.1 0.0 copy-start.4
  33.1 26.6 %fusion.19 = f32[1024,896]{0,1:T(8,128)} fusion(bf16[1024,512]{1,0:T(8,128)(2,1)S(1)} %bitcast.27, f32[896]{0:T(1024)S(1)} %get-tuple-element.49, f32[1024]{0:T(1024)S(1)} %get-tuple-element.41, f32[896]{0:T(1024)S(1)} %get-tuple-element.48, f32[1024]{0:T(1024)S(1)} %get-tuple-element.40, f32[896]{0:T(1024)S(1)} %get-tuple-element.47, ...), kind=kOutput, calls=%fused_computation.23 | convolution fusion | flops 1066139648 | bytes 5697540 | tf_op jit(solution)/shard_map/dot_general | solution.py:33
  59.7 1.8 %all-to-all-done.1 = f32[16,256,128]{2,1,0:T(8,128)} async-done(((f32[16,256,128]{2,1,0:T(8,128)}), f32[16,256,128]{2,1,0:T(8,128)}, u32[]{:S(2)}, u32[]{:S(2)}) %all-to-all-start.1) | async-done | bytes 2097184 | tf_op jit(solution)/shard_map/all_to_all | solution.py:64
  61.6 0.0 copy-done
  61.6 2.3 %convolution_bitcast_fusion = f32[64,128]{1,0:T(8,128)S(1)} fusion(f32[4096,128]{1,0:T(8,128)} %bitcast.3, f32[64,4096]{1,0:T(8,128)S(1)} %copy-done), kind=kOutput, calls=%fused_computation.46 | convolution fusion | flops 201326592 | bytes 3178496 | tf_op jit(solution)/shard_map/dot_general | solution.py:98
  63.9 0.1 collective-permute-start
  64.0 1.2 %collective-permute-done = f32[64,128]{1,0:T(8,128)S(1)} collective-permute-done((f32[64,128]{1,0:T(8,128)S(1)}, f32[64,128]{1,0:T(8,128)S(1)}, u32[]{:S(2)}, u32[]{:S(2)}) %collective-permute-start) | collective-permute-done | bytes 32800 | tf_op jit(solution)/shard_map/ppermute | solution.py:75
  65.2 1.9 %collective-permute-start.1 = (f32[64,128]{1,0:T(8,128)S(1)}, f32[64,128]{1,0:T(8,128)S(1)}, u32[]{:S(2)}, u32[]{:S(2)}) collective-permute-start(f32[64,128]{1,0:T(8,128)S(1)} %add.335), channel_id=1, source_target_pairs={{0,32},{16,48},{32,0},{48,16},{64,96},{80,112},{96,64},{112,80},{1... | collective-permute-start | bytes 98312 | tf_op jit(solution)/shard_map/ppermute | solution.py:75
  67.1 2.0 %collective-permute-done.1 = f32[64,128]{1,0:T(8,128)S(1)} collective-permute-done((f32[64,128]{1,0:T(8,128)S(1)}, f32[64,128]{1,0:T(8,128)S(1)}, u32[]{:S(2)}, u32[]{:S(2)}) %collective-permute-start.1) | collective-permute-done | bytes 32800 | tf_op jit(solution)/shard_map/ppermute | solution.py:75
  69.1 3.9 %collective-permute-start.2 = (f32[64,128]{1,0:T(8,128)S(1)}, f32[64,128]{1,0:T(8,128)S(1)}, u32[]{:S(2)}, u32[]{:S(2)}) collective-permute-start(f32[64,128]{1,0:T(8,128)S(1)} %add.336), channel_id=1, source_target_pairs={{0,64},{16,80},{32,96},{48,112},{64,0},{80,16},{96,32},{112,48},{1... | collective-permute-start | bytes 98312 | tf_op jit(solution)/shard_map/ppermute | solution.py:75
  73.0 1.9 %collective-permute-done.2 = f32[64,128]{1,0:T(8,128)S(1)} collective-permute-done((f32[64,128]{1,0:T(8,128)S(1)}, f32[64,128]{1,0:T(8,128)S(1)}, u32[]{:S(2)}, u32[]{:S(2)}) %collective-permute-start.2) | collective-permute-done | bytes 32800 | tf_op jit(solution)/shard_map/ppermute | solution.py:75
  74.9 0.0 copy-done.2
  74.9 0.0 copy-done.4
  74.9 1.4 %fusion.54 = f32[1024,128]{1,0:T(8,128)} fusion(f32[1024,64]{0,1:T(8,128)S(1)} %bitcast.31, f32[64,128]{1,0:T(8,128)S(1)} %copy-done.4, f32[64,128]{1,0:T(8,128)S(1)} %add.336, f32[64,128]{1,0:T(8,128)S(1)} %collective-permute-done.2), kind=kOutput, calls=%fused_computation.81 | convolution fusion | flops 50348032 | bytes 884736 | tf_op jit(solution)/shard_map/dot_general | solution.py:106
  76.3 0.3 fusion.25
  76.6 5.3 %all-to-all-start.2 = ((f32[16,64,128]{2,1,0:T(8,128)}), f32[16,64,128]{2,1,0:T(8,128)S(1)}, u32[]{:S(2)}, u32[]{:S(2)}) async-start(f32[16,64,128]{2,1,0:T(8,128)} %bitcast.5), calls=%async_computation.2 | async-start | bytes 1048576 | tf_op jit(solution)/shard_map/all_to_all | solution.py:110
  81.9 0.0 copy-start.1
  81.9 5.4 %fusion.48 = f32[1024,128]{0,1:T(8,128)} fusion(bf16[1024,512]{1,0:T(8,128)(2,1)S(1)} %bitcast.29, f32[128]{0:T(128)S(1)} %get-tuple-element.33, f32[1024]{0:T(1024)S(1)} %get-tuple-element.25, f32[128]{0:T(128)S(1)} %get-tuple-element.34, f32[1024]{0:T(1024)S(1)} %get-tuple-element.24, f32[128]{0:T(128)S(1)} %get-tuple-element.35, ...), kind=kOutput, calls=%fused_computation.67 | convolution fusion | flops 152305664 | bytes 1740804 | tf_op jit(solution)/shard_map/dot_general | solution.py:33
  87.3 4.6 %all-to-all-done.2 = f32[16,64,128]{2,1,0:T(8,128)S(1)} async-done(((f32[16,64,128]{2,1,0:T(8,128)}), f32[16,64,128]{2,1,0:T(8,128)S(1)}, u32[]{:S(2)}, u32[]{:S(2)}) %all-to-all-start.2) | async-done | bytes 524320 | tf_op jit(solution)/shard_map/all_to_all | solution.py:110
  92.0 13.1 %all_to_all.20 = f32[16,64,128]{2,1,0:T(8,128)S(1)} all-to-all(f32[16,64,128]{2,1,0:T(8,128)S(1)} %broadcast_in_dim.8), channel_id=1, replica_groups=mesh['pr'=8,'pc'=16] {'pc'}, dimensions={0} | all-to-all | bytes 1048576 | tf_op jit(solution)/shard_map/all_to_all | solution.py:64
  105.2 0.0 copy-done.1
  105.2 4.8 %fusion.29 = f32[1024,128]{1,0:T(8,128)} fusion(f32[1024,128]{1,0:T(8,128)S(1)} %copy-done.1, f32[1024,128]{1,0:T(8,128)S(1)} %bitcast.30, f32[1024,128]{0,1:T(8,128)} %fusion.48, f32[1024,896]{0,1:T(8,128)} %fusion.19), kind=kOutput, calls=%fused_computation.45 | convolution fusion | flops 806486016 | bytes 5767168 | tf_op jit(solution)/shard_map/dot_general | solution.py:53
  (8 shorter events, 0.2 us)
Async XLA Ops:
  0.0 61.6 %copy-start = (f32[64,4096]{1,0:T(8,128)S(1)}, f32[64,4096]{1,0:T(8,128)}, u32[]{:S(2)}) copy-start(f32[64,4096]{1,0:T(8,128)} %param.9) | copy-start | bytes 3145732
  0.0 26.8 %copy-start.3 = (f32[256,128]{1,0:T(8,128)S(1)}, f32[256,128]{1,0:T(8,128)}, u32[]{:S(2)}) copy-start(f32[256,128]{1,0:T(8,128)} %param.10) | copy-start | bytes 393220
  2.0 24.8 %all-to-all-start = ((bf16[16,64,512]{2,1,0:T(8,128)(2,1)}), bf16[16,64,512]{2,1,0:T(8,128)(2,1)S(1)}, u32[]{:S(2)}, u32[]{:S(2)}) async-start(bf16[16,64,512]{2,1,0:T(8,128)(2,1)} %broadcast_in_dim.6), calls=%async_computation | async-start | bytes 2097152 | tf_op jit(solution)/shard_map/all_to_all | solution.py:64
  28.4 33.2 %all-to-all-start.1 = ((f32[16,256,128]{2,1,0:T(8,128)}), f32[16,256,128]{2,1,0:T(8,128)}, u32[]{:S(2)}, u32[]{:S(2)}) async-start(f32[16,256,128]{2,1,0:T(8,128)} %broadcast_in_dim.7), calls=%async_computation.1 | async-start | bytes 4194304 | tf_op jit(solution)/shard_map/all_to_all | solution.py:64
  33.1 41.8 %copy-start.2 = (f32[64,1024]{1,0:T(8,128)S(1)}, f32[64,1024]{1,0:T(8,128)}, u32[]{:S(2)}) copy-start(f32[64,1024]{1,0:T(8,128)} %param.12) | copy-start | bytes 786436
  33.1 41.8 %copy-start.4 = (f32[64,128]{1,0:T(8,128)S(1)}, f32[64,128]{1,0:T(8,128)}, u32[]{:S(2)}) copy-start(f32[64,128]{1,0:T(8,128)} %param.11) | copy-start | bytes 98308
  63.9 1.3 %collective-permute-start = (f32[64,128]{1,0:T(8,128)S(1)}, f32[64,128]{1,0:T(8,128)S(1)}, u32[]{:S(2)}, u32[]{:S(2)}) collective-permute-start(f32[64,128]{1,0:T(8,128)S(1)} %convolution_bitcast_fusion), channel_id=1, source_target_pairs={{0,16},{16,0},{32,48},{48,32},{64,80},{80,64},{96,112},{112,96},{1... | collective-permute-start | bytes 98312 | tf_op jit(solution)/shard_map/ppermute | solution.py:75
  65.2 3.9 %collective-permute-start.1 = (f32[64,128]{1,0:T(8,128)S(1)}, f32[64,128]{1,0:T(8,128)S(1)}, u32[]{:S(2)}, u32[]{:S(2)}) collective-permute-start(f32[64,128]{1,0:T(8,128)S(1)} %add.335), channel_id=1, source_target_pairs={{0,32},{16,48},{32,0},{48,16},{64,96},{80,112},{96,64},{112,80},{1... | collective-permute-start | bytes 98312 | tf_op jit(solution)/shard_map/ppermute | solution.py:75
  69.1 5.8 %collective-permute-start.2 = (f32[64,128]{1,0:T(8,128)S(1)}, f32[64,128]{1,0:T(8,128)S(1)}, u32[]{:S(2)}, u32[]{:S(2)}) collective-permute-start(f32[64,128]{1,0:T(8,128)S(1)} %add.336), channel_id=1, source_target_pairs={{0,64},{16,80},{32,96},{48,112},{64,0},{80,16},{96,32},{112,48},{1... | collective-permute-start | bytes 98312 | tf_op jit(solution)/shard_map/ppermute | solution.py:75
  76.6 15.4 %all-to-all-start.2 = ((f32[16,64,128]{2,1,0:T(8,128)}), f32[16,64,128]{2,1,0:T(8,128)S(1)}, u32[]{:S(2)}, u32[]{:S(2)}) async-start(f32[16,64,128]{2,1,0:T(8,128)} %bitcast.5), calls=%async_computation.2 | async-start | bytes 1048576 | tf_op jit(solution)/shard_map/all_to_all | solution.py:110
  81.9 23.3 %copy-start.1 = (f32[1024,128]{1,0:T(8,128)S(1)}, f32[1024,128]{1,0:T(8,128)}, u32[]{:S(2)}) copy-start(f32[1024,128]{1,0:T(8,128)} %param.13) | copy-start | bytes 1572868

commit v13 on v12

--- a/solution.py
+++ b/solution.py
@@ -70,10 +70,10 @@
 
 
 def butterfly_sum(x, axis, n):
-    step = 1
-    while step < n:
+    step = n // 2
+    while step >= 1:
         x = x + lax.ppermute(x, axis, [(i, i ^ step) for i in range(n)])
-        step *= 2
+        step //= 2
     return x
 
 

time: 111 us -> 113 us (1.018)
  waiting for transfers between devices: 27.7 us -> 29.8 us
    all_to_all x1, waiting for transfers between devices: 4.63 us -> 6.4 us  [body(): lax.all_to_all(spread_alpha.reshape((n_pc, -1) + spread_alpha.shape[1:]),...]
  transfers between devices with their start and end apart: 6 -> 6, of which waited for: 6 -> 6; matrix products, arithmetic and copies ran while one was open for 31% -> 30% of each run, Pallas kernels for 0% -> 0%
where the time goes in v13:
time: 113 us
  matrix products  40.6 us (36%)
  waiting for transfers between devices  29.8 us (26%)
  starting transfers between devices  22.4 us (20%)
  blocking collectives  14 us (12%)
  local copies, waits for them, and re-layouts  3.6 us (3%)
  other arithmetic  2.16 us (2%)
    dot_general x2, matrix products, arc_kernel(): cross = jnp.dot(panel, test.T, preferred_element_type=jnp.float32) / width  32 us
    all_to_all x2, waiting for transfers between devices, gather_rows(): lax.all_to_all(copies, axis, 0, 0, tiled=False).reshape((-1,) + x.shape[1:])  18 us
    all_to_all x1, blocking collectives, gather_rows(): lax.all_to_all(copies, axis, 0, 0, tiled=False).reshape((-1,) + x.shape[1:])  14 us
    all_to_all x2, starting transfers between devices, gather_rows(): lax.all_to_all(copies, axis, 0, 0, tiled=False).reshape((-1,) + x.shape[1:])  11.6 us
    all_to_all x1, waiting for transfers between devices, body(): lax.all_to_all(spread_alpha.reshape((n_pc, -1) + spread_alpha.shape[1:]),...  6.4 us
    ppermute x3, starting transfers between devices, butterfly_sum(): x = x + lax.ppermute(x, axis, [(i, i ^ step) for i in range(n)])  5.52 us
    ppermute x3, waiting for transfers between devices, butterfly_sum(): x = x + lax.ppermute(x, axis, [(i, i ^ step) for i in range(n)])  5.42 us
    all_to_all x1, starting transfers between devices, body(): lax.all_to_all(spread_alpha.reshape((n_pc, -1) + spread_alpha.shape[1:]),...  5.3 us
  transfers between devices with their start and end apart: 6, of which 6 were waited for; matrix products, arithmetic and copies ran while one was open for 30% of the time, Pallas kernels for 0%

profile of v13, /device:TPU:0, one launch (start us, length us, event | category | flops | bytes accessed | tf_op | source)
XLA Modules:
  0.0 112.6 jit_solution(1100747809211764038)
XLA Ops:
  0.0 0.0 copy-start
  0.0 0.0 copy-start.3
  0.0 2.0 %broadcast_in_dim.6 = bf16[16,64,512]{2,1,0:T(8,128)(2,1)} broadcast(bf16[64,512]{1,0:T(8,128)(2,1)} %param.8), dimensions={1,2} | broadcast | bytes 1114112 | tf_op jit(solution)/shard_map/broadcast_in_dim | solution.py:63
  2.0 7.1 %all-to-all-start = ((bf16[16,64,512]{2,1,0:T(8,128)(2,1)}), bf16[16,64,512]{2,1,0:T(8,128)(2,1)S(1)}, u32[]{:S(2)}, u32[]{:S(2)}) async-start(bf16[16,64,512]{2,1,0:T(8,128)(2,1)} %broadcast_in_dim.6), calls=%async_computation | async-start | bytes 2097152 | tf_op jit(solution)/shard_map/all_to_all | solution.py:64
  9.2 1.5 %fusion.26 = f32[1024]{0:T(1024)S(1)} fusion(bf16[16384,512]{1,0:T(8,128)(2,1)} %param.7, s32[]{:T(128)S(6)} %select_n.101), kind=kLoop, calls=%fused_computation.40 | loop fusion | flops 1571840 | bytes 1052676 | tf_op jit(solution)/shard_map/nd,nd->n/dot_general | solution.py:89
  10.7 16.1 %all-to-all-done = bf16[16,64,512]{2,1,0:T(8,128)(2,1)S(1)} async-done(((bf16[16,64,512]{2,1,0:T(8,128)(2,1)}), bf16[16,64,512]{2,1,0:T(8,128)(2,1)S(1)}, u32[]{:S(2)}, u32[]{:S(2)}) %all-to-all-start) | async-done | bytes 1048608 | tf_op jit(solution)/shard_map/all_to_all | solution.py:64
  26.8 0.0 copy-done.3
  26.8 1.5 %broadcast_in_dim.7 = f32[16,256,128]{2,1,0:T(8,128)} broadcast(f32[256,128]{1,0:T(8,128)S(1)} %copy-done.3), dimensions={1,2} | broadcast | bytes 2228224 | tf_op jit(solution)/shard_map/broadcast_in_dim | solution.py:63
  28.4 4.4 %all-to-all-start.1 = ((f32[16,256,128]{2,1,0:T(8,128)}), f32[16,256,128]{2,1,0:T(8,128)}, u32[]{:S(2)}, u32[]{:S(2)}) async-start(f32[16,256,128]{2,1,0:T(8,128)} %broadcast_in_dim.7), calls=%async_computation.1 | async-start | bytes 4194304 | tf_op jit(solution)/shard_map/all_to_all | solution.py:64
  32.8 0.3 fusion.27
  33.1 0.0 copy-start.2
  33.1 0.0 copy-start.4
  33.1 26.6 %fusion.19 = f32[1024,896]{0,1:T(8,128)} fusion(bf16[1024,512]{1,0:T(8,128)(2,1)S(1)} %bitcast.27, f32[896]{0:T(1024)S(1)} %get-tuple-element.49, f32[1024]{0:T(1024)S(1)} %get-tuple-element.41, f32[896]{0:T(1024)S(1)} %get-tuple-element.48, f32[1024]{0:T(1024)S(1)} %get-tuple-element.40, f32[896]{0:T(1024)S(1)} %get-tuple-element.47, ...), kind=kOutput, calls=%fused_computation.23 | convolution fusion | flops 1066139648 | bytes 5697540 | tf_op jit(solution)/shard_map/dot_general | solution.py:33
  59.7 1.8 %all-to-all-done.1 = f32[16,256,128]{2,1,0:T(8,128)} async-done(((f32[16,256,128]{2,1,0:T(8,128)}), f32[16,256,128]{2,1,0:T(8,128)}, u32[]{:S(2)}, u32[]{:S(2)}) %all-to-all-start.1) | async-done | bytes 2097184 | tf_op jit(solution)/shard_map/all_to_all | solution.py:64
  61.6 0.0 copy-done
  61.6 2.3 %convolution_bitcast_fusion = f32[64,128]{1,0:T(8,128)S(1)} fusion(f32[4096,128]{1,0:T(8,128)} %bitcast.3, f32[64,4096]{1,0:T(8,128)S(1)} %copy-done), kind=kOutput, calls=%fused_computation.46 | convolution fusion | flops 201326592 | bytes 3178496 | tf_op jit(solution)/shard_map/dot_general | solution.py:98
  63.9 4.0 %collective-permute-start = (f32[64,128]{1,0:T(8,128)S(1)}, f32[64,128]{1,0:T(8,128)S(1)}, u32[]{:S(2)}, u32[]{:S(2)}) collective-permute-start(f32[64,128]{1,0:T(8,128)S(1)} %convolution_bitcast_fusion), channel_id=1, source_target_pairs={{0,64},{16,80},{32,96},{48,112},{64,0},{80,16},{96,32},{112,48},{1... | collective-permute-start | bytes 98312 | tf_op jit(solution)/shard_map/ppermute | solution.py:75
  67.9 1.9 %collective-permute-done = f32[64,128]{1,0:T(8,128)S(1)} collective-permute-done((f32[64,128]{1,0:T(8,128)S(1)}, f32[64,128]{1,0:T(8,128)S(1)}, u32[]{:S(2)}, u32[]{:S(2)}) %collective-permute-start) | collective-permute-done | bytes 32800 | tf_op jit(solution)/shard_map/ppermute | solution.py:75
  69.8 1.6 %collective-permute-start.1 = (f32[64,128]{1,0:T(8,128)S(1)}, f32[64,128]{1,0:T(8,128)S(1)}, u32[]{:S(2)}, u32[]{:S(2)}) collective-permute-start(f32[64,128]{1,0:T(8,128)S(1)} %add.335), channel_id=1, source_target_pairs={{0,32},{16,48},{32,0},{48,16},{64,96},{80,112},{96,64},{112,80},{1... | collective-permute-start | bytes 98312 | tf_op jit(solution)/shard_map/ppermute | solution.py:75
  71.3 2.3 %collective-permute-done.1 = f32[64,128]{1,0:T(8,128)S(1)} collective-permute-done((f32[64,128]{1,0:T(8,128)S(1)}, f32[64,128]{1,0:T(8,128)S(1)}, u32[]{:S(2)}, u32[]{:S(2)}) %collective-permute-start.1) | collective-permute-done | bytes 32800 | tf_op jit(solution)/shard_map/ppermute | solution.py:75
  73.7 0.0 collective-permute-start.2
  73.7 1.2 %collective-permute-done.2 = f32[64,128]{1,0:T(8,128)S(1)} collective-permute-done((f32[64,128]{1,0:T(8,128)S(1)}, f32[64,128]{1,0:T(8,128)S(1)}, u32[]{:S(2)}, u32[]{:S(2)}) %collective-permute-start.2) | collective-permute-done | bytes 32800 | tf_op jit(solution)/shard_map/ppermute | solution.py:75
  74.9 0.0 copy-done.2
  74.9 0.0 copy-done.4
  74.9 1.4 %fusion.54 = f32[1024,128]{1,0:T(8,128)} fusion(f32[1024,64]{0,1:T(8,128)S(1)} %bitcast.31, f32[64,128]{1,0:T(8,128)S(1)} %copy-done.4, f32[64,128]{1,0:T(8,128)S(1)} %add.336, f32[64,128]{1,0:T(8,128)S(1)} %collective-permute-done.2), kind=kOutput, calls=%fused_computation.81 | convolution fusion | flops 50348032 | bytes 884736 | tf_op jit(solution)/shard_map/dot_general | solution.py:106
  76.3 0.3 fusion.25
  76.6 5.3 %all-to-all-start.2 = ((f32[16,64,128]{2,1,0:T(8,128)}), f32[16,64,128]{2,1,0:T(8,128)S(1)}, u32[]{:S(2)}, u32[]{:S(2)}) async-start(f32[16,64,128]{2,1,0:T(8,128)} %bitcast.5), calls=%async_computation.2 | async-start | bytes 1048576 | tf_op jit(solution)/shard_map/all_to_all | solution.py:110
  81.9 0.0 copy-start.1
  81.9 5.4 %fusion.48 = f32[1024,128]{0,1:T(8,128)} fusion(bf16[1024,512]{1,0:T(8,128)(2,1)S(1)} %bitcast.29, f32[128]{0:T(128)S(1)} %get-tuple-element.33, f32[1024]{0:T(1024)S(1)} %get-tuple-element.25, f32[128]{0:T(128)S(1)} %get-tuple-element.34, f32[1024]{0:T(1024)S(1)} %get-tuple-element.24, f32[128]{0:T(128)S(1)} %get-tuple-element.35, ...), kind=kOutput, calls=%fused_computation.67 | convolution fusion | flops 152305664 | bytes 1740804 | tf_op jit(solution)/shard_map/dot_general | solution.py:33
  87.3 6.4 %all-to-all-done.2 = f32[16,64,128]{2,1,0:T(8,128)S(1)} async-done(((f32[16,64,128]{2,1,0:T(8,128)}), f32[16,64,128]{2,1,0:T(8,128)S(1)}, u32[]{:S(2)}, u32[]{:S(2)}) %all-to-all-start.2) | async-done | bytes 524320 | tf_op jit(solution)/shard_map/all_to_all | solution.py:110
  93.8 14.0 %all_to_all.20 = f32[16,64,128]{2,1,0:T(8,128)S(1)} all-to-all(f32[16,64,128]{2,1,0:T(8,128)S(1)} %broadcast_in_dim.8), channel_id=1, replica_groups=mesh['pr'=8,'pc'=16] {'pc'}, dimensions={0} | all-to-all | bytes 1048576 | tf_op jit(solution)/shard_map/all_to_all | solution.py:64
  107.8 0.0 copy-done.1
  107.8 4.8 %fusion.29 = f32[1024,128]{1,0:T(8,128)} fusion(f32[1024,128]{1,0:T(8,128)S(1)} %copy-done.1, f32[1024,128]{1,0:T(8,128)S(1)} %bitcast.30, f32[1024,128]{0,1:T(8,128)} %fusion.48, f32[1024,896]{0,1:T(8,128)} %fusion.19), kind=kOutput, calls=%fused_computation.45 | convolution fusion | flops 806486016 | bytes 5767168 | tf_op jit(solution)/shard_map/dot_general | solution.py:53
  (8 shorter events, 0.2 us)
Async XLA Ops:
  0.0 61.6 %copy-start = (f32[64,4096]{1,0:T(8,128)S(1)}, f32[64,4096]{1,0:T(8,128)}, u32[]{:S(2)}) copy-start(f32[64,4096]{1,0:T(8,128)} %param.9) | copy-start | bytes 3145732
  0.0 26.8 %copy-start.3 = (f32[256,128]{1,0:T(8,128)S(1)}, f32[256,128]{1,0:T(8,128)}, u32[]{:S(2)}) copy-start(f32[256,128]{1,0:T(8,128)} %param.10) | copy-start | bytes 393220
  2.0 24.8 %all-to-all-start = ((bf16[16,64,512]{2,1,0:T(8,128)(2,1)}), bf16[16,64,512]{2,1,0:T(8,128)(2,1)S(1)}, u32[]{:S(2)}, u32[]{:S(2)}) async-start(bf16[16,64,512]{2,1,0:T(8,128)(2,1)} %broadcast_in_dim.6), calls=%async_computation | async-start | bytes 2097152 | tf_op jit(solution)/shard_map/all_to_all | solution.py:64
  28.4 33.2 %all-to-all-start.1 = ((f32[16,256,128]{2,1,0:T(8,128)}), f32[16,256,128]{2,1,0:T(8,128)}, u32[]{:S(2)}, u32[]{:S(2)}) async-start(f32[16,256,128]{2,1,0:T(8,128)} %broadcast_in_dim.7), calls=%async_computation.1 | async-start | bytes 4194304 | tf_op jit(solution)/shard_map/all_to_all | solution.py:64
  33.1 41.8 %copy-start.2 = (f32[64,1024]{1,0:T(8,128)S(1)}, f32[64,1024]{1,0:T(8,128)}, u32[]{:S(2)}) copy-start(f32[64,1024]{1,0:T(8,128)} %param.12) | copy-start | bytes 786436
  33.1 41.8 %copy-start.4 = (f32[64,128]{1,0:T(8,128)S(1)}, f32[64,128]{1,0:T(8,128)}, u32[]{:S(2)}) copy-start(f32[64,128]{1,0:T(8,128)} %param.11) | copy-start | bytes 98308
  63.9 5.9 %collective-permute-start = (f32[64,128]{1,0:T(8,128)S(1)}, f32[64,128]{1,0:T(8,128)S(1)}, u32[]{:S(2)}, u32[]{:S(2)}) collective-permute-start(f32[64,128]{1,0:T(8,128)S(1)} %convolution_bitcast_fusion), channel_id=1, source_target_pairs={{0,64},{16,80},{32,96},{48,112},{64,0},{80,16},{96,32},{112,48},{1... | collective-permute-start | bytes 98312 | tf_op jit(solution)/shard_map/ppermute | solution.py:75
  69.8 3.9 %collective-permute-start.1 = (f32[64,128]{1,0:T(8,128)S(1)}, f32[64,128]{1,0:T(8,128)S(1)}, u32[]{:S(2)}, u32[]{:S(2)}) collective-permute-start(f32[64,128]{1,0:T(8,128)S(1)} %add.335), channel_id=1, source_target_pairs={{0,32},{16,48},{32,0},{48,16},{64,96},{80,112},{96,64},{112,80},{1... | collective-permute-start | bytes 98312 | tf_op jit(solution)/shard_map/ppermute | solution.py:75
  73.7 1.2 %collective-permute-start.2 = (f32[64,128]{1,0:T(8,128)S(1)}, f32[64,128]{1,0:T(8,128)S(1)}, u32[]{:S(2)}, u32[]{:S(2)}) collective-permute-start(f32[64,128]{1,0:T(8,128)S(1)} %add.336), channel_id=1, source_target_pairs={{0,16},{16,0},{32,48},{48,32},{64,80},{80,64},{96,112},{112,96},{1... | collective-permute-start | bytes 98312 | tf_op jit(solution)/shard_map/ppermute | solution.py:75
  76.6 17.2 %all-to-all-start.2 = ((f32[16,64,128]{2,1,0:T(8,128)}), f32[16,64,128]{2,1,0:T(8,128)S(1)}, u32[]{:S(2)}, u32[]{:S(2)}) async-start(f32[16,64,128]{2,1,0:T(8,128)} %bitcast.5), calls=%async_computation.2 | async-start | bytes 1048576 | tf_op jit(solution)/shard_map/all_to_all | solution.py:110
  81.9 25.9 %copy-start.1 = (f32[1024,128]{1,0:T(8,128)S(1)}, f32[1024,128]{1,0:T(8,128)}, u32[]{:S(2)}) copy-start(f32[1024,128]{1,0:T(8,128)} %param.13) | copy-start | bytes 1572868

commit v14 on v12

--- a/solution.py
+++ b/solution.py
@@ -110,9 +110,11 @@
     blocks = lax.all_to_all(
         spread_alpha.reshape((n_pc, -1) + spread_alpha.shape[1:]), "pc", 0, 0, tiled=False
     )
+    own_block = blocks.sum(0)
+    own_block, panel_late = lax.optimization_barrier((own_block, panel_late))
+    alpha_panel = gather_rows(own_block, "pc", n_pc)
     kern_b = arc_kernel(panel_late, test_own[split:], test_norms[split:])
-    kern_b, blocks = lax.optimization_barrier((kern_b, blocks))
-    alpha_panel = gather_rows(blocks.sum(0), "pc", n_pc)
+    kern_b, alpha_panel = lax.optimization_barrier((kern_b, alpha_panel))
     update = contract_rows(jnp.concatenate([kern_a, kern_b], axis=1), alpha_panel)
     return predictions_in + update
 

time: 111 us -> 112 us (level)
  blocking collectives: 13.1 us -> 0 us
  waiting for transfers between devices: 27.7 us -> 37.6 us
  starting transfers between devices: 22.8 us -> 26.5 us
    all_to_all x1 -> x0, blocking collectives: 13.1 us -> none  [gather_rows(): lax.all_to_all(copies, axis, 0, 0, tiled=False).reshape((-1,) + x.shape[1:])]
    all_to_all x1, waiting for transfers between devices: 4.63 us -> 10.1 us  [body(): lax.all_to_all(spread_alpha.reshape((n_pc, -1) + spread_alpha.shape[1:]),...]
    all_to_all x2 -> x3, waiting for transfers between devices: 18 us -> 22.4 us  [gather_rows(): lax.all_to_all(copies, axis, 0, 0, tiled=False).reshape((-1,) + x.shape[1:])]
    all_to_all x2 -> x3, starting transfers between devices: 11.6 us -> 15.3 us  [gather_rows(): lax.all_to_all(copies, axis, 0, 0, tiled=False).reshape((-1,) + x.shape[1:])]
  transfers between devices with their start and end apart: 6 -> 7, of which waited for: 6 -> 7; matrix products, arithmetic and copies ran while one was open for 31% -> 30% of each run, Pallas kernels for 0% -> 0%
where the time goes in v14:
time: 112 us; the launch traced here: 111 us
  matrix products  40.6 us (36%)
  waiting for transfers between devices  37.6 us (34%)
  starting transfers between devices  26.5 us (24%)
  local copies, waits for them, and re-layouts  4.38 us (4%)
  other arithmetic  2.16 us (2%)
    dot_general x2, matrix products, arc_kernel(): cross = jnp.dot(panel, test.T, preferred_element_type=jnp.float32) / width  32 us
    all_to_all x3, waiting for transfers between devices, gather_rows(): lax.all_to_all(copies, axis, 0, 0, tiled=False).reshape((-1,) + x.shape[1:])  22.4 us
    all_to_all x3, starting transfers between devices, gather_rows(): lax.all_to_all(copies, axis, 0, 0, tiled=False).reshape((-1,) + x.shape[1:])  15.3 us
    all_to_all x1, waiting for transfers between devices, body(): lax.all_to_all(spread_alpha.reshape((n_pc, -1) + spread_alpha.shape[1:]),...  10.1 us
    ppermute x3, starting transfers between devices, butterfly_sum(): x = x + lax.ppermute(x, axis, [(i, i ^ step) for i in range(n)])  5.88 us
    all_to_all x1, starting transfers between devices, body(): lax.all_to_all(spread_alpha.reshape((n_pc, -1) + spread_alpha.shape[1:]),...  5.29 us
    ppermute x3, waiting for transfers between devices, butterfly_sum(): x = x + lax.ppermute(x, axis, [(i, i ^ step) for i in range(n)])  5.08 us
    dot_general x1, matrix products, contract_rows(): lax.dot_general(left, right, (((0,), (0,)), ((), ())), precision=lax.Prec...  4.81 us
  transfers between devices with their start and end apart: 7, of which 7 were waited for; matrix products, arithmetic and copies ran while one was open for 30% of the time, Pallas kernels for 0%

profile of v14, /device:TPU:0, one launch (start us, length us, event | category | flops | bytes accessed | tf_op | source)
XLA Modules:
  0.0 111.3 jit_solution(1545245044871955158)
XLA Ops:
  0.0 0.0 copy-start
  0.0 0.0 copy-start.3
  0.0 2.0 %broadcast_in_dim.6 = bf16[16,64,512]{2,1,0:T(8,128)(2,1)} broadcast(bf16[64,512]{1,0:T(8,128)(2,1)} %param.8), dimensions={1,2} | broadcast | bytes 1114112 | tf_op jit(solution)/shard_map/broadcast_in_dim | solution.py:63
  2.0 7.1 %all-to-all-start = ((bf16[16,64,512]{2,1,0:T(8,128)(2,1)}), bf16[16,64,512]{2,1,0:T(8,128)(2,1)S(1)}, u32[]{:S(2)}, u32[]{:S(2)}) async-start(bf16[16,64,512]{2,1,0:T(8,128)(2,1)} %broadcast_in_dim.6), calls=%async_computation | async-start | bytes 2097152 | tf_op jit(solution)/shard_map/all_to_all | solution.py:64
  9.2 1.5 %fusion.26 = f32[1024]{0:T(1024)S(1)} fusion(bf16[16384,512]{1,0:T(8,128)(2,1)} %param.7, s32[]{:T(128)S(6)} %select_n.101), kind=kLoop, calls=%fused_computation.40 | loop fusion | flops 1571840 | bytes 1052676 | tf_op jit(solution)/shard_map/nd,nd->n/dot_general | solution.py:89
  10.7 16.1 %all-to-all-done = bf16[16,64,512]{2,1,0:T(8,128)(2,1)S(1)} async-done(((bf16[16,64,512]{2,1,0:T(8,128)(2,1)}), bf16[16,64,512]{2,1,0:T(8,128)(2,1)S(1)}, u32[]{:S(2)}, u32[]{:S(2)}) %all-to-all-start) | async-done | bytes 1048608 | tf_op jit(solution)/shard_map/all_to_all | solution.py:64
  26.8 0.0 copy-done.3
  26.8 1.5 %broadcast_in_dim.7 = f32[16,256,128]{2,1,0:T(8,128)} broadcast(f32[256,128]{1,0:T(8,128)S(1)} %copy-done.3), dimensions={1,2} | broadcast | bytes 2228224 | tf_op jit(solution)/shard_map/broadcast_in_dim | solution.py:63
  28.3 4.4 %all-to-all-start.1 = ((f32[16,256,128]{2,1,0:T(8,128)}), f32[16,256,128]{2,1,0:T(8,128)}, u32[]{:S(2)}, u32[]{:S(2)}) async-start(f32[16,256,128]{2,1,0:T(8,128)} %broadcast_in_dim.7), calls=%async_computation.1 | async-start | bytes 4194304 | tf_op jit(solution)/shard_map/all_to_all | solution.py:64
  32.8 0.3 fusion.27
  33.1 0.0 copy-start.2
  33.1 0.0 copy-start.4
  33.1 26.6 %fusion.19 = f32[1024,896]{0,1:T(8,128)} fusion(bf16[1024,512]{1,0:T(8,128)(2,1)S(1)} %bitcast.27, f32[896]{0:T(1024)S(1)} %get-tuple-element.53, f32[1024]{0:T(1024)S(1)} %get-tuple-element.45, f32[896]{0:T(1024)S(1)} %get-tuple-element.52, f32[1024]{0:T(1024)S(1)} %get-tuple-element.44, f32[896]{0:T(1024)S(1)} %get-tuple-element.51, ...), kind=kOutput, calls=%fused_computation.23 | convolution fusion | flops 1066139648 | bytes 5697540 | tf_op jit(solution)/shard_map/dot_general | solution.py:33
  59.7 1.8 %all-to-all-done.1 = f32[16,256,128]{2,1,0:T(8,128)} async-done(((f32[16,256,128]{2,1,0:T(8,128)}), f32[16,256,128]{2,1,0:T(8,128)}, u32[]{:S(2)}, u32[]{:S(2)}) %all-to-all-start.1) | async-done | bytes 2097184 | tf_op jit(solution)/shard_map/all_to_all | solution.py:64
  61.5 0.0 copy-done
  61.5 2.3 %convolution_bitcast_fusion = f32[64,128]{1,0:T(8,128)S(1)} fusion(f32[4096,128]{1,0:T(8,128)} %bitcast.3, f32[64,4096]{1,0:T(8,128)S(1)} %copy-done), kind=kOutput, calls=%fused_computation.46 | convolution fusion | flops 201326592 | bytes 3178496 | tf_op jit(solution)/shard_map/dot_general | solution.py:98
  63.9 0.1 collective-permute-start
  64.0 1.2 %collective-permute-done = f32[64,128]{1,0:T(8,128)S(1)} collective-permute-done((f32[64,128]{1,0:T(8,128)S(1)}, f32[64,128]{1,0:T(8,128)S(1)}, u32[]{:S(2)}, u32[]{:S(2)}) %collective-permute-start) | collective-permute-done | bytes 32800 | tf_op jit(solution)/shard_map/ppermute | solution.py:75
  65.2 1.9 %collective-permute-start.1 = (f32[64,128]{1,0:T(8,128)S(1)}, f32[64,128]{1,0:T(8,128)S(1)}, u32[]{:S(2)}, u32[]{:S(2)}) collective-permute-start(f32[64,128]{1,0:T(8,128)S(1)} %add.335), channel_id=1, source_target_pairs={{0,32},{16,48},{32,0},{48,16},{64,96},{80,112},{96,64},{112,80},{1... | collective-permute-start | bytes 98312 | tf_op jit(solution)/shard_map/ppermute | solution.py:75
  67.1 2.0 %collective-permute-done.1 = f32[64,128]{1,0:T(8,128)S(1)} collective-permute-done((f32[64,128]{1,0:T(8,128)S(1)}, f32[64,128]{1,0:T(8,128)S(1)}, u32[]{:S(2)}, u32[]{:S(2)}) %collective-permute-start.1) | collective-permute-done | bytes 32800 | tf_op jit(solution)/shard_map/ppermute | solution.py:75
  69.1 3.9 %collective-permute-start.2 = (f32[64,128]{1,0:T(8,128)S(1)}, f32[64,128]{1,0:T(8,128)S(1)}, u32[]{:S(2)}, u32[]{:S(2)}) collective-permute-start(f32[64,128]{1,0:T(8,128)S(1)} %add.336), channel_id=1, source_target_pairs={{0,64},{16,80},{32,96},{48,112},{64,0},{80,16},{96,32},{112,48},{1... | collective-permute-start | bytes 98312 | tf_op jit(solution)/shard_map/ppermute | solution.py:75
  73.0 1.9 %collective-permute-done.2 = f32[64,128]{1,0:T(8,128)S(1)} collective-permute-done((f32[64,128]{1,0:T(8,128)S(1)}, f32[64,128]{1,0:T(8,128)S(1)}, u32[]{:S(2)}, u32[]{:S(2)}) %collective-permute-start.2) | collective-permute-done | bytes 32800 | tf_op jit(solution)/shard_map/ppermute | solution.py:75
  74.9 0.0 copy-done.2
  74.9 0.0 copy-done.4
  74.9 1.4 %fusion.54 = f32[1024,128]{1,0:T(8,128)} fusion(f32[1024,64]{0,1:T(8,128)S(1)} %bitcast.31, f32[64,128]{1,0:T(8,128)S(1)} %copy-done.4, f32[64,128]{1,0:T(8,128)S(1)} %add.336, f32[64,128]{1,0:T(8,128)S(1)} %collective-permute-done.2), kind=kOutput, calls=%fused_computation.81 | convolution fusion | flops 50348032 | bytes 884736 | tf_op jit(solution)/shard_map/dot_general | solution.py:106
  76.3 5.3 %all-to-all-start.2 = ((f32[16,64,128]{2,1,0:T(8,128)}), f32[16,64,128]{2,1,0:T(8,128)S(1)}, u32[]{:S(2)}, u32[]{:S(2)}) async-start(f32[16,64,128]{2,1,0:T(8,128)} %bitcast.5), calls=%async_computation.2 | async-start | bytes 1048576 | tf_op jit(solution)/shard_map/all_to_all | solution.py:110
  81.6 10.1 %all-to-all-done.2 = f32[16,64,128]{2,1,0:T(8,128)S(1)} async-done(((f32[16,64,128]{2,1,0:T(8,128)}), f32[16,64,128]{2,1,0:T(8,128)S(1)}, u32[]{:S(2)}, u32[]{:S(2)}) %all-to-all-start.2) | async-done | bytes 524320 | tf_op jit(solution)/shard_map/all_to_all | solution.py:110
  91.7 0.3 fusion.25
  92.0 0.8 broadcast_in_dim.8
  92.8 3.8 %all-to-all-start.3 = ((f32[16,64,128]{2,1,0:T(8,128)}), f32[16,64,128]{2,1,0:T(8,128)S(1)}, u32[]{:S(2)}, u32[]{:S(2)}) async-start(f32[16,64,128]{2,1,0:T(8,128)} %broadcast_in_dim.8), calls=%async_computation.3 | async-start | bytes 1048576 | tf_op jit(solution)/shard_map/all_to_all | solution.py:64
  96.6 0.0 copy-start.1
  96.6 5.4 %fusion.48 = f32[1024,128]{0,1:T(8,128)} fusion(bf16[1024,512]{1,0:T(8,128)(2,1)S(1)} %bitcast.29, f32[128]{0:T(128)S(1)} %get-tuple-element.37, f32[1024]{0:T(1024)S(1)} %get-tuple-element.29, f32[128]{0:T(128)S(1)} %get-tuple-element.38, f32[1024]{0:T(1024)S(1)} %get-tuple-element.28, f32[128]{0:T(128)S(1)} %get-tuple-element.39, ...), kind=kOutput, calls=%fused_computation.67 | convolution fusion | flops 152305664 | bytes 1740804 | tf_op jit(solution)/shard_map/dot_general | solution.py:33
  102.0 4.5 %all-to-all-done.3 = f32[16,64,128]{2,1,0:T(8,128)S(1)} async-done(((f32[16,64,128]{2,1,0:T(8,128)}), f32[16,64,128]{2,1,0:T(8,128)S(1)}, u32[]{:S(2)}, u32[]{:S(2)}) %all-to-all-start.3) | async-done | bytes 524320 | tf_op jit(solution)/shard_map/all_to_all | solution.py:64
  106.5 0.0 copy-done.1
  106.5 4.8 %fusion.29 = f32[1024,128]{1,0:T(8,128)} fusion(f32[1024,128]{1,0:T(8,128)S(1)} %copy-done.1, f32[1024,128]{1,0:T(8,128)S(1)} %bitcast.30, f32[1024,128]{0,1:T(8,128)} %fusion.48, f32[1024,896]{0,1:T(8,128)} %fusion.19), kind=kOutput, calls=%fused_computation.45 | convolution fusion | flops 806486016 | bytes 5767168 | tf_op jit(solution)/shard_map/dot_general | solution.py:53
  (7 shorter events, 0.1 us)
Async XLA Ops:
  0.0 61.5 %copy-start = (f32[64,4096]{1,0:T(8,128)S(1)}, f32[64,4096]{1,0:T(8,128)}, u32[]{:S(2)}) copy-start(f32[64,4096]{1,0:T(8,128)} %param.9) | copy-start | bytes 3145732
  0.0 26.8 %copy-start.3 = (f32[256,128]{1,0:T(8,128)S(1)}, f32[256,128]{1,0:T(8,128)}, u32[]{:S(2)}) copy-start(f32[256,128]{1,0:T(8,128)} %param.10) | copy-start | bytes 393220
  2.0 24.8 %all-to-all-start = ((bf16[16,64,512]{2,1,0:T(8,128)(2,1)}), bf16[16,64,512]{2,1,0:T(8,128)(2,1)S(1)}, u32[]{:S(2)}, u32[]{:S(2)}) async-start(bf16[16,64,512]{2,1,0:T(8,128)(2,1)} %broadcast_in_dim.6), calls=%async_computation | async-start | bytes 2097152 | tf_op jit(solution)/shard_map/all_to_all | solution.py:64
  28.3 33.2 %all-to-all-start.1 = ((f32[16,256,128]{2,1,0:T(8,128)}), f32[16,256,128]{2,1,0:T(8,128)}, u32[]{:S(2)}, u32[]{:S(2)}) async-start(f32[16,256,128]{2,1,0:T(8,128)} %broadcast_in_dim.7), calls=%async_computation.1 | async-start | bytes 4194304 | tf_op jit(solution)/shard_map/all_to_all | solution.py:64
  33.1 41.8 %copy-start.2 = (f32[64,1024]{1,0:T(8,128)S(1)}, f32[64,1024]{1,0:T(8,128)}, u32[]{:S(2)}) copy-start(f32[64,1024]{1,0:T(8,128)} %param.12) | copy-start | bytes 786436
  33.1 41.8 %copy-start.4 = (f32[64,128]{1,0:T(8,128)S(1)}, f32[64,128]{1,0:T(8,128)}, u32[]{:S(2)}) copy-start(f32[64,128]{1,0:T(8,128)} %param.11) | copy-start | bytes 98308
  63.9 1.3 %collective-permute-start = (f32[64,128]{1,0:T(8,128)S(1)}, f32[64,128]{1,0:T(8,128)S(1)}, u32[]{:S(2)}, u32[]{:S(2)}) collective-permute-start(f32[64,128]{1,0:T(8,128)S(1)} %convolution_bitcast_fusion), channel_id=1, source_target_pairs={{0,16},{16,0},{32,48},{48,32},{64,80},{80,64},{96,112},{112,96},{1... | collective-permute-start | bytes 98312 | tf_op jit(solution)/shard_map/ppermute | solution.py:75
  65.2 3.9 %collective-permute-start.1 = (f32[64,128]{1,0:T(8,128)S(1)}, f32[64,128]{1,0:T(8,128)S(1)}, u32[]{:S(2)}, u32[]{:S(2)}) collective-permute-start(f32[64,128]{1,0:T(8,128)S(1)} %add.335), channel_id=1, source_target_pairs={{0,32},{16,48},{32,0},{48,16},{64,96},{80,112},{96,64},{112,80},{1... | collective-permute-start | bytes 98312 | tf_op jit(solution)/shard_map/ppermute | solution.py:75
  69.1 5.8 %collective-permute-start.2 = (f32[64,128]{1,0:T(8,128)S(1)}, f32[64,128]{1,0:T(8,128)S(1)}, u32[]{:S(2)}, u32[]{:S(2)}) collective-permute-start(f32[64,128]{1,0:T(8,128)S(1)} %add.336), channel_id=1, source_target_pairs={{0,64},{16,80},{32,96},{48,112},{64,0},{80,16},{96,32},{112,48},{1... | collective-permute-start | bytes 98312 | tf_op jit(solution)/shard_map/ppermute | solution.py:75
  76.3 15.4 %all-to-all-start.2 = ((f32[16,64,128]{2,1,0:T(8,128)}), f32[16,64,128]{2,1,0:T(8,128)S(1)}, u32[]{:S(2)}, u32[]{:S(2)}) async-start(f32[16,64,128]{2,1,0:T(8,128)} %bitcast.5), calls=%async_computation.2 | async-start | bytes 1048576 | tf_op jit(solution)/shard_map/all_to_all | solution.py:110
  92.8 13.7 %all-to-all-start.3 = ((f32[16,64,128]{2,1,0:T(8,128)}), f32[16,64,128]{2,1,0:T(8,128)S(1)}, u32[]{:S(2)}, u32[]{:S(2)}) async-start(f32[16,64,128]{2,1,0:T(8,128)} %broadcast_in_dim.8), calls=%async_computation.3 | async-start | bytes 1048576 | tf_op jit(solution)/shard_map/all_to_all | solution.py:64
  96.6 9.9 %copy-start.1 = (f32[1024,128]{1,0:T(8,128)S(1)}, f32[1024,128]{1,0:T(8,128)}, u32[]{:S(2)}) copy-start(f32[1024,128]{1,0:T(8,128)} %param.13) | copy-start | bytes 1572868

commit v15 on v12

--- a/solution.py
+++ b/solution.py
@@ -91,7 +91,7 @@
     )
     inverse_t = jnp.transpose(inverse_block)
     inverse_t, alpha_below = lax.optimization_barrier((inverse_t, alpha_below))
-    split = rows - rows // 8
+    split = rows - 3 * rows // 16
     kern_a = arc_kernel(panel_all, test_own[:split], test_norms[:split])
     gathered = gather_rows(alpha_below, "pc", n_pc)
     kern_a, gathered = lax.optimization_barrier((kern_a, gathered))

time: 111 us -> 109 us (0.982)
  starting transfers between devices: 22.8 us -> 21.2 us
    all_to_all x2, waiting for transfers between devices: 18 us -> 19.6 us  [gather_rows(): lax.all_to_all(copies, axis, 0, 0, tiled=False).reshape((-1,) + x.shape[1:])]
    all_to_all x1, starting transfers between devices: 5.3 us -> 3.79 us  [body(): lax.all_to_all(spread_alpha.reshape((n_pc, -1) + spread_alpha.shape[1:]),...]
where the time goes in v15:
time: 109 us; the launch traced here: 108 us
  matrix products  39.6 us (36%)
  waiting for transfers between devices  28.3 us (26%)
  starting transfers between devices  21.2 us (19%)
  blocking collectives  13.4 us (12%)
  local copies, waits for them, and re-layouts  3.62 us (3%)
  other arithmetic  2.23 us (2%)
    dot_general x2, matrix products, arc_kernel(): cross = jnp.dot(panel, test.T, preferred_element_type=jnp.float32) / width  31.2 us
    all_to_all x2, waiting for transfers between devices, gather_rows(): lax.all_to_all(copies, axis, 0, 0, tiled=False).reshape((-1,) + x.shape[1:])  19.6 us
    all_to_all x1, blocking collectives, gather_rows(): lax.all_to_all(copies, axis, 0, 0, tiled=False).reshape((-1,) + x.shape[1:])  13.4 us
    all_to_all x2, starting transfers between devices, gather_rows(): lax.all_to_all(copies, axis, 0, 0, tiled=False).reshape((-1,) + x.shape[1:])  11.6 us
    ppermute x3, starting transfers between devices, butterfly_sum(): x = x + lax.ppermute(x, axis, [(i, i ^ step) for i in range(n)])  5.88 us
    ppermute x3, waiting for transfers between devices, butterfly_sum(): x = x + lax.ppermute(x, axis, [(i, i ^ step) for i in range(n)])  5 us
    dot_general x1, matrix products, contract_rows(): lax.dot_general(left, right, (((0,), (0,)), ((), ())), precision=lax.Prec...  4.67 us
    all_to_all x1, starting transfers between devices, body(): lax.all_to_all(spread_alpha.reshape((n_pc, -1) + spread_alpha.shape[1:]),...  3.79 us
  transfers between devices with their start and end apart: 6, of which 6 were waited for; matrix products, arithmetic and copies ran while one was open for 31% of the time, Pallas kernels for 0%

profile of v15, /device:TPU:0, one launch (start us, length us, event | category | flops | bytes accessed | tf_op | source)
XLA Modules:
  0.0 108.5 jit_solution(2596523163167689618)
XLA Ops:
  0.0 0.0 copy-start
  0.0 0.0 copy-start.2
  0.0 2.0 %broadcast_in_dim.6 = bf16[16,64,512]{2,1,0:T(8,128)(2,1)} broadcast(bf16[64,512]{1,0:T(8,128)(2,1)} %param.8), dimensions={1,2} | broadcast | bytes 1114112 | tf_op jit(solution)/shard_map/broadcast_in_dim | solution.py:63
  2.0 7.1 %all-to-all-start = ((bf16[16,64,512]{2,1,0:T(8,128)(2,1)}), bf16[16,64,512]{2,1,0:T(8,128)(2,1)S(1)}, u32[]{:S(2)}, u32[]{:S(2)}) async-start(bf16[16,64,512]{2,1,0:T(8,128)(2,1)} %broadcast_in_dim.6), calls=%async_computation | async-start | bytes 2097152 | tf_op jit(solution)/shard_map/all_to_all | solution.py:64
  9.2 1.5 %fusion.26 = f32[1024]{0:T(1024)S(1)} fusion(bf16[16384,512]{1,0:T(8,128)(2,1)} %param.7, s32[]{:T(128)S(6)} %select_n.101), kind=kLoop, calls=%fused_computation.40 | loop fusion | flops 1571840 | bytes 1052676 | tf_op jit(solution)/shard_map/nd,nd->n/dot_general | solution.py:89
  10.7 16.1 %all-to-all-done = bf16[16,64,512]{2,1,0:T(8,128)(2,1)S(1)} async-done(((bf16[16,64,512]{2,1,0:T(8,128)(2,1)}), bf16[16,64,512]{2,1,0:T(8,128)(2,1)S(1)}, u32[]{:S(2)}, u32[]{:S(2)}) %all-to-all-start) | async-done | bytes 1048608 | tf_op jit(solution)/shard_map/all_to_all | solution.py:64
  26.8 0.0 copy-done.2
  26.8 1.6 %broadcast_in_dim.7 = f32[16,256,128]{2,1,0:T(8,128)} broadcast(f32[256,128]{1,0:T(8,128)S(1)} %copy-done.2), dimensions={1,2} | broadcast | bytes 2228224 | tf_op jit(solution)/shard_map/broadcast_in_dim | solution.py:63
  28.4 4.4 %all-to-all-start.1 = ((f32[16,256,128]{2,1,0:T(8,128)}), f32[16,256,128]{2,1,0:T(8,128)}, u32[]{:S(2)}, u32[]{:S(2)}) async-start(f32[16,256,128]{2,1,0:T(8,128)} %broadcast_in_dim.7), calls=%async_computation.1 | async-start | bytes 4194304 | tf_op jit(solution)/shard_map/all_to_all | solution.py:64
  32.8 0.3 fusion.27
  33.1 24.9 %fusion.19 = f32[1024,832]{0,1:T(8,128)} fusion(bf16[1024,512]{1,0:T(8,128)(2,1)S(1)} %bitcast.27, f32[832]{0:T(1024)S(1)} %get-tuple-element.49, f32[1024]{0:T(1024)S(1)} %get-tuple-element.41, f32[832]{0:T(1024)S(1)} %get-tuple-element.48, f32[1024]{0:T(1024)S(1)} %get-tuple-element.40, f32[832]{0:T(1024)S(1)} %get-tuple-element.47, ...), kind=kOutput, calls=%fused_computation.23 | convolution fusion | flops 989986816 | bytes 5367812 | tf_op jit(solution)/shard_map/dot_general | solution.py:33
  58.1 0.0 copy-start.1
  58.1 0.0 copy-start.3
  58.1 3.5 %all-to-all-done.1 = f32[16,256,128]{2,1,0:T(8,128)} async-done(((f32[16,256,128]{2,1,0:T(8,128)}), f32[16,256,128]{2,1,0:T(8,128)}, u32[]{:S(2)}, u32[]{:S(2)}) %all-to-all-start.1) | async-done | bytes 2097184 | tf_op jit(solution)/shard_map/all_to_all | solution.py:64
  61.6 0.0 copy-done
  61.6 2.3 %convolution_bitcast_fusion = f32[64,128]{1,0:T(8,128)S(1)} fusion(f32[4096,128]{1,0:T(8,128)} %bitcast.3, f32[64,4096]{1,0:T(8,128)S(1)} %copy-done), kind=kOutput, calls=%fused_computation.50 | convolution fusion | flops 201326592 | bytes 3178496 | tf_op jit(solution)/shard_map/dot_general | solution.py:98
  63.9 0.1 collective-permute-start
  64.0 1.2 %collective-permute-done = f32[64,128]{1,0:T(8,128)S(1)} collective-permute-done((f32[64,128]{1,0:T(8,128)S(1)}, f32[64,128]{1,0:T(8,128)S(1)}, u32[]{:S(2)}, u32[]{:S(2)}) %collective-permute-start) | collective-permute-done | bytes 32800 | tf_op jit(solution)/shard_map/ppermute | solution.py:75
  65.2 1.9 %collective-permute-start.1 = (f32[64,128]{1,0:T(8,128)S(1)}, f32[64,128]{1,0:T(8,128)S(1)}, u32[]{:S(2)}, u32[]{:S(2)}) collective-permute-start(f32[64,128]{1,0:T(8,128)S(1)} %add.335), channel_id=1, source_target_pairs={{0,32},{16,48},{32,0},{48,16},{64,96},{80,112},{96,64},{112,80},{1... | collective-permute-start | bytes 98312 | tf_op jit(solution)/shard_map/ppermute | solution.py:75
  67.1 2.0 %collective-permute-done.1 = f32[64,128]{1,0:T(8,128)S(1)} collective-permute-done((f32[64,128]{1,0:T(8,128)S(1)}, f32[64,128]{1,0:T(8,128)S(1)}, u32[]{:S(2)}, u32[]{:S(2)}) %collective-permute-start.1) | collective-permute-done | bytes 32800 | tf_op jit(solution)/shard_map/ppermute | solution.py:75
  69.1 3.9 %collective-permute-start.2 = (f32[64,128]{1,0:T(8,128)S(1)}, f32[64,128]{1,0:T(8,128)S(1)}, u32[]{:S(2)}, u32[]{:S(2)}) collective-permute-start(f32[64,128]{1,0:T(8,128)S(1)} %add.336), channel_id=1, source_target_pairs={{0,64},{16,80},{32,96},{48,112},{64,0},{80,16},{96,32},{112,48},{1... | collective-permute-start | bytes 98312 | tf_op jit(solution)/shard_map/ppermute | solution.py:75
  73.0 0.1 add_sqrt_fusion.15
  73.1 1.8 %collective-permute-done.2 = f32[64,128]{1,0:T(8,128)S(1)} collective-permute-done((f32[64,128]{1,0:T(8,128)S(1)}, f32[64,128]{1,0:T(8,128)S(1)}, u32[]{:S(2)}, u32[]{:S(2)}) %collective-permute-start.2) | collective-permute-done | bytes 32800 | tf_op jit(solution)/shard_map/ppermute | solution.py:75
  74.9 0.0 copy-done.1
  74.9 0.0 copy-done.3
  74.9 1.4 %fusion.54 = f32[1024,128]{1,0:T(8,128)} fusion(f32[1024,64]{0,1:T(8,128)S(1)} %bitcast.31, f32[64,128]{1,0:T(8,128)S(1)} %copy-done.3, f32[64,128]{1,0:T(8,128)S(1)} %add.336, f32[64,128]{1,0:T(8,128)S(1)} %collective-permute-done.2), kind=kOutput, calls=%fused_computation.81 | convolution fusion | flops 50348032 | bytes 884736 | tf_op jit(solution)/shard_map/dot_general | solution.py:106
  76.3 0.3 fusion.25
  76.6 3.8 %all-to-all-start.2 = ((f32[16,64,128]{2,1,0:T(8,128)}), f32[16,64,128]{2,1,0:T(8,128)S(1)}, u32[]{:S(2)}, u32[]{:S(2)}) async-start(f32[16,64,128]{2,1,0:T(8,128)} %bitcast.5), calls=%async_computation.2 | async-start | bytes 1048576 | tf_op jit(solution)/shard_map/all_to_all | solution.py:110
  80.4 6.3 %fusion.48 = f32[1024,192]{0,1:T(8,128)S(1)} fusion(bf16[1024,512]{1,0:T(8,128)(2,1)S(1)} %bitcast.29, f32[192]{0:T(256)S(1)} %get-tuple-element.33, f32[1024]{0:T(1024)S(1)} %get-tuple-element.25, f32[192]{0:T(256)S(1)} %get-tuple-element.32, f32[1024]{0:T(1024)S(1)} %get-tuple-element.24, f32[192]{0:T(256)S(1)} %get-tuple-element.31, ...), kind=kOutput, calls=%fused_computation.67 | convolution fusion | flops 228458496 | bytes 2070532 | tf_op jit(solution)/shard_map/dot_general | solution.py:33
  86.7 3.7 %all-to-all-done.2 = f32[16,64,128]{2,1,0:T(8,128)S(1)} async-done(((f32[16,64,128]{2,1,0:T(8,128)}), f32[16,64,128]{2,1,0:T(8,128)S(1)}, u32[]{:S(2)}, u32[]{:S(2)}) %all-to-all-start.2) | async-done | bytes 524320 | tf_op jit(solution)/shard_map/all_to_all | solution.py:110
  90.4 13.4 %all_to_all.20 = f32[16,64,128]{2,1,0:T(8,128)S(1)} all-to-all(f32[16,64,128]{2,1,0:T(8,128)S(1)} %broadcast_in_dim.8), channel_id=1, replica_groups=mesh['pr'=8,'pc'=16] {'pc'}, dimensions={0} | all-to-all | bytes 1048576 | tf_op jit(solution)/shard_map/all_to_all | solution.py:64
  103.8 4.7 %fusion.29 = f32[1024,128]{1,0:T(8,128)} fusion(f32[1024,128]{1,0:T(8,128)} %param.13, f32[1024,128]{1,0:T(8,128)S(1)} %bitcast.30, f32[1024,192]{0,1:T(8,128)S(1)} %fusion.48, f32[1024,832]{0,1:T(8,128)} %fusion.19), kind=kOutput, calls=%fused_computation.45 | convolution fusion | flops 806486016 | bytes 5767168 | tf_op jit(solution)/shard_map/dot_general | solution.py:53
  (7 shorter events, 0.1 us)
Async XLA Ops:
  0.0 61.6 %copy-start = (f32[64,4096]{1,0:T(8,128)S(1)}, f32[64,4096]{1,0:T(8,128)}, u32[]{:S(2)}) copy-start(f32[64,4096]{1,0:T(8,128)} %param.9) | copy-start | bytes 3145732
  0.0 26.8 %copy-start.2 = (f32[256,128]{1,0:T(8,128)S(1)}, f32[256,128]{1,0:T(8,128)}, u32[]{:S(2)}) copy-start(f32[256,128]{1,0:T(8,128)} %param.10) | copy-start | bytes 393220
  2.0 24.8 %all-to-all-start = ((bf16[16,64,512]{2,1,0:T(8,128)(2,1)}), bf16[16,64,512]{2,1,0:T(8,128)(2,1)S(1)}, u32[]{:S(2)}, u32[]{:S(2)}) async-start(bf16[16,64,512]{2,1,0:T(8,128)(2,1)} %broadcast_in_dim.6), calls=%async_computation | async-start | bytes 2097152 | tf_op jit(solution)/shard_map/all_to_all | solution.py:64
  28.4 33.2 %all-to-all-start.1 = ((f32[16,256,128]{2,1,0:T(8,128)}), f32[16,256,128]{2,1,0:T(8,128)}, u32[]{:S(2)}, u32[]{:S(2)}) async-start(f32[16,256,128]{2,1,0:T(8,128)} %broadcast_in_dim.7), calls=%async_computation.1 | async-start | bytes 4194304 | tf_op jit(solution)/shard_map/all_to_all | solution.py:64
  58.1 16.8 %copy-start.1 = (f32[64,1024]{1,0:T(8,128)S(1)}, f32[64,1024]{1,0:T(8,128)}, u32[]{:S(2)}) copy-start(f32[64,1024]{1,0:T(8,128)} %param.12) | copy-start | bytes 786436
  58.1 16.8 %copy-start.3 = (f32[64,128]{1,0:T(8,128)S(1)}, f32[64,128]{1,0:T(8,128)}, u32[]{:S(2)}) copy-start(f32[64,128]{1,0:T(8,128)} %param.11) | copy-start | bytes 98308
  63.9 1.3 %collective-permute-start = (f32[64,128]{1,0:T(8,128)S(1)}, f32[64,128]{1,0:T(8,128)S(1)}, u32[]{:S(2)}, u32[]{:S(2)}) collective-permute-start(f32[64,128]{1,0:T(8,128)S(1)} %convolution_bitcast_fusion), channel_id=1, source_target_pairs={{0,16},{16,0},{32,48},{48,32},{64,80},{80,64},{96,112},{112,96},{1... | collective-permute-start | bytes 98312 | tf_op jit(solution)/shard_map/ppermute | solution.py:75
  65.2 3.9 %collective-permute-start.1 = (f32[64,128]{1,0:T(8,128)S(1)}, f32[64,128]{1,0:T(8,128)S(1)}, u32[]{:S(2)}, u32[]{:S(2)}) collective-permute-start(f32[64,128]{1,0:T(8,128)S(1)} %add.335), channel_id=1, source_target_pairs={{0,32},{16,48},{32,0},{48,16},{64,96},{80,112},{96,64},{112,80},{1... | collective-permute-start | bytes 98312 | tf_op jit(solution)/shard_map/ppermute | solution.py:75
  69.1 5.8 %collective-permute-start.2 = (f32[64,128]{1,0:T(8,128)S(1)}, f32[64,128]{1,0:T(8,128)S(1)}, u32[]{:S(2)}, u32[]{:S(2)}) collective-permute-start(f32[64,128]{1,0:T(8,128)S(1)} %add.336), channel_id=1, source_target_pairs={{0,64},{16,80},{32,96},{48,112},{64,0},{80,16},{96,32},{112,48},{1... | collective-permute-start | bytes 98312 | tf_op jit(solution)/shard_map/ppermute | solution.py:75
  76.6 13.8 %all-to-all-start.2 = ((f32[16,64,128]{2,1,0:T(8,128)}), f32[16,64,128]{2,1,0:T(8,128)S(1)}, u32[]{:S(2)}, u32[]{:S(2)}) async-start(f32[16,64,128]{2,1,0:T(8,128)} %bitcast.5), calls=%async_computation.2 | async-start | bytes 1048576 | tf_op jit(solution)/shard_map/all_to_all | solution.py:110

commit v16 on v15

--- a/solution.py
+++ b/solution.py
@@ -91,7 +91,7 @@
     )
     inverse_t = jnp.transpose(inverse_block)
     inverse_t, alpha_below = lax.optimization_barrier((inverse_t, alpha_below))
-    split = rows - 3 * rows // 16
+    split = rows - rows // 4
     kern_a = arc_kernel(panel_all, test_own[:split], test_norms[:split])
     gathered = gather_rows(alpha_below, "pc", n_pc)
     kern_a, gathered = lax.optimization_barrier((kern_a, gathered))

time: 109 us -> 112 us (1.028)
  blocking collectives: 13.4 us -> 16.2 us
  matrix products: 39.6 us -> 40.9 us
  waiting for transfers between devices: 28.3 us -> 27.1 us
    all_to_all x1, waiting for transfers between devices: 3.67 us -> 0.76 us  [body(): lax.all_to_all(spread_alpha.reshape((n_pc, -1) + spread_alpha.shape[1:]),...]
    all_to_all x1, blocking collectives: 13.4 us -> 16.2 us  [gather_rows(): lax.all_to_all(copies, axis, 0, 0, tiled=False).reshape((-1,) + x.shape[1:])]
    all_to_all x2, waiting for transfers between devices: 19.6 us -> 21.3 us  [gather_rows(): lax.all_to_all(copies, axis, 0, 0, tiled=False).reshape((-1,) + x.shape[1:])]
    dot_general x2, matrix products: 31.2 us -> 32.4 us  [arc_kernel(): cross = jnp.dot(panel, test.T, preferred_element_type=jnp.float32) / width]
where the time goes in v16:
time: 112 us; the launch traced here: 111 us
  matrix products  40.9 us (37%)
  waiting for transfers between devices  27.1 us (24%)
  starting transfers between devices  21.2 us (19%)
  blocking collectives  16.2 us (14%)
  local copies, waits for them, and re-layouts  3.64 us (3%)
  other arithmetic  2.16 us (2%)
    dot_general x2, matrix products, arc_kernel(): cross = jnp.dot(panel, test.T, preferred_element_type=jnp.float32) / width  32.4 us
    all_to_all x2, waiting for transfers between devices, gather_rows(): lax.all_to_all(copies, axis, 0, 0, tiled=False).reshape((-1,) + x.shape[1:])  21.3 us
    all_to_all x1, blocking collectives, gather_rows(): lax.all_to_all(copies, axis, 0, 0, tiled=False).reshape((-1,) + x.shape[1:])  16.2 us
    all_to_all x2, starting transfers between devices, gather_rows(): lax.all_to_all(copies, axis, 0, 0, tiled=False).reshape((-1,) + x.shape[1:])  11.6 us
    ppermute x3, starting transfers between devices, butterfly_sum(): x = x + lax.ppermute(x, axis, [(i, i ^ step) for i in range(n)])  5.88 us
    ppermute x3, waiting for transfers between devices, butterfly_sum(): x = x + lax.ppermute(x, axis, [(i, i ^ step) for i in range(n)])  5.06 us
    dot_general x1, matrix products, contract_rows(): lax.dot_general(left, right, (((0,), (0,)), ((), ())), precision=lax.Prec...  4.82 us
    all_to_all x1, starting transfers between devices, body(): lax.all_to_all(spread_alpha.reshape((n_pc, -1) + spread_alpha.shape[1:]),...  3.77 us
  transfers between devices with their start and end apart: 6, of which 6 were waited for; matrix products, arithmetic and copies ran while one was open for 31% of the time, Pallas kernels for 0%

profile of v16, /device:TPU:0, one launch (start us, length us, event | category | flops | bytes accessed | tf_op | source)
XLA Modules:
  0.0 111.3 jit_solution(17075482496151924243)
XLA Ops:
  0.0 0.0 copy-start
  0.0 0.0 copy-start.3
  0.0 2.0 %broadcast_in_dim.6 = bf16[16,64,512]{2,1,0:T(8,128)(2,1)} broadcast(bf16[64,512]{1,0:T(8,128)(2,1)} %param.8), dimensions={1,2} | broadcast | bytes 1114112 | tf_op jit(solution)/shard_map/broadcast_in_dim | solution.py:63
  2.0 7.1 %all-to-all-start = ((bf16[16,64,512]{2,1,0:T(8,128)(2,1)}), bf16[16,64,512]{2,1,0:T(8,128)(2,1)S(1)}, u32[]{:S(2)}, u32[]{:S(2)}) async-start(bf16[16,64,512]{2,1,0:T(8,128)(2,1)} %broadcast_in_dim.6), calls=%async_computation | async-start | bytes 2097152 | tf_op jit(solution)/shard_map/all_to_all | solution.py:64
  9.2 1.5 %fusion.26 = f32[1024]{0:T(1024)S(1)} fusion(bf16[16384,512]{1,0:T(8,128)(2,1)} %param.7, s32[]{:T(128)S(6)} %select_n.101), kind=kLoop, calls=%fused_computation.40 | loop fusion | flops 1571840 | bytes 1052676 | tf_op jit(solution)/shard_map/nd,nd->n/dot_general | solution.py:89
  10.7 16.1 %all-to-all-done = bf16[16,64,512]{2,1,0:T(8,128)(2,1)S(1)} async-done(((bf16[16,64,512]{2,1,0:T(8,128)(2,1)}), bf16[16,64,512]{2,1,0:T(8,128)(2,1)S(1)}, u32[]{:S(2)}, u32[]{:S(2)}) %all-to-all-start) | async-done | bytes 1048608 | tf_op jit(solution)/shard_map/all_to_all | solution.py:64
  26.8 0.0 copy-done.3
  26.8 1.6 %broadcast_in_dim.7 = f32[16,256,128]{2,1,0:T(8,128)} broadcast(f32[256,128]{1,0:T(8,128)S(1)} %copy-done.3), dimensions={1,2} | broadcast | bytes 2228224 | tf_op jit(solution)/shard_map/broadcast_in_dim | solution.py:63
  28.4 4.4 %all-to-all-start.1 = ((f32[16,256,128]{2,1,0:T(8,128)}), f32[16,256,128]{2,1,0:T(8,128)}, u32[]{:S(2)}, u32[]{:S(2)}) async-start(f32[16,256,128]{2,1,0:T(8,128)} %broadcast_in_dim.7), calls=%async_computation.1 | async-start | bytes 4194304 | tf_op jit(solution)/shard_map/all_to_all | solution.py:64
  32.8 0.3 fusion.27
  33.2 23.3 %fusion.19 = f32[1024,768]{0,1:T(8,128)} fusion(bf16[1024,512]{1,0:T(8,128)(2,1)S(1)} %bitcast.27, f32[768]{0:T(1024)S(1)} %get-tuple-element.49, f32[1024]{0:T(1024)S(1)} %get-tuple-element.41, f32[768]{0:T(1024)S(1)} %get-tuple-element.48, f32[1024]{0:T(1024)S(1)} %get-tuple-element.40, f32[768]{0:T(1024)S(1)} %get-tuple-element.47, ...), kind=kOutput, calls=%fused_computation.23 | convolution fusion | flops 913833984 | bytes 5038084 | tf_op jit(solution)/shard_map/dot_general | solution.py:33
  56.4 0.0 copy-start.2
  56.4 0.0 copy-start.4
  56.4 5.2 %all-to-all-done.1 = f32[16,256,128]{2,1,0:T(8,128)} async-done(((f32[16,256,128]{2,1,0:T(8,128)}), f32[16,256,128]{2,1,0:T(8,128)}, u32[]{:S(2)}, u32[]{:S(2)}) %all-to-all-start.1) | async-done | bytes 2097184 | tf_op jit(solution)/shard_map/all_to_all | solution.py:64
  61.6 0.0 copy-done
  61.6 2.3 %convolution_bitcast_fusion = f32[64,128]{1,0:T(8,128)S(1)} fusion(f32[4096,128]{1,0:T(8,128)} %bitcast.3, f32[64,4096]{1,0:T(8,128)S(1)} %copy-done), kind=kOutput, calls=%fused_computation.50 | convolution fusion | flops 201326592 | bytes 3178496 | tf_op jit(solution)/shard_map/dot_general | solution.py:98
  63.9 0.1 collective-permute-start
  64.0 1.2 %collective-permute-done = f32[64,128]{1,0:T(8,128)S(1)} collective-permute-done((f32[64,128]{1,0:T(8,128)S(1)}, f32[64,128]{1,0:T(8,128)S(1)}, u32[]{:S(2)}, u32[]{:S(2)}) %collective-permute-start) | collective-permute-done | bytes 32800 | tf_op jit(solution)/shard_map/ppermute | solution.py:75
  65.2 1.9 %collective-permute-start.1 = (f32[64,128]{1,0:T(8,128)S(1)}, f32[64,128]{1,0:T(8,128)S(1)}, u32[]{:S(2)}, u32[]{:S(2)}) collective-permute-start(f32[64,128]{1,0:T(8,128)S(1)} %add.335), channel_id=1, source_target_pairs={{0,32},{16,48},{32,0},{48,16},{64,96},{80,112},{96,64},{112,80},{1... | collective-permute-start | bytes 98312 | tf_op jit(solution)/shard_map/ppermute | solution.py:75
  67.2 2.0 %collective-permute-done.1 = f32[64,128]{1,0:T(8,128)S(1)} collective-permute-done((f32[64,128]{1,0:T(8,128)S(1)}, f32[64,128]{1,0:T(8,128)S(1)}, u32[]{:S(2)}, u32[]{:S(2)}) %collective-permute-start.1) | collective-permute-done | bytes 32800 | tf_op jit(solution)/shard_map/ppermute | solution.py:75
  69.2 3.9 %collective-permute-start.2 = (f32[64,128]{1,0:T(8,128)S(1)}, f32[64,128]{1,0:T(8,128)S(1)}, u32[]{:S(2)}, u32[]{:S(2)}) collective-permute-start(f32[64,128]{1,0:T(8,128)S(1)} %add.336), channel_id=1, source_target_pairs={{0,64},{16,80},{32,96},{48,112},{64,0},{80,16},{96,32},{112,48},{1... | collective-permute-start | bytes 98312 | tf_op jit(solution)/shard_map/ppermute | solution.py:75
  73.1 1.9 %collective-permute-done.2 = f32[64,128]{1,0:T(8,128)S(1)} collective-permute-done((f32[64,128]{1,0:T(8,128)S(1)}, f32[64,128]{1,0:T(8,128)S(1)}, u32[]{:S(2)}, u32[]{:S(2)}) %collective-permute-start.2) | collective-permute-done | bytes 32800 | tf_op jit(solution)/shard_map/ppermute | solution.py:75
  74.9 0.0 copy-done.2
  74.9 0.0 copy-done.4
  74.9 1.4 %fusion.54 = f32[1024,128]{1,0:T(8,128)} fusion(f32[1024,64]{0,1:T(8,128)S(1)} %bitcast.31, f32[64,128]{1,0:T(8,128)S(1)} %copy-done.4, f32[64,128]{1,0:T(8,128)S(1)} %add.336, f32[64,128]{1,0:T(8,128)S(1)} %collective-permute-done.2), kind=kOutput, calls=%fused_computation.81 | convolution fusion | flops 50348032 | bytes 884736 | tf_op jit(solution)/shard_map/dot_general | solution.py:106
  76.3 0.3 fusion.25
  76.6 3.8 %all-to-all-start.2 = ((f32[16,64,128]{2,1,0:T(8,128)}), f32[16,64,128]{2,1,0:T(8,128)S(1)}, u32[]{:S(2)}, u32[]{:S(2)}) async-start(f32[16,64,128]{2,1,0:T(8,128)} %bitcast.5), calls=%async_computation.2 | async-start | bytes 1048576 | tf_op jit(solution)/shard_map/all_to_all | solution.py:110
  80.4 0.0 copy-start.1
  80.4 9.1 %fusion.47 = f32[1024,256]{0,1:T(8,128)} fusion(bf16[1024,512]{1,0:T(8,128)(2,1)S(1)} %bitcast.29, f32[256]{0:T(256)S(1)} %get-tuple-element.33, f32[1024]{0:T(1024)S(1)} %get-tuple-element.25, f32[256]{0:T(256)S(1)} %get-tuple-element.32, f32[1024]{0:T(1024)S(1)} %get-tuple-element.24, f32[256]{0:T(256)S(1)} %get-tuple-element.31, ...), kind=kOutput, calls=%fused_computation.66 | convolution fusion | flops 304611328 | bytes 2400260 | tf_op jit(solution)/shard_map/dot_general | solution.py:33
  89.5 0.8 all-to-all-done.2
  90.4 16.2 %all_to_all.20 = f32[16,64,128]{2,1,0:T(8,128)S(1)} all-to-all(f32[16,64,128]{2,1,0:T(8,128)S(1)} %broadcast_in_dim.8), channel_id=1, replica_groups=mesh['pr'=8,'pc'=16] {'pc'}, dimensions={0} | all-to-all | bytes 1048576 | tf_op jit(solution)/shard_map/all_to_all | solution.py:64
  106.5 0.0 copy-done.1
  106.5 4.8 %fusion.29 = f32[1024,128]{1,0:T(8,128)} fusion(f32[1024,128]{1,0:T(8,128)S(1)} %copy-done.1, f32[1024,128]{1,0:T(8,128)S(1)} %bitcast.30, f32[1024,256]{0,1:T(8,128)} %fusion.47, f32[1024,768]{0,1:T(8,128)} %fusion.19), kind=kOutput, calls=%fused_computation.49 | convolution fusion | flops 806486016 | bytes 5767168 | tf_op jit(solution)/shard_map/dot_general | solution.py:53
  (8 shorter events, 0.2 us)
Async XLA Ops:
  0.0 61.6 %copy-start = (f32[64,4096]{1,0:T(8,128)S(1)}, f32[64,4096]{1,0:T(8,128)}, u32[]{:S(2)}) copy-start(f32[64,4096]{1,0:T(8,128)} %param.9) | copy-start | bytes 3145732
  0.0 26.8 %copy-start.3 = (f32[256,128]{1,0:T(8,128)S(1)}, f32[256,128]{1,0:T(8,128)}, u32[]{:S(2)}) copy-start(f32[256,128]{1,0:T(8,128)} %param.10) | copy-start | bytes 393220
  2.0 24.8 %all-to-all-start = ((bf16[16,64,512]{2,1,0:T(8,128)(2,1)}), bf16[16,64,512]{2,1,0:T(8,128)(2,1)S(1)}, u32[]{:S(2)}, u32[]{:S(2)}) async-start(bf16[16,64,512]{2,1,0:T(8,128)(2,1)} %broadcast_in_dim.6), calls=%async_computation | async-start | bytes 2097152 | tf_op jit(solution)/shard_map/all_to_all | solution.py:64
  28.4 33.2 %all-to-all-start.1 = ((f32[16,256,128]{2,1,0:T(8,128)}), f32[16,256,128]{2,1,0:T(8,128)}, u32[]{:S(2)}, u32[]{:S(2)}) async-start(f32[16,256,128]{2,1,0:T(8,128)} %broadcast_in_dim.7), calls=%async_computation.1 | async-start | bytes 4194304 | tf_op jit(solution)/shard_map/all_to_all | solution.py:64
  56.4 18.5 %copy-start.2 = (f32[64,1024]{1,0:T(8,128)S(1)}, f32[64,1024]{1,0:T(8,128)}, u32[]{:S(2)}) copy-start(f32[64,1024]{1,0:T(8,128)} %param.12) | copy-start | bytes 786436
  56.4 18.5 %copy-start.4 = (f32[64,128]{1,0:T(8,128)S(1)}, f32[64,128]{1,0:T(8,128)}, u32[]{:S(2)}) copy-start(f32[64,128]{1,0:T(8,128)} %param.11) | copy-start | bytes 98308
  63.9 1.3 %collective-permute-start = (f32[64,128]{1,0:T(8,128)S(1)}, f32[64,128]{1,0:T(8,128)S(1)}, u32[]{:S(2)}, u32[]{:S(2)}) collective-permute-start(f32[64,128]{1,0:T(8,128)S(1)} %convolution_bitcast_fusion), channel_id=1, source_target_pairs={{0,16},{16,0},{32,48},{48,32},{64,80},{80,64},{96,112},{112,96},{1... | collective-permute-start | bytes 98312 | tf_op jit(solution)/shard_map/ppermute | solution.py:75
  65.2 3.9 %collective-permute-start.1 = (f32[64,128]{1,0:T(8,128)S(1)}, f32[64,128]{1,0:T(8,128)S(1)}, u32[]{:S(2)}, u32[]{:S(2)}) collective-permute-start(f32[64,128]{1,0:T(8,128)S(1)} %add.335), channel_id=1, source_target_pairs={{0,32},{16,48},{32,0},{48,16},{64,96},{80,112},{96,64},{112,80},{1... | collective-permute-start | bytes 98312 | tf_op jit(solution)/shard_map/ppermute | solution.py:75
  69.2 5.8 %collective-permute-start.2 = (f32[64,128]{1,0:T(8,128)S(1)}, f32[64,128]{1,0:T(8,128)S(1)}, u32[]{:S(2)}, u32[]{:S(2)}) collective-permute-start(f32[64,128]{1,0:T(8,128)S(1)} %add.336), channel_id=1, source_target_pairs={{0,64},{16,80},{32,96},{48,112},{64,0},{80,16},{96,32},{112,48},{1... | collective-permute-start | bytes 98312 | tf_op jit(solution)/shard_map/ppermute | solution.py:75
  76.6 13.7 %all-to-all-start.2 = ((f32[16,64,128]{2,1,0:T(8,128)}), f32[16,64,128]{2,1,0:T(8,128)S(1)}, u32[]{:S(2)}, u32[]{:S(2)}) async-start(f32[16,64,128]{2,1,0:T(8,128)} %bitcast.5), calls=%async_computation.2 | async-start | bytes 1048576 | tf_op jit(solution)/shard_map/all_to_all | solution.py:110
  80.4 26.1 %copy-start.1 = (f32[1024,128]{1,0:T(8,128)S(1)}, f32[1024,128]{1,0:T(8,128)}, u32[]{:S(2)}) copy-start(f32[1024,128]{1,0:T(8,128)} %param.13) | copy-start | bytes 1572868
